TPU v7x, 256 devices: a whole 4x4x8 slice. The times are simulated.
256 devices in a mesh: row: 8 (over z), col: 32 (over y, x, core).
Axes of the slice: x: 4, y: 4, z: 8, core: 2. Of those that a mesh axis runs over, the one named last changes fastest.
Arguments:
- embeds: bfloat16 [24576, 768], P('col'), may hold values from -6 to 6
- labels: bfloat16 [24576, 1000], P('col'), may hold values from -6 to 6
- sharpness: float32 [24576], P('col'), may hold values from 0.5 to 100
- pattern: int32 [192, 16], P('col'), may hold values from 0 to 191, as said below
- mask_pos: int32 [24576, 50], P('col'), may hold values from 0 to 2047, as said below
Outputs:
- propagated: bfloat16 [24576, 1000], P('col', 'row')
Inputs may be any that keep to these rules, and one draw needn't show every extreme that they name: `pattern`: split the row blocks into runs of 6 and the slots into runs of 2; within one run of row blocks and one run of slots, ids that lie in the same run of 6 block ids are equal. `mask_pos`: the 50 positions of a row are distinct; position k * 128 + m names row m of the row block's k-th candidate block.
All inputs are finite; a program needn't handle non-finite values.
Results may differ from a plain program's by a relative error of at most 0.012.
Values may be sent and summed in bfloat16 or wider, within the bound.
No kernel may reach another device: no remote copies, remote signals or barrier semaphores. Data moves between devices by JAX's collectives and lax.ppermute only.
A program may use at most 128 MiB of HBM per device.

v0:
```python
import math

import jax
import jax.numpy as jnp
from jax import lax
from jax.sharding import PartitionSpec as P

BLOCK = 128
SLOTS = 16


mixing = 0.75
lowest_logit = -1e30


def body(embeds, labels, sharpness, pattern, mask_pos):
    rows_here, width = embeds.shape
    classes = labels.shape[1]
    n_col = lax.axis_size("col")
    n_row = lax.axis_size("row")
    row_pos = lax.axis_index("row")
    blocks_here = rows_here // BLOCK
    slots_here = SLOTS // n_row
    span = slots_here * BLOCK
    my_slots = lax.dynamic_slice_in_dim(pattern, row_pos * slots_here, slots_here, 1)
    owners = my_slots // blocks_here
    local_ids = my_slots % blocks_here
    peers = jnp.arange(n_col, dtype=jnp.int32)
    wanted = jnp.max(jnp.where(owners[..., None] == peers, local_ids[..., None], 0), axis=(0, 1))
    requested = lax.all_to_all(wanted, "col", split_axis=0, concat_axis=0, tiled=True)
    embedding_tiles = embeds.reshape(blocks_here, BLOCK, width)
    lab_blocks = labels.reshape(blocks_here, BLOCK, classes)
    send_emb = embedding_tiles[requested]
    send_lab = lab_blocks[requested]
    shifted = mask_pos - row_pos * span
    shifted = jnp.where((shifted >= 0) & (shifted < span), shifted, span)
    row_ids = jnp.arange(rows_here, dtype=jnp.int32)[:, None]
    in_mask = (
        jnp.zeros((rows_here, span), jnp.float32).at[row_ids, shifted].set(1.0, mode="drop") > 0.5
    )
    in_mask = in_mask.reshape(blocks_here, BLOCK, span)

    def propagate_using(weight_matrix, fetched_lab):
        candidate_ids = fetched_lab[owners].reshape(blocks_here, span, classes)
        blended_rows = jnp.einsum(
            "tmg,tgh->tmh", weight_matrix, candidate_ids, preferred_element_type=jnp.float32
        )
        return blended_rows.reshape(rows_here, classes)

    fetched_emb, fetched_lab = (
        lax.all_to_all(send_emb, "col", split_axis=0, concat_axis=0, tiled=True),
        lax.all_to_all(send_lab, "col", split_axis=0, concat_axis=0, tiled=True),
    )
    candidate_ids = fetched_emb[owners].reshape(blocks_here, span, width)
    scores = jnp.einsum(
        "evg,erg->evr", embedding_tiles, candidate_ids, preferred_element_type=jnp.float32
    ) / math.sqrt(width)
    logits = scores * sharpness.reshape(blocks_here, BLOCK, 1)
    local_max = jnp.max(jnp.where(in_mask, logits, lowest_logit), axis=2)
    top = lax.pmax(local_max, "row")
    totals = lax.psum(
        jnp.sum(jnp.where(in_mask, jnp.exp(logits - top[..., None]), 0.0), axis=2), "row"
    )
    weight_matrix = jnp.where(
        in_mask, jnp.exp(logits - top[..., None]) / totals[..., None], 0.0
    ).astype(jnp.bfloat16)
    partial_one = propagate_using(weight_matrix, fetched_lab)
    summed = lax.psum(partial_one.astype(jnp.bfloat16), "row").astype(jnp.float32)
    spread = (mixing * summed + (1.0 - mixing) * labels.astype(jnp.float32)).astype(jnp.bfloat16)
    send_spread = spread.reshape(blocks_here, BLOCK, classes)[requested]
    fetched_spread = lax.all_to_all(send_spread, "col", split_axis=0, concat_axis=0, tiled=True)
    partial_two = propagate_using(weight_matrix, fetched_spread)
    share = lax.psum_scatter(
        partial_two.astype(jnp.bfloat16), "row", scatter_dimension=1, tiled=True
    ).astype(jnp.float32)
    per_device = classes // n_row
    seed_part = lax.dynamic_slice_in_dim(labels, row_pos * per_device, per_device, 1)
    return (mixing * share + (1.0 - mixing) * seed_part.astype(jnp.float32)).astype(jnp.bfloat16)


def solution(mesh):
    placed = (P("col", None), P("col", None), P("col"), P("col", None), P("col", None))
    return jax.shard_map(
        body, mesh=mesh, in_specs=placed, out_specs=P("col", "row"), check_vma=False
    )
```

profile of v0, /device:TPU:1, one launch (start us, length us, event | category | flops | bytes accessed | tf_op | source)
XLA Modules:
  0.0 602.6 jit_solution(12061529373204525564)
XLA Ops:
  6.5 0.0 copy-start
  6.5 0.9 compare_select_fusion.2
  7.4 0.1 fusion.4
  7.5 0.1 copy.62
  7.6 15.3 %all_to_all.27 = s32[32,1,1]{2,1,0:T(1,128)S(1)} all-to-all(s32[32,1,1]{2,1,0:T(1,128)S(1)} %copy.62), channel_id=1, replica_groups=mesh['row'=8,'col'=32] {'col'}, dimensions={0} | all-to-all | bytes 256 | tf_op jit(solution)/shard_map/all_to_all | solution.py:30
  22.9 0.7 reduce.2
  23.6 0.0 copy-done
  23.6 3.6 gather_fusion
  27.2 0.0 copy-start.3
  27.2 5.3 all-to-all-start.1
  32.5 0.0 copy-done.3
  32.5 1.6 copy.66
  34.1 1.9 copy.67
  36.1 4.9 gather_fusion.2
  41.0 0.0 copy-start.9
  41.0 0.0 copy-start.8
  41.0 64.9 %all-to-all-done.1 = bf16[32,128,768]{2,1,0:T(8,128)(2,1)} async-done(((bf16[32,128,768]{2,1,0:T(8,128)(2,1)}), bf16[32,128,768]{2,1,0:T(8,128)(2,1)}, u32[]{:S(2)}, u32[]{:S(2)}) %all-to-all-start.1) | async-done | bytes 6291488 | tf_op jit(solution)/shard_map/all_to_all | solution.py:51
  105.8 9.5 %all-to-all-start.2 = ((bf16[32,128,1000]{1,2,0:T(8,128)(2,1)}), bf16[32,128,1000]{1,2,0:T(8,128)(2,1)}, u32[]{:S(2)}, u32[]{:S(2)}) async-start(bf16[32,128,1000]{1,2,0:T(8,128)(2,1)} %gather_fusion.2), calls=%async_computation.2 | async-start | bytes 16384000 | tf_op jit(solution)/shard_map/all_to_all | solution.py:52
  115.3 0.0 copy-start.7
  115.3 0.0 all-reduce.4.cloned.1.call-start
  115.4 0.1 reshape.89
  115.5 0.0 copy-done.6
  115.5 0.0 copy-done.9
  115.6 0.1 multiply_reduce_fusion
  115.7 0.0 copy-done.8
  115.7 0.1 and_reduce_fusion
  115.8 0.2 copy.61
  116.0 0.3 reshape.127
  116.4 140.8 %scatter_custom_fusion = f32[196608]{0:T(1024)S(1)} fusion(s32[38400]{0:T(1024)S(1)} %reshape.127, f32[38400]{0:T(1024)S(1)} %broadcast.66, f32[]{:T(128)} %constant.21.clone.1), kind=kCustom, calls=%fused_computation.18 | custom fusion | bytes 786436
  257.2 0.1 broadcast_compare_fusion
  257.3 0.2 reshape.65
  257.5 1.0 copy.65
  258.5 0.0 copy-done.7
  258.5 3.5 gather_fusion.1
  262.0 3.2 select_reduce_fusion.1
  265.2 16.4 %pmax.7 = f32[6,128]{1,0:T(8,128)S(1)} all-reduce(f32[6,128]{1,0:T(8,128)} %get-tuple-element.8), channel_id=1, replica_groups=mesh['row'=8,'col'=32] {'row'}, use_global_device_ids=true, to_apply=%region_3.4 | all-reduce | flops 768 | bytes 6144 | tf_op jit(solution)/shard_map/pmax | solution.py:60
  281.5 1.4 select_reduce_fusion
  283.0 10.8 %psum.14 = f32[6,128]{1,0:T(8,128)S(1)} all-reduce(f32[6,128]{1,0:T(8,128)S(1)} %select_reduce_fusion), channel_id=1, replica_groups=mesh['row'=8,'col'=32] {'row'}, use_global_device_ids=true, to_apply=%region_5.6 | all-reduce | flops 768 | bytes 6144 | tf_op jit(solution)/shard_map/psum | solution.py:61
  293.7 0.0 all-to-all-done.2
  293.7 6.1 %gather_fusion.3 = bf16[12,128,1000]{1,2,0:T(8,128)(2,1)} fusion(bf16[32,128,1000]{1,2,0:T(8,128)(2,1)} %all-to-all-done.2, s32[1024]{0:T(1024)S(1)} %pad_clamp_fusion), kind=kCustom, calls=%fused_computation.3 | custom fusion | bytes 6144048 | tf_op jit(solution)/shard_map/gather | solution.py:44
  299.8 4.7 copy.68
  304.5 0.0 copy-done.4
  304.5 0.0 copy-done.5
  304.5 4.3 convolution_convert_fusion.1
  308.8 2.7 copy.71
  311.5 0.0 all-reduce.4.cloned.1.call-update
  311.5 0.2 all-reduce.6.cloned.1.call-start
  311.8 80.7 %all-reduce.4.cloned.1.call-done = bf16[768,1000]{1,0:T(8,128)(2,1)} async-done(((bf16[768,1000]{1,0:T(8,128)(2,1)}), bf16[768,1000]{1,0:T(8,128)(2,1)}) %all-reduce.4.cloned.1.call-update) | async-done | bytes 1536016 | tf_op jit(solution)/shard_map/psum | solution.py:68
  392.4 0.0 copy-done.2
  392.4 3.3 add_convert_fusion
  395.7 1.9 copy.73
  397.7 4.9 gather_fusion.4
  402.6 105.2 %all_to_all.28 = bf16[32,128,1000]{1,2,0:T(8,128)(2,1)} all-to-all(bf16[32,128,1000]{1,2,0:T(8,128)(2,1)} %gather_fusion.4), channel_id=1, replica_groups=mesh['row'=8,'col'=32] {'col'}, dimensions={0} | all-to-all | bytes 16384000 | tf_op jit(solution)/shard_map/all_to_all | solution.py:71
  507.7 6.1 %gather_fusion.5 = bf16[12,128,1000]{1,2,0:T(8,128)(2,1)} fusion(bf16[32,128,1000]{1,2,0:T(8,128)(2,1)} %all_to_all.28, s32[1024]{0:T(1024)S(1)} %pad_clamp_fusion), kind=kCustom, calls=%fused_computation.5 | custom fusion | bytes 6144048 | tf_op jit(solution)/shard_map/gather | solution.py:44
  513.8 4.6 copy.74
  518.4 3.3 convolution_convert_fusion
  521.8 0.0 copy-start.10
  521.8 1.6 copy.77
  523.4 0.0 all-reduce.6.cloned.1.call-update
  523.4 0.0 copy-done.10
  523.4 0.6 dynamic-slice
  524.7 69.1 %all-reduce.6.cloned.1.call-done = bf16[768,1000]{1,0:T(8,128)(2,1)} async-done(((bf16[768,1000]{1,0:T(8,128)(2,1)}), bf16[768,1000]{1,0:T(8,128)(2,1)}) %all-reduce.6.cloned.1.call-update) | async-done | bytes 1536016
  593.7 2.0 add_convert_fusion.1
  595.7 0.0 copy-done.1
  (13 shorter events, 0.1 us)
Async XLA Ops:
  6.5 17.1 %copy-start = (bf16[768,768]{1,0:T(8,128)(2,1)S(1)}, bf16[768,768]{1,0:T(8,128)(2,1)}, u32[]{:S(2)}) copy-start(bf16[768,768]{1,0:T(8,128)(2,1)} %param.5) | copy-start | bytes 3538948
  27.2 5.3 copy-start.3
  27.2 78.6 %all-to-all-start.1 = ((bf16[32,128,768]{2,1,0:T(8,128)(2,1)}), bf16[32,128,768]{2,1,0:T(8,128)(2,1)}, u32[]{:S(2)}, u32[]{:S(2)}) async-start(bf16[32,128,768]{2,1,0:T(8,128)(2,1)} %gather_fusion), calls=%async_computation.1 | async-start | bytes 12582912 | tf_op jit(solution)/shard_map/all_to_all | solution.py:51
  41.0 74.5 %copy-start.6 = (s32[768,50]{0,1:T(8,128)S(1)}, s32[768,50]{0,1:T(8,128)}, u32[]{:S(2)}) copy-start(s32[768,50]{0,1:T(8,128)} %param.9) | copy-start | bytes 460804
  41.0 74.6 %copy-start.9 = (s32[2]{0:T(128)S(1)}, s32[2]{0:T(128)}, u32[]{:S(2)}) copy-start(s32[2]{0:T(128)} %constant.70) | copy-start | bytes 28
  41.0 74.7 %copy-start.8 = (s32[2]{0:T(128)S(1)}, s32[2]{0:T(128)}, u32[]{:S(2)}) copy-start(s32[2]{0:T(128)} %constant.73) | copy-start | bytes 28
  105.8 187.9 %all-to-all-start.2 = ((bf16[32,128,1000]{1,2,0:T(8,128)(2,1)}), bf16[32,128,1000]{1,2,0:T(8,128)(2,1)}, u32[]{:S(2)}, u32[]{:S(2)}) async-start(bf16[32,128,1000]{1,2,0:T(8,128)(2,1)} %gather_fusion.2), calls=%async_computation.2 | async-start | bytes 16384000 | tf_op jit(solution)/shard_map/all_to_all | solution.py:52
  115.3 143.1 %copy-start.7 = (f32[768]{0:T(1024)S(1)}, f32[768]{0:T(1024)}, u32[]{:S(2)}) copy-start(f32[768]{0:T(1024)} %param.7) | copy-start | bytes 9220
  115.3 277.1 %all-reduce.4.cloned.1.call-start = ((), (), s32[]{:S(2)}) async-start(), calls=%async_computation.4 | async-start | bytes 3145728 | tf_op jit(solution)/shard_map/psum | solution.py:68
  299.8 4.7 copy-start.4
  299.8 4.7 copy-start.5
  308.8 83.6 %copy-start.2 = (bf16[768,1000]{1,0:T(8,128)(2,1)S(1)}, bf16[768,1000]{1,0:T(8,128)(2,1)}, u32[]{:S(2)}) copy-start(bf16[768,1000]{1,0:T(8,128)(2,1)} %copy.66) | copy-start | bytes 4608004
  311.5 282.2 %all-reduce.6.cloned.1.call-start = ((), (), s32[]{:S(2)}) async-start(), calls=%async_computation.5 | async-start | bytes 3145728
  518.4 77.3 %copy-start.1 = (bf16[768,768]{1,0:T(8,128)(2,1)S(1)}, bf16[768,768]{1,0:T(8,128)(2,1)}, u32[]{:S(2)}) copy-start(bf16[768,768]{1,0:T(8,128)(2,1)} %param.5) | copy-start | bytes 3538948
  521.8 1.6 copy-start.10
Sparse Core Ops, SparseCore 0:
  311.7 80.7 all-reduce.3
  523.5 70.1 all-reduce.5
where the time goes:
time: 607 us; the launch traced here: 603 us
  waiting for transfers between devices  215 us (35%)
  local copies, waits for them, and re-layouts  191 us (31%)
  blocking collectives  148 us (24%)
  starting transfers between devices  15 us (2%)
  between operations  14.3 us (2%)
  matrix products  10.8 us (2%)
  other arithmetic  8.76 us (1%)
    unnamed x28, local copies, waits for them, and re-layouts  144 us
    all_to_all x1, blocking collectives, body(): lax.all_to_all(send_spread, 'col', split_axis=0, concat_axis=0, tiled=True)  105 us
    psum x1, waiting for transfers between devices, body(): lax.psum(partial_one.astype(jnp.bfloat16), 'row').astype(jnp.float32)  80.7 us
    unnamed x3, waiting for transfers between devices  69.1 us
    all_to_all x1, waiting for transfers between devices, body(): lax.all_to_all(send_emb, 'col', split_axis=0, concat_axis=0, tiled=True)  64.9 us
    gather x4, local copies, waits for them, and re-layouts, propagate_using(): candidate_ids = fetched_lab[owners].reshape(blocks_here, span, classes)  21.5 us
    pmax x1, blocking collectives, body(): top = lax.pmax(local_max, 'row')  16.4 us
    all_to_all x1, blocking collectives, body(): lax.all_to_all(wanted, 'col', split_axis=0, concat_axis=0, tiled=True)  15.3 us
  transfers between devices with their start and end apart: 4, of which 3 were waited for; matrix products, arithmetic and copies ran while one was open for 27% of the time, Pallas kernels for 0%

commit v1 on v0

--- a/solution.py
+++ b/solution.py
@@ -34,10 +34,8 @@
     send_lab = lab_blocks[requested]
     shifted = mask_pos - row_pos * span
     shifted = jnp.where((shifted >= 0) & (shifted < span), shifted, span)
-    row_ids = jnp.arange(rows_here, dtype=jnp.int32)[:, None]
-    in_mask = (
-        jnp.zeros((rows_here, span), jnp.float32).at[row_ids, shifted].set(1.0, mode="drop") > 0.5
-    )
+    positions = jnp.arange(span, dtype=jnp.int32)
+    in_mask = jnp.any(shifted[:, :, None] == positions[None, None, :], axis=1)
     in_mask = in_mask.reshape(blocks_here, BLOCK, span)
 
     def propagate_using(weight_matrix, fetched_lab):
@@ -57,10 +55,10 @@
     ) / math.sqrt(width)
     logits = scores * sharpness.reshape(blocks_here, BLOCK, 1)
     local_max = jnp.max(jnp.where(in_mask, logits, lowest_logit), axis=2)
-    top = lax.pmax(local_max, "row")
-    totals = lax.psum(
-        jnp.sum(jnp.where(in_mask, jnp.exp(logits - top[..., None]), 0.0), axis=2), "row"
-    )
+    local_sum = jnp.sum(jnp.where(in_mask, jnp.exp(logits - local_max[..., None]), 0.0), axis=2)
+    stats = lax.all_gather(jnp.stack([local_max, local_sum]), "row")
+    top = jnp.max(stats[:, 0], axis=0)
+    totals = jnp.sum(stats[:, 1] * jnp.exp(stats[:, 0] - top), axis=0)
     weight_matrix = jnp.where(
         in_mask, jnp.exp(logits - top[..., None]) / totals[..., None], 0.0
     ).astype(jnp.bfloat16)
@@ -71,11 +69,12 @@
     fetched_spread = lax.all_to_all(send_spread, "col", split_axis=0, concat_axis=0, tiled=True)
     partial_two = propagate_using(weight_matrix, fetched_spread)
     share = lax.psum_scatter(
-        partial_two.astype(jnp.bfloat16), "row", scatter_dimension=1, tiled=True
+        partial_two.astype(jnp.bfloat16), "row", scatter_dimension=0, tiled=True
     ).astype(jnp.float32)
-    per_device = classes // n_row
-    seed_part = lax.dynamic_slice_in_dim(labels, row_pos * per_device, per_device, 1)
-    return (mixing * share + (1.0 - mixing) * seed_part.astype(jnp.float32)).astype(jnp.bfloat16)
+    rows_dev = rows_here // n_row
+    seed_rows = lax.dynamic_slice_in_dim(labels, row_pos * rows_dev, rows_dev, 0)
+    mine = (mixing * share + (1.0 - mixing) * seed_rows.astype(jnp.float32)).astype(jnp.bfloat16)
+    return lax.all_to_all(mine, "row", split_axis=1, concat_axis=0, tiled=True)
 
 
 def solution(mesh):

time: 607 us -> 500 us (0.82)
  local copies, waits for them, and re-layouts: 191 us -> 51.2 us
  waiting for transfers between devices: 215 us -> 234 us
  blocking collectives: 148 us -> 158 us
    unnamed x28 -> x22, local copies, waits for them, and re-layouts: 144 us -> 3.22 us
    unnamed x3 -> x2, waiting for transfers between devices: 69.1 us -> 0.03 us
    all_to_all x1, waiting for transfers between devices: 0.01 us -> 59 us  [body(): lax.all_to_all(send_lab, 'col', split_axis=0, concat_axis=0, tiled=True)]
    reduce_scatter x0 -> x1, waiting for transfers between devices: none -> 32.3 us  [body(): lax.psum_scatter(partial_two.astype(jnp.bfloat16), 'row', scatter_dimensi...]
    all_gather x0 -> x1, blocking collectives: none -> 24.5 us  [body(): stats = lax.all_gather(jnp.stack([local_max, local_sum]), 'row')]
    pmax x1 -> x0, blocking collectives: 16.4 us -> none  [body(): top = lax.pmax(local_max, 'row')]
    all_to_all x0 -> x1, blocking collectives: none -> 13 us  [body(): return lax.all_to_all(mine, 'row', split_axis=1, concat_axis=0, tiled=True)]
    psum x1 -> x0, blocking collectives: 10.8 us -> none  [body(): lax.psum(jnp.sum(jnp.where(in_mask, jnp.exp(logits - top[..., None]), 0.0...]
  transfers between devices with their start and end apart: 4 -> 4, of which waited for: 3 -> 4; matrix products, arithmetic and copies ran while one was open for 27% -> 4% of each run, Pallas kernels for 0% -> 0%
where the time goes in v1:
time: 500 us; the launch traced here: 495 us
  waiting for transfers between devices  234 us (47%)
  blocking collectives  158 us (32%)
  local copies, waits for them, and re-layouts  51.2 us (10%)
  starting transfers between devices  14.8 us (3%)
  between operations  13.6 us (3%)
  other arithmetic  13.5 us (3%)
  matrix products  9.37 us (2%)
    all_to_all x1, blocking collectives, body(): lax.all_to_all(send_spread, 'col', split_axis=0, concat_axis=0, tiled=True)  105 us
    psum x1, waiting for transfers between devices, body(): lax.psum(partial_one.astype(jnp.bfloat16), 'row').astype(jnp.float32)  78.3 us
    all_to_all x1, waiting for transfers between devices, body(): lax.all_to_all(send_emb, 'col', split_axis=0, concat_axis=0, tiled=True)  64.8 us
    all_to_all x1, waiting for transfers between devices, body(): lax.all_to_all(send_lab, 'col', split_axis=0, concat_axis=0, tiled=True)  59 us
    reduce_scatter x1, waiting for transfers between devices, body(): lax.psum_scatter(partial_two.astype(jnp.bfloat16), 'row', scatter_dimensi...  32.3 us
    all_gather x1, blocking collectives, body(): stats = lax.all_gather(jnp.stack([local_max, local_sum]), 'row')  24.5 us
    gather x4, local copies, waits for them, and re-layouts, propagate_using(): candidate_ids = fetched_lab[owners].reshape(blocks_here, span, classes)  21.5 us
    all_to_all x1, blocking collectives, body(): lax.all_to_all(wanted, 'col', split_axis=0, concat_axis=0, tiled=True)  15.3 us
  transfers between devices with their start and end apart: 4, of which 4 were waited for; matrix products, arithmetic and copies ran while one was open for 4% of the time, Pallas kernels for 0%

profile of v1, /device:TPU:1, one launch (start us, length us, event | category | flops | bytes accessed | tf_op | source)
XLA Modules:
  0.0 494.9 jit_solution(15213027220432271386)
XLA Ops:
  6.5 0.0 copy-start
  6.5 0.9 compare_select_fusion.1
  7.4 0.1 fusion.5
  7.5 0.1 copy.88
  7.6 15.3 %all_to_all.46 = s32[32,1,1]{2,1,0:T(1,128)S(1)} all-to-all(s32[32,1,1]{2,1,0:T(1,128)S(1)} %copy.88), channel_id=1, replica_groups=mesh['row'=8,'col'=32] {'col'}, dimensions={0} | all-to-all | bytes 256 | tf_op jit(solution)/shard_map/all_to_all | solution.py:30
  22.9 0.7 reduce.1
  23.6 0.0 copy-done
  23.6 3.6 gather_fusion
  27.2 0.0 copy-start.3
  27.2 5.3 %all-to-all-start.1 = ((bf16[32,128,768]{2,1,0:T(8,128)(2,1)}), bf16[32,128,768]{2,1,0:T(8,128)(2,1)}, u32[]{:S(2)}, u32[]{:S(2)}) async-start(bf16[32,128,768]{2,1,0:T(8,128)(2,1)} %gather_fusion), calls=%async_computation.1 | async-start | bytes 12582912 | tf_op jit(solution)/shard_map/all_to_all | solution.py:49
  32.5 0.0 copy-done.3
  32.5 1.6 copy.93
  34.1 1.9 copy.94
  36.1 4.9 gather_fusion.2
  41.0 0.0 copy-start.8
  41.0 0.0 copy-start.9
  41.0 64.8 %all-to-all-done.1 = bf16[32,128,768]{2,1,0:T(8,128)(2,1)} async-done(((bf16[32,128,768]{2,1,0:T(8,128)(2,1)}), bf16[32,128,768]{2,1,0:T(8,128)(2,1)}, u32[]{:S(2)}, u32[]{:S(2)}) %all-to-all-start.1) | async-done | bytes 6291488 | tf_op jit(solution)/shard_map/all_to_all | solution.py:49
  105.8 9.5 %all-to-all-start.2 = ((bf16[32,128,1000]{1,2,0:T(8,128)(2,1)}), bf16[32,128,1000]{1,2,0:T(8,128)(2,1)}, u32[]{:S(2)}, u32[]{:S(2)}) async-start(bf16[32,128,1000]{1,2,0:T(8,128)(2,1)} %gather_fusion.2), calls=%async_computation.2 | async-start | bytes 16384000 | tf_op jit(solution)/shard_map/all_to_all | solution.py:50
  115.3 0.0 all-reduce.2.cloned.1.call-start
  115.4 0.1 reshape.86
  115.5 0.0 copy-done.8
  115.5 7.2 %fusion = pred[768,256]{1,0:T(8,128)(4,1)S(1)} fusion(s32[768,50]{0,1:T(8,128)S(1)} %and_select_fusion), kind=kLoop, calls=%fused_computation.7 | loop fusion | flops 19464192 | bytes 350208 | tf_op jit(solution)/shard_map/reduce_or | solution.py:38
  122.7 1.0 copy.92
  123.7 0.0 copy-done.9
  123.7 3.5 gather_fusion.1
  127.2 0.0 copy-start.6
  127.2 1.8 select_reduce_fusion.1
  129.0 0.0 copy-start.4
  129.0 0.9 copy-done.4
  129.8 0.0 copy-done.6
  129.8 0.2 select_reduce_fusion
  130.1 24.5 %all-gather = f32[16,6,128]{2,1,0:T(8,128)S(1)} all-gather(f32[2,6,128]{2,1,0:T(8,128)S(1)} %pad_maximum_fusion), channel_id=2, replica_groups=mesh['row'=8,'col'=32] {'row'}, dimensions={0}, use_global_device_ids=true | all-gather | bytes 55296 | tf_op jit(solution)/shard_map/all_gather | solution.py:59
  154.6 59.0 %all-to-all-done.2 = bf16[32,128,1000]{1,2,0:T(8,128)(2,1)} async-done(((bf16[32,128,1000]{1,2,0:T(8,128)(2,1)}), bf16[32,128,1000]{1,2,0:T(8,128)(2,1)}, u32[]{:S(2)}, u32[]{:S(2)}) %all-to-all-start.2) | async-done | bytes 8192032 | tf_op jit(solution)/shard_map/all_to_all | solution.py:50
  213.6 6.1 %gather_fusion.3 = bf16[12,128,1000]{1,2,0:T(8,128)(2,1)} fusion(bf16[32,128,1000]{1,2,0:T(8,128)(2,1)} %all-to-all-done.2, s32[1024]{0:T(1024)S(1)} %pad_clamp_fusion), kind=kCustom, calls=%fused_computation.3 | custom fusion | bytes 6144048 | tf_op jit(solution)/shard_map/gather | solution.py:42
  219.7 0.0 copy-start.5
  219.7 0.0 copy-start.7
  219.7 4.7 copy.95
  224.4 0.0 copy-done.5
  224.4 0.0 copy-done.7
  224.4 4.3 convolution_convert_fusion.1
  228.7 0.0 copy-start.2
  228.7 2.7 copy.98
  231.4 0.0 all-reduce.2.cloned.1.call-update
  231.4 0.0 reduce-scatter.2.cloned.1.call-start
  231.5 78.3 %all-reduce.2.cloned.1.call-done = bf16[768,1000]{1,0:T(8,128)(2,1)} async-done(((bf16[768,1000]{1,0:T(8,128)(2,1)}), bf16[768,1000]{1,0:T(8,128)(2,1)}) %all-reduce.2.cloned.1.call-update) | async-done | bytes 1536016 | tf_op jit(solution)/shard_map/psum | solution.py:66
  309.7 0.0 copy-done.2
  309.7 3.3 add_convert_fusion
  313.0 1.9 copy.100
  315.0 4.9 gather_fusion.4
  319.9 105.1 %all_to_all.47 = bf16[32,128,1000]{1,2,0:T(8,128)(2,1)} all-to-all(bf16[32,128,1000]{1,2,0:T(8,128)(2,1)} %gather_fusion.4), channel_id=1, replica_groups=mesh['row'=8,'col'=32] {'col'}, dimensions={0} | all-to-all | bytes 16384000 | tf_op jit(solution)/shard_map/all_to_all | solution.py:69
  425.0 6.1 %gather_fusion.5 = bf16[12,128,1000]{1,2,0:T(8,128)(2,1)} fusion(bf16[32,128,1000]{1,2,0:T(8,128)(2,1)} %all_to_all.47, s32[1024]{0:T(1024)S(1)} %pad_clamp_fusion), kind=kCustom, calls=%fused_computation.5 | custom fusion | bytes 6144048 | tf_op jit(solution)/shard_map/gather | solution.py:42
  431.1 4.6 copy.101
  435.7 0.0 copy-start.1
  435.7 3.3 convolution_convert_fusion
  439.1 1.6 copy.104
  440.7 0.0 reduce-scatter.2.cloned.1.call-update
  440.7 32.3 %reduce-scatter.2.cloned.1.call-done = bf16[96,1000]{1,0:T(8,128)(2,1)} async-done(((bf16[768,1000]{1,0:T(8,128)(2,1)}), bf16[96,1000]{1,0:T(8,128)(2,1)}) %reduce-scatter.2.cloned.1.call-update) | async-done | bytes 192016 | tf_op jit(solution)/shard_map/reduce_scatter | solution.py:71
  473.0 1.1 add_convert_fusion.1
  474.1 0.3 all_to_all.37
  474.4 13.0 %all_to_all.48 = bf16[96,8,125]{2,0,1:T(8,128)(2,1)S(1)} all-to-all(bf16[96,8,125]{2,0,1:T(8,128)(2,1)S(1)} %copy.106), channel_id=1, replica_groups=mesh['row'=8,'col'=32] {'row'}, dimensions={1} | all-to-all | bytes 384000 | tf_op jit(solution)/shard_map/all_to_all | solution.py:77
  487.3 0.7 copy.118
  488.0 0.0 copy-done.1
  (9 shorter events, 0.1 us)
Async XLA Ops:
  6.5 17.1 %copy-start = (bf16[768,768]{1,0:T(8,128)(2,1)S(1)}, bf16[768,768]{1,0:T(8,128)(2,1)}, u32[]{:S(2)}) copy-start(bf16[768,768]{1,0:T(8,128)(2,1)} %param.5) | copy-start | bytes 3538948
  27.2 5.3 %copy-start.3 = (bf16[768,1000]{0,1:T(8,128)(2,1)S(1)}, bf16[768,1000]{0,1:T(8,128)(2,1)}, u32[]{:S(2)}) copy-start(bf16[768,1000]{0,1:T(8,128)(2,1)} %param.6) | copy-start | bytes 4608004
  27.2 78.6 %all-to-all-start.1 = ((bf16[32,128,768]{2,1,0:T(8,128)(2,1)}), bf16[32,128,768]{2,1,0:T(8,128)(2,1)}, u32[]{:S(2)}, u32[]{:S(2)}) async-start(bf16[32,128,768]{2,1,0:T(8,128)(2,1)} %gather_fusion), calls=%async_computation.1 | async-start | bytes 12582912 | tf_op jit(solution)/shard_map/all_to_all | solution.py:49
  41.0 74.5 %copy-start.8 = (s32[768,50]{0,1:T(8,128)S(1)}, s32[768,50]{0,1:T(8,128)}, u32[]{:S(2)}) copy-start(s32[768,50]{0,1:T(8,128)} %param.9) | copy-start | bytes 460804
  41.0 82.7 %copy-start.9 = (f32[768]{0:T(1024)S(1)}, f32[768]{0:T(1024)}, u32[]{:S(2)}) copy-start(f32[768]{0:T(1024)} %param.7) | copy-start | bytes 9220
  105.8 107.8 %all-to-all-start.2 = ((bf16[32,128,1000]{1,2,0:T(8,128)(2,1)}), bf16[32,128,1000]{1,2,0:T(8,128)(2,1)}, u32[]{:S(2)}, u32[]{:S(2)}) async-start(bf16[32,128,1000]{1,2,0:T(8,128)(2,1)} %gather_fusion.2), calls=%async_computation.2 | async-start | bytes 16384000 | tf_op jit(solution)/shard_map/all_to_all | solution.py:50
  115.3 194.4 %all-reduce.2.cloned.1.call-start = ((), (), s32[]{:S(2)}) async-start(), calls=%async_computation.6 | async-start | bytes 3145728 | tf_op jit(solution)/shard_map/psum | solution.py:66
  127.2 2.7 copy-start.6
  129.0 0.9 copy-start.4
  219.7 4.7 copy-start.5
  219.7 4.7 copy-start.7
  228.7 81.1 %copy-start.2 = (bf16[768,1000]{1,0:T(8,128)(2,1)S(1)}, bf16[768,1000]{1,0:T(8,128)(2,1)}, u32[]{:S(2)}) copy-start(bf16[768,1000]{1,0:T(8,128)(2,1)} %copy.93) | copy-start | bytes 4608004
  231.4 241.6 %reduce-scatter.2.cloned.1.call-start = ((), (), s32[]{:S(2)}) async-start(), calls=%async_computation.7 | async-start | bytes 1769472 | tf_op jit(solution)/shard_map/reduce_scatter | solution.py:71
  435.7 52.3 %copy-start.1 = (bf16[768,768]{1,0:T(8,128)(2,1)S(1)}, bf16[768,768]{1,0:T(8,128)(2,1)}, u32[]{:S(2)}) copy-start(bf16[768,768]{1,0:T(8,128)(2,1)} %param.5) | copy-start | bytes 3538948
Sparse Core Ops, SparseCore 0:
  231.5 78.1 all-reduce.1
  440.8 32.1 reduce-scatter.1

commit v2 on v1

v2 whole, which is shorter than its diff:
```python
import math

import jax
import jax.numpy as jnp
from jax import lax
from jax.sharding import PartitionSpec as P

BLOCK = 128
SLOTS = 16
CHUNKS = 4


mixing = 0.75
lowest_logit = -1e30


def body(embeds, labels, sharpness, pattern, mask_pos):
    rows_here, width = embeds.shape
    classes = labels.shape[1]
    n_col = lax.axis_size("col")
    n_row = lax.axis_size("row")
    row_pos = lax.axis_index("row")
    blocks_here = rows_here // BLOCK
    slots_here = SLOTS // n_row
    span = slots_here * BLOCK
    my_slots = lax.dynamic_slice_in_dim(pattern, row_pos * slots_here, slots_here, 1)
    owners = my_slots // blocks_here
    local_ids = my_slots % blocks_here
    peers = jnp.arange(n_col, dtype=jnp.int32)
    wanted = jnp.max(jnp.where(owners[..., None] == peers, local_ids[..., None], 0), axis=(0, 1))
    requested = lax.all_to_all(wanted, "col", split_axis=0, concat_axis=0, tiled=True)
    embedding_tiles = embeds.reshape(blocks_here, BLOCK, width)
    send_emb = embedding_tiles[requested]
    shifted = mask_pos - row_pos * span
    shifted = jnp.where((shifted >= 0) & (shifted < span), shifted, span)
    positions = jnp.arange(span, dtype=jnp.int32)
    in_mask = jnp.any(shifted[:, :, None] == positions[None, None, :], axis=1)
    in_mask = in_mask.reshape(blocks_here, BLOCK, span)

    def propagate_using(weight_matrix, fetched_lab):
        width_here = fetched_lab.shape[-1]
        candidate_ids = fetched_lab[owners].reshape(blocks_here, span, width_here)
        blended_rows = jnp.einsum(
            "tmg,tgh->tmh", weight_matrix, candidate_ids, preferred_element_type=jnp.float32
        )
        return blended_rows.reshape(rows_here, width_here)

    fetched_emb = lax.all_to_all(send_emb, "col", split_axis=0, concat_axis=0, tiled=True)
    candidate_ids = fetched_emb[owners].reshape(blocks_here, span, width)
    scores = jnp.einsum(
        "evg,erg->evr", embedding_tiles, candidate_ids, preferred_element_type=jnp.float32
    ) / math.sqrt(width)
    logits = scores * sharpness.reshape(blocks_here, BLOCK, 1)
    local_max = jnp.max(jnp.where(in_mask, logits, lowest_logit), axis=2)
    local_sum = jnp.sum(jnp.where(in_mask, jnp.exp(logits - local_max[..., None]), 0.0), axis=2)
    stats = lax.all_gather(jnp.stack([local_max, local_sum]), "row")
    top = jnp.max(stats[:, 0], axis=0)
    totals = jnp.sum(stats[:, 1] * jnp.exp(stats[:, 0] - top), axis=0)
    weight_matrix = jnp.where(
        in_mask, jnp.exp(logits - top[..., None]) / totals[..., None], 0.0
    ).astype(jnp.bfloat16)
    rows_dev = rows_here // n_row
    piece = classes // CHUNKS
    lab_chunks = labels.reshape(rows_here, CHUNKS, piece).transpose(1, 0, 2)
    fetched = []
    for k in range(CHUNKS):
        send_lab = lab_chunks[k].reshape(blocks_here, BLOCK, piece)[requested]
        fetched.append(lax.all_to_all(send_lab, "col", split_axis=0, concat_axis=0, tiled=True))
    sums = []
    for k in range(CHUNKS):
        partial_one = propagate_using(weight_matrix, fetched[k]).astype(jnp.bfloat16)
        if k > 0:
            partial_one, sums[k - 1] = lax.optimization_barrier((partial_one, sums[k - 1]))
        sums.append(lax.psum(partial_one, "row"))
    spreads = []
    for k in range(CHUNKS):
        summed = sums[k].astype(jnp.float32)
        spread = (mixing * summed + (1.0 - mixing) * lab_chunks[k].astype(jnp.float32)).astype(jnp.bfloat16)
        send_spread = spread.reshape(blocks_here, BLOCK, piece)[requested]
        spreads.append(lax.all_to_all(send_spread, "col", split_axis=0, concat_axis=0, tiled=True))
    shares = []
    for k in range(CHUNKS):
        partial_two = propagate_using(weight_matrix, spreads[k]).astype(jnp.bfloat16)
        if k > 0:
            partial_two, shares[k - 1] = lax.optimization_barrier((partial_two, shares[k - 1]))
        shares.append(lax.psum_scatter(partial_two, "row", scatter_dimension=0, tiled=True))
    outs = []
    for k in range(CHUNKS):
        seed_rows = lax.dynamic_slice_in_dim(lab_chunks[k], row_pos * rows_dev, rows_dev, 0)
        share = shares[k].astype(jnp.float32)
        outs.append((mixing * share + (1.0 - mixing) * seed_rows.astype(jnp.float32)).astype(jnp.bfloat16))
    mine = jnp.concatenate(outs, axis=1)
    return lax.all_to_all(mine, "row", split_axis=1, concat_axis=0, tiled=True)


def solution(mesh):
    placed = (P("col", None), P("col", None), P("col"), P("col", None), P("col", None))
    return jax.shard_map(
        body, mesh=mesh, in_specs=placed, out_specs=P("col", "row"), check_vma=False
    )
```

time: 500 us -> 810 us (1.62)
  waiting for transfers between devices: 234 us -> 591 us
  blocking collectives: 158 us -> 36.9 us
  starting transfers between devices: 14.8 us -> 74.7 us
  local copies, waits for them, and re-layouts: 51.2 us -> 61.3 us
    psum x1 -> x4, waiting for transfers between devices: 78.3 us -> 283 us  [body(): sums.append(lax.psum(partial_one, 'row'))]
    all_to_all x2 -> x0, blocking collectives: 120 us -> none  [the longest x1 105 us: body(): lax.all_to_all(send_spread, 'col', split_axis=0, concat_axis=0, tiled=True)]
    unnamed x2 -> x12, waiting for transfers between devices: 0.03 us -> 99.9 us
    all_to_all x0 -> x5, waiting for transfers between devices: none -> 78.3 us  [the longest x4 75.4 us: body(): lax.all_to_all(send_spread, 'col', split_axis=0, concat_axis=0, tiled=True)]
    all_to_all x0 -> x5, starting transfers between devices: none -> 40.5 us  [the longest x4 31.9 us: body(): lax.all_to_all(send_spread, 'col', split_axis=0, concat_axis=0, tiled=True)]
    reduce_scatter x1 -> x0, waiting for transfers between devices: 32.3 us -> none  [body(): lax.psum_scatter(partial_two.astype(jnp.bfloat16), 'row', scatter_dimensi...]
    all_to_all x1 -> x4, starting transfers between devices: 9.5 us -> 27.3 us  [body(): lax.all_to_all(send_lab, 'col', split_axis=0, concat_axis=0, tiled=True)]
    gather x6 -> x16, local copies, waits for them, and re-layouts: 31.3 us -> 34.5 us  [the longest x8 18.4 us: propagate_using(): candidate_ids = fetched_lab[owners].reshape(blocks_here, span, width_here)]
  transfers between devices with their start and end apart: 4 -> 18, of which waited for: 4 -> 15; matrix products, arithmetic and copies ran while one was open for 4% -> 9% of each run, Pallas kernels for 0% -> 0%
where the time goes in v2:
time: 810 us; the launch traced here: 803 us
  waiting for transfers between devices  591 us (73%)
  starting transfers between devices  74.7 us (9%)
  local copies, waits for them, and re-layouts  61.3 us (8%)
  blocking collectives  36.9 us (5%)
  other arithmetic  17.1 us (2%)
  between operations  13.9 us (2%)
    psum x4, waiting for transfers between devices, body(): sums.append(lax.psum(partial_one, 'row'))  283 us
    unnamed x12, waiting for transfers between devices  99.9 us
    all_to_all x4, waiting for transfers between devices, body(): lax.all_to_all(send_spread, 'col', split_axis=0, concat_axis=0, tiled=True)  75.4 us
    all_to_all x1, waiting for transfers between devices, body(): lax.all_to_all(send_emb, 'col', split_axis=0, concat_axis=0, tiled=True)  70.2 us
    all_to_all x4, waiting for transfers between devices, body(): lax.all_to_all(send_lab, 'col', split_axis=0, concat_axis=0, tiled=True)  59.6 us
    all_to_all x4, starting transfers between devices, body(): lax.all_to_all(send_spread, 'col', split_axis=0, concat_axis=0, tiled=True)  31.9 us
    all_to_all x4, starting transfers between devices, body(): lax.all_to_all(send_lab, 'col', split_axis=0, concat_axis=0, tiled=True)  27.3 us
    all_gather x1, blocking collectives, body(): stats = lax.all_gather(jnp.stack([local_max, local_sum]), 'row')  24.3 us
  transfers between devices with their start and end apart: 18, of which 15 were waited for; matrix products, arithmetic and copies ran while one was open for 9% of the time, Pallas kernels for 0%

profile of v2, /device:TPU:1, one launch (start us, length us, event | category | flops | bytes accessed | tf_op | source)
XLA Modules:
  0.0 803.2 jit_solution(6084548880981616726)
XLA Ops:
  6.5 1.5 compare_select_fusion.1
  8.8 8.6 %all-to-all-start = ((s32[32,1,1]{2,1,0:T(1,128)}), s32[32,1,1]{2,1,0:T(1,128)S(1)}, u32[]{:S(2)}, u32[]{:S(2)}) async-start(s32[32,1,1]{2,1,0:T(1,128)} %copy.173), calls=%async_computation | async-start | bytes 32768 | tf_op jit(solution)/shard_map/all_to_all | solution.py:31
  17.4 1.8 reshape.139
  19.2 1.0 fusion.16
  20.2 1.2 copy.182
  21.4 2.9 all-to-all-done
  24.3 1.2 reduce.1
  26.1 2.0 gather_fusion.6
  28.1 5.0 all-to-all-start.4
  33.1 1.2 copy.180
  34.3 2.0 gather_fusion.4
  36.3 25.2 %all-to-all-done.4 = bf16[32,128,250]{2,1,0:T(8,128)(2,1)} async-done(((bf16[32,128,250]{2,1,0:T(8,128)(2,1)}), bf16[32,128,250]{2,1,0:T(8,128)(2,1)}, u32[]{:S(2)}, u32[]{:S(2)}) %all-to-all-start.4) | async-done | bytes 2048032 | tf_op jit(solution)/shard_map/all_to_all | solution.py:68
  61.5 6.5 all-to-all-start.3
  68.0 3.6 gather_fusion
  71.6 24.8 %all-to-all-done.3 = bf16[32,128,250]{2,1,0:T(8,128)(2,1)} async-done(((bf16[32,128,250]{2,1,0:T(8,128)(2,1)}), bf16[32,128,250]{2,1,0:T(8,128)(2,1)}, u32[]{:S(2)}, u32[]{:S(2)}) %all-to-all-start.3) | async-done | bytes 2048032 | tf_op jit(solution)/shard_map/all_to_all | solution.py:68
  96.3 6.6 all-to-all-start.1
  103.0 1.2 copy.178
  104.1 2.0 gather_fusion.2
  106.1 70.2 %all-to-all-done.1 = bf16[32,128,768]{2,1,0:T(8,128)(2,1)} async-done(((bf16[32,128,768]{2,1,0:T(8,128)(2,1)}), bf16[32,128,768]{2,1,0:T(8,128)(2,1)}, u32[]{:S(2)}, u32[]{:S(2)}) %all-to-all-start.1) | async-done | bytes 6291488 | tf_op jit(solution)/shard_map/all_to_all | solution.py:48
  176.3 9.3 %all-to-all-start.2 = ((bf16[32,128,250]{2,1,0:T(8,128)(2,1)}), bf16[32,128,250]{2,1,0:T(8,128)(2,1)}, u32[]{:S(2)}, u32[]{:S(2)}) async-start(bf16[32,128,250]{2,1,0:T(8,128)(2,1)} %gather_fusion.2), calls=%async_computation.2 | async-start | bytes 4194304 | tf_op jit(solution)/shard_map/all_to_all | solution.py:68
  185.7 7.2 fusion
  192.9 1.0 copy.177
  194.1 2.1 gather_fusion.12
  196.2 3.1 gather_fusion.7
  199.3 5.0 gather_fusion.1
  204.3 9.6 %all-to-all-done.2 = bf16[32,128,250]{2,1,0:T(8,128)(2,1)} async-done(((bf16[32,128,250]{2,1,0:T(8,128)(2,1)}), bf16[32,128,250]{2,1,0:T(8,128)(2,1)}, u32[]{:S(2)}, u32[]{:S(2)}) %all-to-all-start.2) | async-done | bytes 2048032 | tf_op jit(solution)/shard_map/all_to_all | solution.py:68
  214.0 6.5 all-to-all-start.7
  220.5 2.5 select_reduce_fusion.1
  223.3 24.3 %all-gather = f32[16,6,128]{2,1,0:T(8,128)S(1)} all-gather(f32[2,6,128]{2,1,0:T(8,128)S(1)} %pad_maximum_fusion.1), channel_id=2, replica_groups=mesh['row'=8,'col'=32] {'row'}, dimensions={0}, use_global_device_ids=true | all-gather | bytes 55296 | tf_op jit(solution)/shard_map/all_gather | solution.py:56
  249.1 2.2 gather_fusion.5
  251.7 68.9 %all-reduce.5.cloned.1.call-done = bf16[768,250]{0,1:T(8,128)(2,1)} async-done(((bf16[768,250]{0,1:T(8,128)(2,1)}), bf16[768,250]{0,1:T(8,128)(2,1)}) %all-reduce.5.cloned.1.call-update) | async-done | bytes 384016 | tf_op jit(solution)/shard_map/psum | solution.py:74
  321.6 2.2 gather_fusion.3
  324.1 70.6 %all-reduce.7.cloned.1.call-done = bf16[768,250]{0,1:T(8,128)(2,1)} async-done(((bf16[768,250]{0,1:T(8,128)(2,1)}), bf16[768,250]{0,1:T(8,128)(2,1)}) %all-reduce.7.cloned.1.call-update) | async-done | bytes 384016 | tf_op jit(solution)/shard_map/psum | solution.py:74
  395.7 2.2 gather_fusion.13
  398.3 70.6 %all-reduce.9.cloned.1.call-done = bf16[768,250]{0,1:T(8,128)(2,1)} async-done(((bf16[768,250]{0,1:T(8,128)(2,1)}), bf16[768,250]{0,1:T(8,128)(2,1)}) %all-reduce.9.cloned.1.call-update) | async-done | bytes 384016 | tf_op jit(solution)/shard_map/psum | solution.py:74
  469.8 73.1 %all-reduce.11.cloned.1.call-done = bf16[768,250]{0,1:T(8,128)(2,1)} async-done(((bf16[768,250]{0,1:T(8,128)(2,1)}), bf16[768,250]{0,1:T(8,128)(2,1)}) %all-reduce.11.cloned.1.call-update) | async-done | bytes 384016 | tf_op jit(solution)/shard_map/psum | solution.py:74
  542.9 2.8 fusion.4
  545.7 1.2 copy.188
  546.9 2.0 gather_fusion.10
  548.9 12.9 %all-to-all-start.6 = ((bf16[32,128,250]{2,1,0:T(8,128)(2,1)}), bf16[32,128,250]{2,1,0:T(8,128)(2,1)}, u32[]{:S(2)}, u32[]{:S(2)}) async-start(bf16[32,128,250]{2,1,0:T(8,128)(2,1)} %gather_fusion.10), calls=%async_computation.6 | async-start | bytes 4194304 | tf_op jit(solution)/shard_map/all_to_all | solution.py:80
  562.0 2.0 gather_fusion.8
  564.0 26.4 %all-to-all-done.6 = bf16[32,128,250]{2,1,0:T(8,128)(2,1)} async-done(((bf16[32,128,250]{2,1,0:T(8,128)(2,1)}), bf16[32,128,250]{2,1,0:T(8,128)(2,1)}, u32[]{:S(2)}, u32[]{:S(2)}) %all-to-all-start.6) | async-done | bytes 2048032 | tf_op jit(solution)/shard_map/all_to_all | solution.py:80
  590.4 6.1 all-to-all-start.5
  596.7 2.0 gather_fusion.14
  598.7 26.2 %all-to-all-done.5 = bf16[32,128,250]{2,1,0:T(8,128)(2,1)} async-done(((bf16[32,128,250]{2,1,0:T(8,128)(2,1)}), bf16[32,128,250]{2,1,0:T(8,128)(2,1)}, u32[]{:S(2)}, u32[]{:S(2)}) %all-to-all-start.5) | async-done | bytes 2048032 | tf_op jit(solution)/shard_map/all_to_all | solution.py:80
  624.9 6.5 all-to-all-start.8
  631.4 2.2 gather_fusion.11
  633.6 1.1 convolution_convert_fusion.3
  634.9 2.0 gather_fusion.16
  636.9 22.8 %all-to-all-done.8 = bf16[32,128,250]{2,1,0:T(8,128)(2,1)} async-done(((bf16[32,128,250]{2,1,0:T(8,128)(2,1)}), bf16[32,128,250]{2,1,0:T(8,128)(2,1)}, u32[]{:S(2)}, u32[]{:S(2)}) %all-to-all-start.8) | async-done | bytes 2048032 | tf_op jit(solution)/shard_map/all_to_all | solution.py:80
  659.7 6.5 all-to-all-start.9
  666.2 2.2 gather_fusion.9
  668.4 1.1 convolution_convert_fusion.4
  670.5 2.2 gather_fusion.15
  672.7 1.1 convolution_convert_fusion.1
  673.8 31.6 %reduce-scatter.15.cloned.1.call-done = bf16[96,250]{1,0:T(8,128)(2,1)} async-done(((bf16[768,250]{1,0:T(8,128)(2,1)}), bf16[96,250]{1,0:T(8,128)(2,1)}) %reduce-scatter.15.cloned.1.call-update) | async-done | bytes 48016
  706.4 2.2 gather_fusion.17
  708.6 1.1 convolution_convert_fusion
  709.6 33.4 %reduce-scatter.17.cloned.1.call-done = bf16[96,250]{1,0:T(8,128)(2,1)} async-done(((bf16[768,250]{1,0:T(8,128)(2,1)}), bf16[96,250]{1,0:T(8,128)(2,1)}) %reduce-scatter.17.cloned.1.call-update) | async-done | bytes 48016
  744.0 1.0 fusion.9
  745.0 1.0 fusion.8
  746.0 1.0 fusion.7
  747.1 34.7 %reduce-scatter.19.cloned.1.call-done = bf16[96,250]{1,0:T(8,128)(2,1)} async-done(((bf16[768,250]{1,0:T(8,128)(2,1)}), bf16[96,250]{1,0:T(8,128)(2,1)}) %reduce-scatter.19.cloned.1.call-update) | async-done | bytes 48016
  783.1 12.6 %all_to_all.76 = bf16[96,8,125]{2,0,1:T(8,128)(2,1)S(1)} all-to-all(bf16[96,8,125]{2,0,1:T(8,128)(2,1)S(1)} %copy.203), channel_id=1, replica_groups=mesh['row'=8,'col'=32] {'row'}, dimensions={1} | all-to-all | bytes 384000 | tf_op jit(solution)/shard_map/all_to_all | solution.py:93
  (71 shorter events, 12.9 us)
Async XLA Ops:
  6.5 61.4 %copy-start = (bf16[768,768]{1,0:T(8,128)(2,1)S(1)}, bf16[768,768]{1,0:T(8,128)(2,1)}, u32[]{:S(2)}) copy-start(bf16[768,768]{1,0:T(8,128)(2,1)} %param.5) | copy-start | bytes 3538948
  8.8 15.5 %all-to-all-start = ((s32[32,1,1]{2,1,0:T(1,128)}), s32[32,1,1]{2,1,0:T(1,128)S(1)}, u32[]{:S(2)}, u32[]{:S(2)}) async-start(s32[32,1,1]{2,1,0:T(1,128)} %copy.173), calls=%async_computation | async-start | bytes 32768 | tf_op jit(solution)/shard_map/all_to_all | solution.py:31
  28.1 33.4 %all-to-all-start.4 = ((bf16[32,128,250]{2,1,0:T(8,128)(2,1)}), bf16[32,128,250]{2,1,0:T(8,128)(2,1)}, u32[]{:S(2)}, u32[]{:S(2)}) async-start(bf16[32,128,250]{2,1,0:T(8,128)(2,1)} %gather_fusion.6), calls=%async_computation.4 | async-start | bytes 4194304 | tf_op jit(solution)/shard_map/all_to_all | solution.py:68
  61.5 34.9 %all-to-all-start.3 = ((bf16[32,128,250]{2,1,0:T(8,128)(2,1)}), bf16[32,128,250]{2,1,0:T(8,128)(2,1)}, u32[]{:S(2)}, u32[]{:S(2)}) async-start(bf16[32,128,250]{2,1,0:T(8,128)(2,1)} %gather_fusion.4), calls=%async_computation.3 | async-start | bytes 4194304 | tf_op jit(solution)/shard_map/all_to_all | solution.py:68
  96.3 79.9 %all-to-all-start.1 = ((bf16[32,128,768]{2,1,0:T(8,128)(2,1)}), bf16[32,128,768]{2,1,0:T(8,128)(2,1)}, u32[]{:S(2)}, u32[]{:S(2)}) async-start(bf16[32,128,768]{2,1,0:T(8,128)(2,1)} %gather_fusion), calls=%async_computation.1 | async-start | bytes 12582912 | tf_op jit(solution)/shard_map/all_to_all | solution.py:48
  106.1 79.5 %copy-start.7 = (s32[6,2]{1,0:T(8,128)S(1)}, s32[6,2]{1,0:T(8,128)}, u32[]{:S(2)}) copy-start(s32[6,2]{1,0:T(8,128)} %get-tuple-element.29) | copy-start | bytes 148
  106.1 79.6 %copy-start.6 = (s32[768,50]{0,1:T(8,128)S(1)}, s32[768,50]{0,1:T(8,128)}, u32[]{:S(2)}) copy-start(s32[768,50]{0,1:T(8,128)} %param.9) | copy-start | bytes 460804
  106.1 88.0 %copy-start.8 = (f32[768]{0:T(1024)S(1)}, f32[768]{0:T(1024)}, u32[]{:S(2)}) copy-start(f32[768]{0:T(1024)} %param.7) | copy-start | bytes 9220
  176.3 37.7 %all-to-all-start.2 = ((bf16[32,128,250]{2,1,0:T(8,128)(2,1)}), bf16[32,128,250]{2,1,0:T(8,128)(2,1)}, u32[]{:S(2)}, u32[]{:S(2)}) async-start(bf16[32,128,250]{2,1,0:T(8,128)(2,1)} %gather_fusion.2), calls=%async_computation.2 | async-start | bytes 4194304 | tf_op jit(solution)/shard_map/all_to_all | solution.py:68
  204.3 16.2 %copy-start.3 = (pred[6,128,256]{1,2,0:T(32,128)(4,1)S(1)}, pred[6,128,256]{1,2,0:T(32,128)(4,1)}, u32[]{:S(2)}) copy-start(pred[6,128,256]{1,2,0:T(32,128)(4,1)} %copy.177) | copy-start | bytes 589828
  214.0 181.8 %all-to-all-start.7 = ((bf16[32,128,250]{2,1,0:T(8,128)(2,1)}), bf16[32,128,250]{2,1,0:T(8,128)(2,1)}, u32[]{:S(2)}, u32[]{:S(2)}) async-start(bf16[32,128,250]{2,1,0:T(8,128)(2,1)} %gather_fusion.12), calls=%async_computation.7 | async-start | bytes 4194304 | tf_op jit(solution)/shard_map/all_to_all | solution.py:68
  220.5 100.1 %all-reduce.5.cloned.1.call-start = ((), (), s32[]{:S(2)}) async-start(), calls=%async_computation.15 | async-start | bytes 786432 | tf_op jit(solution)/shard_map/psum | solution.py:74
  220.5 27.1 %copy-start.4 = (pred[6,128,256]{1,2,0:T(32,128)(4,1)S(1)}, pred[6,128,256]{1,2,0:T(32,128)(4,1)}, u32[]{:S(2)}) copy-start(pred[6,128,256]{1,2,0:T(32,128)(4,1)} %copy.177) | copy-start | bytes 589828
  223.0 24.8 %copy-start.2 = (bf16[12,128,250]{2,1,0:T(8,128)(2,1)S(1)}, bf16[12,128,250]{2,1,0:T(8,128)(2,1)}, u32[]{:S(2)}) copy-start(bf16[12,128,250]{2,1,0:T(8,128)(2,1)} %gather_fusion.7) | copy-start | bytes 2304004
  249.1 145.6 %all-reduce.7.cloned.1.call-start = ((), (), s32[]{:S(2)}) async-start(), calls=%async_computation.16 | async-start | bytes 786432 | tf_op jit(solution)/shard_map/psum | solution.py:74
  321.5 147.4 %all-reduce.9.cloned.1.call-start = ((), (), s32[]{:S(2)}) async-start(), calls=%async_computation.17 | async-start | bytes 786432 | tf_op jit(solution)/shard_map/psum | solution.py:74
  395.7 147.2 %all-reduce.11.cloned.1.call-start = ((), (), s32[]{:S(2)}) async-start(), calls=%async_computation.18 | async-start | bytes 786432 | tf_op jit(solution)/shard_map/psum | solution.py:74
  548.9 12.9 %copy-start.5 = (bf16[768,250]{0,1:T(8,128)(2,1)S(1)}, bf16[768,250]{0,1:T(8,128)(2,1)}, u32[]{:S(2)}) copy-start(bf16[768,250]{0,1:T(8,128)(2,1)} %get-tuple-element.33) | copy-start | bytes 1152004
  548.9 41.5 %all-to-all-start.6 = ((bf16[32,128,250]{2,1,0:T(8,128)(2,1)}), bf16[32,128,250]{2,1,0:T(8,128)(2,1)}, u32[]{:S(2)}, u32[]{:S(2)}) async-start(bf16[32,128,250]{2,1,0:T(8,128)(2,1)} %gather_fusion.10), calls=%async_computation.6 | async-start | bytes 4194304 | tf_op jit(solution)/shard_map/all_to_all | solution.py:80
  590.4 34.5 %all-to-all-start.5 = ((bf16[32,128,250]{2,1,0:T(8,128)(2,1)}), bf16[32,128,250]{2,1,0:T(8,128)(2,1)}, u32[]{:S(2)}, u32[]{:S(2)}) async-start(bf16[32,128,250]{2,1,0:T(8,128)(2,1)} %gather_fusion.8), calls=%async_computation.5 | async-start | bytes 4194304 | tf_op jit(solution)/shard_map/all_to_all | solution.py:80
  624.9 34.8 %all-to-all-start.8 = ((bf16[32,128,250]{2,1,0:T(8,128)(2,1)}), bf16[32,128,250]{2,1,0:T(8,128)(2,1)}, u32[]{:S(2)}, u32[]{:S(2)}) async-start(bf16[32,128,250]{2,1,0:T(8,128)(2,1)} %gather_fusion.14), calls=%async_computation.8 | async-start | bytes 4194304 | tf_op jit(solution)/shard_map/all_to_all | solution.py:80
  631.3 38.2 %reduce-scatter.13.cloned.1.call-start = ((), (), s32[]{:S(2)}) async-start(), calls=%async_computation.19 | async-start | bytes 442368
  659.7 46.7 %all-to-all-start.9 = ((bf16[32,128,250]{2,1,0:T(8,128)(2,1)}), bf16[32,128,250]{2,1,0:T(8,128)(2,1)}, u32[]{:S(2)}, u32[]{:S(2)}) async-start(bf16[32,128,250]{2,1,0:T(8,128)(2,1)} %gather_fusion.16), calls=%async_computation.9 | async-start | bytes 4194304 | tf_op jit(solution)/shard_map/all_to_all | solution.py:80
  666.2 39.2 %reduce-scatter.15.cloned.1.call-start = ((), (), s32[]{:S(2)}) async-start(), calls=%async_computation.20 | async-start | bytes 442368
  670.5 72.6 %reduce-scatter.17.cloned.1.call-start = ((), (), s32[]{:S(2)}) async-start(), calls=%async_computation.21 | async-start | bytes 442368
  706.3 75.4 %reduce-scatter.19.cloned.1.call-start = ((), (), s32[]{:S(2)}) async-start(), calls=%async_computation.22 | async-start | bytes 442368
  708.6 87.8 %copy-start.1 = (bf16[768,768]{1,0:T(8,128)(2,1)S(1)}, bf16[768,768]{1,0:T(8,128)(2,1)}, u32[]{:S(2)}) copy-start(bf16[768,768]{1,0:T(8,128)(2,1)} %param.5) | copy-start | bytes 3538948
Sparse Core Ops, SparseCore 0:
  249.2 71.3 all-reduce.4
  322.9 71.7 all-reduce.6
  397.0 71.8 all-reduce.8
  471.1 71.8 all-reduce.10
  634.8 32.3 reduce-scatter.12
  670.6 34.7 reduce-scatter.14
  707.9 35.1 reduce-scatter.16
  745.6 36.1 reduce-scatter.18

commit v3 on v1

v3 whole, which is shorter than its diff:
```python
import math

import jax
import jax.numpy as jnp
from jax import lax
from jax.sharding import PartitionSpec as P

BLOCK = 128
SLOTS = 16


mixing = 0.75
lowest_logit = -1e30


def body(embeds, labels, sharpness, pattern, mask_pos):
    rows_here, width = embeds.shape
    classes = labels.shape[1]
    n_col = lax.axis_size("col")
    n_row = lax.axis_size("row")
    row_pos = lax.axis_index("row")
    blocks_here = rows_here // BLOCK
    slots_here = SLOTS // n_row
    span = slots_here * BLOCK
    per_device = classes // n_row
    owners = pattern // blocks_here
    local_ids = pattern % blocks_here
    peers = jnp.arange(n_col, dtype=jnp.int32)
    grouped_owners = owners.reshape(blocks_here, n_row, slots_here)
    grouped_ids = local_ids.reshape(blocks_here, n_row, slots_here)
    wanted = jnp.max(
        jnp.where(grouped_owners[..., None] == peers, grouped_ids[..., None], 0), axis=(0, 2)
    )
    requested = lax.all_to_all(wanted.T, "col", split_axis=0, concat_axis=0, tiled=True)
    embedding_tiles = embeds.reshape(blocks_here, BLOCK, width)
    send_emb = embedding_tiles[lax.dynamic_index_in_dim(requested, row_pos, 1, keepdims=False)]
    my_labels = lax.dynamic_slice_in_dim(labels, row_pos * per_device, per_device, 1)
    lab_blocks = my_labels.reshape(blocks_here, BLOCK, per_device)
    send_lab = lab_blocks[requested]
    shifted = mask_pos - row_pos * span
    shifted = jnp.where((shifted >= 0) & (shifted < span), shifted, span)
    positions = jnp.arange(span, dtype=jnp.int32)
    in_mask = jnp.any(shifted[:, :, None] == positions[None, None, :], axis=1)
    in_mask = in_mask.reshape(blocks_here, BLOCK, span)

    my_owners = lax.dynamic_slice_in_dim(owners, row_pos * slots_here, slots_here, 1)
    fetched_emb = lax.all_to_all(send_emb, "col", split_axis=0, concat_axis=0, tiled=True)
    fetched_lab = lax.all_to_all(send_lab, "col", split_axis=0, concat_axis=0, tiled=True)
    candidate_ids = fetched_emb[my_owners].reshape(blocks_here, span, width)
    scores = jnp.einsum(
        "evg,erg->evr", embedding_tiles, candidate_ids, preferred_element_type=jnp.float32
    ) / math.sqrt(width)
    logits = scores * sharpness.reshape(blocks_here, BLOCK, 1)
    local_max = jnp.max(jnp.where(in_mask, logits, lowest_logit), axis=2)
    local_sum = jnp.sum(jnp.where(in_mask, jnp.exp(logits - local_max[..., None]), 0.0), axis=2)
    stats = lax.all_gather(jnp.stack([local_max, local_sum]), "row")
    top = jnp.max(stats[:, 0], axis=0)
    totals = jnp.sum(stats[:, 1] * jnp.exp(stats[:, 0] - top), axis=0)
    weight_matrix = jnp.where(
        in_mask, jnp.exp(logits - top[..., None]) / totals[..., None], 0.0
    ).astype(jnp.bfloat16)
    all_weights = lax.all_gather(weight_matrix, "row")
    group_ids = jnp.arange(SLOTS, dtype=jnp.int32) // slots_here

    def propagate_using(fetched, seed):
        candidates = fetched[owners, group_ids[None, :]]
        candidates = candidates.reshape(blocks_here, n_row, span, per_device)
        pieces = jnp.einsum(
            "gtmk,tgkc->gtmc", all_weights, candidates, preferred_element_type=jnp.float32
        ).astype(jnp.bfloat16)
        summed = jnp.sum(pieces.astype(jnp.float32), axis=0).reshape(rows_here, per_device)
        return (mixing * summed + (1.0 - mixing) * seed.astype(jnp.float32)).astype(jnp.bfloat16)

    spread = propagate_using(fetched_lab, my_labels)
    send_spread = spread.reshape(blocks_here, BLOCK, per_device)[requested]
    fetched_spread = lax.all_to_all(send_spread, "col", split_axis=0, concat_axis=0, tiled=True)
    return propagate_using(fetched_spread, my_labels)


def solution(mesh):
    placed = (P("col", None), P("col", None), P("col"), P("col", None), P("col", None))
    return jax.shard_map(
        body, mesh=mesh, in_specs=placed, out_specs=P("col", "row"), check_vma=False
    )
```

time: 500 us -> 394 us (0.79)
  waiting for transfers between devices: 234 us -> 116 us
  local copies, waits for them, and re-layouts: 51.2 us -> 90.6 us
  blocking collectives: 158 us -> 128 us
  starting transfers between devices: 14.8 us -> 23.3 us
    psum x1 -> x0, waiting for transfers between devices: 78.3 us -> none  [body(): lax.psum(partial_one.astype(jnp.bfloat16), 'row').astype(jnp.float32)]
    reduce_scatter x1 -> x0, waiting for transfers between devices: 32.3 us -> none  [body(): lax.psum_scatter(partial_two.astype(jnp.bfloat16), 'row', scatter_dimensi...]
    all_to_all x2 -> x0, blocking collectives: 28.3 us -> none  [the longest x1 15.3 us: body(): lax.all_to_all(wanted, 'col', split_axis=0, concat_axis=0, tiled=True)]
    all_to_all x3, local copies, waits for them, and re-layouts: 0.37 us -> 24.4 us  [the longest x1 11.9 us: body(): lax.all_to_all(send_lab, 'col', split_axis=0, concat_axis=0, tiled=True)]
    gather x1 -> x2, local copies, waits for them, and re-layouts: 4.88 us -> 20.2 us  [body(): send_lab = lab_blocks[requested]]
    all_to_all x1, waiting for transfers between devices: 64.8 us -> 52.7 us  [body(): lax.all_to_all(send_emb, 'col', split_axis=0, concat_axis=0, tiled=True)]
    gather x7 -> x6, local copies, waits for them, and re-layouts: 33.5 us -> 43.2 us  [the longest x2 20.2 us: body(): send_spread = spread.reshape(blocks_here, BLOCK, per_device)[requested]]
    all_to_all x0 -> x1, starting transfers between devices: none -> 8.58 us  [body(): lax.all_to_all(wanted.T, 'col', split_axis=0, concat_axis=0, tiled=True)]
  transfers between devices with their start and end apart: 4 -> 4, of which waited for: 4 -> 3; matrix products, arithmetic and copies ran while one was open for 4% -> 14% of each run, Pallas kernels for 0% -> 0%
where the time goes in v3:
time: 394 us; the launch traced here: 392 us
  blocking collectives  128 us (32%)
  waiting for transfers between devices  116 us (29%)
  local copies, waits for them, and re-layouts  90.6 us (23%)
  starting transfers between devices  23.3 us (6%)
  between operations  13.6 us (3%)
  matrix products  10.4 us (3%)
  other arithmetic  9.59 us (2%)
    all_to_all x1, blocking collectives, body(): lax.all_to_all(send_spread, 'col', split_axis=0, concat_axis=0, tiled=True)  104 us
    all_to_all x1, waiting for transfers between devices, body(): lax.all_to_all(send_lab, 'col', split_axis=0, concat_axis=0, tiled=True)  56.8 us
    all_to_all x1, waiting for transfers between devices, body(): lax.all_to_all(send_emb, 'col', split_axis=0, concat_axis=0, tiled=True)  52.7 us
    all_gather x1, blocking collectives, body(): stats = lax.all_gather(jnp.stack([local_max, local_sum]), 'row')  24.7 us
    gather x2, local copies, waits for them, and re-layouts, body(): send_lab = lab_blocks[requested]  20.2 us
    gather x2, local copies, waits for them, and re-layouts, body(): send_spread = spread.reshape(blocks_here, BLOCK, per_device)[requested]  20.2 us
    gather x2, local copies, waits for them, and re-layouts, propagate_using(): candidates = fetched[owners, group_ids[None, :]]  13.1 us
    all_to_all x1, local copies, waits for them, and re-layouts, body(): lax.all_to_all(send_lab, 'col', split_axis=0, concat_axis=0, tiled=True)  11.9 us
  transfers between devices with their start and end apart: 4, of which 3 were waited for; matrix products, arithmetic and copies ran while one was open for 14% of the time, Pallas kernels for 0%

profile of v3, /device:TPU:1, one launch (start us, length us, event | category | flops | bytes accessed | tf_op | source)
XLA Modules:
  0.0 392.4 jit_solution(2725386275091367859)
XLA Ops:
  6.5 0.0 copy-start
  6.5 0.8 add_select_fusion.1
  7.4 0.1 copy.134
  7.4 0.1 copy.135
  7.5 0.1 copy.136
  7.6 0.1 copy.137
  7.7 0.1 select_reduce_fusion.2
  7.8 0.7 copy.138
  8.5 8.6 %all-to-all-start = ((s32[32,1,8]{2,1,0:T(1,128)}), s32[32,1,8]{2,1,0:T(1,128)S(1)}, u32[]{:S(2)}, u32[]{:S(2)}) async-start(s32[32,1,8]{2,1,0:T(1,128)} %copy.138), calls=%async_computation | async-start | bytes 32768 | tf_op jit(solution)/shard_map/all_to_all | solution.py:34
  17.1 6.9 %all-to-all-done = s32[32,1,8]{2,1,0:T(1,128)S(1)} async-done(((s32[32,1,8]{2,1,0:T(1,128)}), s32[32,1,8]{2,1,0:T(1,128)S(1)}, u32[]{:S(2)}, u32[]{:S(2)}) %all-to-all-start) | async-done | bytes 1056 | tf_op jit(solution)/shard_map/all_to_all | solution.py:34
  24.0 0.7 dynamic-slice_reduce_fusion
  24.7 4.9 %gather_fusion = bf16[32,128,768]{2,1,0:T(8,128)(2,1)} fusion(bf16[6,128,768]{2,1,0:T(8,128)(2,1)} %bitcast.66, s32[1024]{0:T(1024)S(1)} %pad_clamp_fusion.2), kind=kCustom, calls=%fused_computation | custom fusion | bytes 12583040 | tf_op jit(solution)/shard_map/gather | solution.py:36
  29.6 5.1 %all-to-all-start.1 = ((bf16[32,128,768]{2,1,0:T(8,128)(2,1)}), bf16[32,128,768]{2,1,0:T(8,128)(2,1)}, u32[]{:S(2)}, u32[]{:S(2)}) async-start(bf16[32,128,768]{2,1,0:T(8,128)(2,1)} %gather_fusion), calls=%async_computation.1 | async-start | bytes 12582912 | tf_op jit(solution)/shard_map/all_to_all | solution.py:47
  34.8 0.0 copy-done
  34.8 0.1 constant_dynamic-slice_fusion
  34.8 0.2 copy.158
  35.0 0.1 reshape.129
  35.1 8.5 %gather_fusion.2 = bf16[256,128,125]{2,1,0:T(8,128)(2,1)} fusion(bf16[6,128,125]{2,1,0:T(8,128)(2,1)S(1)} %bitcast.62, s32[1024]{0:T(1024)S(1)} %pad_clamp_fusion), kind=kCustom, calls=%fused_computation.2 | custom fusion | bytes 16385024 | tf_op jit(solution)/shard_map/gather | solution.py:39
  43.6 11.8 %copy.146 = bf16[32,8,128,125]{2,1,3,0:T(8,128)(2,1)} copy(bf16[32,8,128,125]{3,2,1,0:T(8,128)(2,1)} %bitcast.65) | data formatting | bytes 16384000 | tf_op jit(solution)/shard_map/gather | solution.py:39
  55.4 0.0 copy-start.3
  55.4 0.0 copy-start.5
  55.4 52.7 %all-to-all-done.1 = bf16[32,128,768]{2,1,0:T(8,128)(2,1)} async-done(((bf16[32,128,768]{2,1,0:T(8,128)(2,1)}), bf16[32,128,768]{2,1,0:T(8,128)(2,1)}, u32[]{:S(2)}, u32[]{:S(2)}) %all-to-all-start.1) | async-done | bytes 6291488 | tf_op jit(solution)/shard_map/all_to_all | solution.py:47
  108.1 9.5 %all-to-all-start.2 = ((bf16[32,8,128,125]{2,1,3,0:T(8,128)(2,1)}), bf16[32,8,128,125]{2,1,3,0:T(8,128)(2,1)}, u32[]{:S(2)}, u32[]{:S(2)}) async-start(bf16[32,8,128,125]{2,1,3,0:T(8,128)(2,1)} %copy.146), calls=%async_computation.2 | async-start | bytes 16384000 | tf_op jit(solution)/shard_map/all_to_all | solution.py:48
  117.6 0.0 copy-start.2
  117.6 0.0 all-gather.4.cloned.1.call-start
  117.7 0.1 compare_select_fusion.2
  117.8 0.1 reshape.121
  117.9 0.0 copy-done.3
  117.9 7.2 %fusion = pred[768,256]{1,0:T(8,128)(4,1)S(1)} fusion(s32[768,50]{0,1:T(8,128)S(1)} %and_select_fusion), kind=kLoop, calls=%fused_computation.7 | loop fusion | flops 19464192 | bytes 350208 | tf_op jit(solution)/shard_map/reduce_or | solution.py:43
  125.1 0.3 copy.142
  125.4 0.0 copy-done.5
  125.4 5.0 %gather_fusion.1 = bf16[12,128,768]{2,1,0:T(8,128)(2,1)} fusion(bf16[32,128,768]{2,1,0:T(8,128)(2,1)} %all-to-all-done.1, s32[1024]{0:T(1024)S(1)} %pad_clamp_fusion.1), kind=kCustom, calls=%fused_computation.1 | custom fusion | bytes 4718640 | tf_op jit(solution)/shard_map/gather | solution.py:49
  130.4 0.0 copy-done.2
  130.4 0.0 copy-start.4
  130.4 2.5 select_reduce_fusion.1
  132.9 0.2 select_reduce_fusion
  133.1 24.7 %all-gather = f32[16,6,128]{2,1,0:T(8,128)S(1)} all-gather(f32[2,6,128]{2,1,0:T(8,128)S(1)} %pad_maximum_fusion), channel_id=2, replica_groups=mesh['row'=8,'col'=32] {'row'}, dimensions={0}, use_global_device_ids=true | all-gather | bytes 55296 | tf_op jit(solution)/shard_map/all_gather | solution.py:56
  157.8 0.2 select_convert_fusion
  158.0 0.9 copy.143
  159.0 0.0 all-gather.4.cloned.1.call-update
  159.0 0.0 copy-done.4
  159.0 0.1 reshape.135
  159.1 56.8 %all-to-all-done.2 = bf16[32,8,128,125]{2,1,3,0:T(8,128)(2,1)} async-done(((bf16[32,8,128,125]{2,1,3,0:T(8,128)(2,1)}), bf16[32,8,128,125]{2,1,3,0:T(8,128)(2,1)}, u32[]{:S(2)}, u32[]{:S(2)}) %all-to-all-start.2) | async-done | bytes 8192032 | tf_op jit(solution)/shard_map/all_to_all | solution.py:48
  215.9 11.9 %copy.147 = bf16[32,8,128,125]{3,2,1,0:T(8,128)(2,1)} copy(bf16[32,8,128,125]{2,1,3,0:T(8,128)(2,1)} %all-to-all-done.2) | data formatting | bytes 16384000 | tf_op jit(solution)/shard_map/all_to_all | solution.py:48
  227.7 6.5 %gather_fusion.3 = bf16[96,128,125]{2,1,0:T(8,128)(2,1)} fusion(bf16[32,8,128,125]{3,2,1,0:T(8,128)(2,1)} %copy.147, s32[96]{0:T(128)S(1)} %reshape.135), kind=kCustom, calls=%fused_computation.3 | custom fusion | bytes 6144768 | tf_op jit(solution)/shard_map/gather | solution.py:66
  234.3 0.0 all-gather.4.cloned.1.call-done
  234.3 4.0 %convert_reduce_fusion.1 = f32[6,128,125]{2,1,0:T(8,128)S(1)} fusion(bf16[8,6,128,256]{3,2,1,0:T(8,128)(2,1)} %bitcast.80, bf16[6,8,256,125]{3,2,1,0:T(8,128)(2,1)} %bitcast.68), kind=kOutput, calls=%fused_computation.13 | convolution fusion | flops 395424000 | bytes 6601728 | tf_op jit(solution)/shard_map/gtmk,tgkc->gtmc/dot_general | solution.py:68
  238.3 0.1 fusion.17
  238.4 8.5 %gather_fusion.4 = bf16[256,128,125]{2,1,0:T(8,128)(2,1)} fusion(bf16[6,128,125]{2,1,0:T(8,128)(2,1)S(1)} %bitcast.63, s32[1024]{0:T(1024)S(1)} %pad_clamp_fusion), kind=kCustom, calls=%fused_computation.4 | custom fusion | bytes 16385024 | tf_op jit(solution)/shard_map/gather | solution.py:75
  246.9 11.8 %copy.150 = bf16[32,8,128,125]{2,1,3,0:T(8,128)(2,1)} copy(bf16[32,8,128,125]{3,2,1,0:T(8,128)(2,1)} %bitcast.64) | data formatting | bytes 16384000 | tf_op jit(solution)/shard_map/gather | solution.py:75
  258.6 103.7 %all_to_all.27 = bf16[32,8,128,125]{2,1,3,0:T(8,128)(2,1)} all-to-all(bf16[32,8,128,125]{2,1,3,0:T(8,128)(2,1)} %copy.150), channel_id=1, replica_groups=mesh['row'=8,'col'=32] {'col'}, dimensions={0} | all-to-all | bytes 16384000 | tf_op jit(solution)/shard_map/all_to_all | solution.py:76
  362.4 11.9 %copy.151 = bf16[32,8,128,125]{3,2,1,0:T(8,128)(2,1)} copy(bf16[32,8,128,125]{2,1,3,0:T(8,128)(2,1)} %all_to_all.27) | data formatting | bytes 16384000 | tf_op jit(solution)/shard_map/all_to_all | solution.py:76
  374.2 6.5 %gather_fusion.5 = bf16[96,128,125]{2,1,0:T(8,128)(2,1)} fusion(bf16[32,8,128,125]{3,2,1,0:T(8,128)(2,1)} %copy.151, s32[96]{0:T(128)S(1)} %reshape.135), kind=kCustom, calls=%fused_computation.5 | custom fusion | bytes 6144768 | tf_op jit(solution)/shard_map/gather | solution.py:66
  380.8 0.0 copy-start.1
  380.8 4.0 %convert_reduce_fusion = f32[6,128,125]{2,1,0:T(8,128)S(1)} fusion(bf16[8,6,128,256]{3,2,1,0:T(8,128)(2,1)} %bitcast.81, bf16[6,8,256,125]{3,2,1,0:T(8,128)(2,1)} %bitcast.69), kind=kOutput, calls=%fused_computation.12 | convolution fusion | flops 395424000 | bytes 6601728 | tf_op jit(solution)/shard_map/gtmk,tgkc->gtmc/dot_general | solution.py:68
  384.8 0.7 fusion.16
  385.5 0.0 copy-done.1
  (14 shorter events, 0.2 us)
Async XLA Ops:
  6.5 28.2 %copy-start = (bf16[768,1000]{0,1:T(8,128)(2,1)S(1)}, bf16[768,1000]{0,1:T(8,128)(2,1)}, u32[]{:S(2)}) copy-start(bf16[768,1000]{0,1:T(8,128)(2,1)} %param.6) | copy-start | bytes 4608004
  8.5 15.5 %all-to-all-start = ((s32[32,1,8]{2,1,0:T(1,128)}), s32[32,1,8]{2,1,0:T(1,128)S(1)}, u32[]{:S(2)}, u32[]{:S(2)}) async-start(s32[32,1,8]{2,1,0:T(1,128)} %copy.138), calls=%async_computation | async-start | bytes 32768 | tf_op jit(solution)/shard_map/all_to_all | solution.py:34
  29.6 78.5 %all-to-all-start.1 = ((bf16[32,128,768]{2,1,0:T(8,128)(2,1)}), bf16[32,128,768]{2,1,0:T(8,128)(2,1)}, u32[]{:S(2)}, u32[]{:S(2)}) async-start(bf16[32,128,768]{2,1,0:T(8,128)(2,1)} %gather_fusion), calls=%async_computation.1 | async-start | bytes 12582912 | tf_op jit(solution)/shard_map/all_to_all | solution.py:47
  55.4 62.5 %copy-start.3 = (s32[768,50]{0,1:T(8,128)S(1)}, s32[768,50]{0,1:T(8,128)}, u32[]{:S(2)}) copy-start(s32[768,50]{0,1:T(8,128)} %param.9) | copy-start | bytes 460804
  55.4 70.0 %copy-start.5 = (f32[768]{0:T(1024)S(1)}, f32[768]{0:T(1024)}, u32[]{:S(2)}) copy-start(f32[768]{0:T(1024)} %param.7) | copy-start | bytes 9220
  108.1 107.8 %all-to-all-start.2 = ((bf16[32,8,128,125]{2,1,3,0:T(8,128)(2,1)}), bf16[32,8,128,125]{2,1,3,0:T(8,128)(2,1)}, u32[]{:S(2)}, u32[]{:S(2)}) async-start(bf16[32,8,128,125]{2,1,3,0:T(8,128)(2,1)} %copy.146), calls=%async_computation.2 | async-start | bytes 16384000 | tf_op jit(solution)/shard_map/all_to_all | solution.py:48
  117.6 12.8 %copy-start.2 = (bf16[768,768]{1,0:T(8,128)(2,1)S(1)}, bf16[768,768]{1,0:T(8,128)(2,1)}, u32[]{:S(2)}) copy-start(bf16[768,768]{1,0:T(8,128)(2,1)} %param.5) | copy-start | bytes 3538948
  117.6 116.7 %all-gather.4.cloned.1.call-start = ((), (), s32[]{:S(2)}) async-start(), calls=%async_computation.4 | async-start | bytes 3538944 | tf_op jit(solution)/shard_map/all_gather | solution.py:62
  130.4 28.6 %copy-start.4 = (s32[6,16]{1,0:T(8,128)S(1)}, s32[6,16]{1,0:T(8,128)}, u32[]{:S(2)}) copy-start(s32[6,16]{1,0:T(8,128)} %param.8) | copy-start | bytes 1156
  380.8 4.8 %copy-start.1 = (bf16[768,1000]{0,1:T(8,128)(2,1)S(1)}, bf16[768,1000]{0,1:T(8,128)(2,1)}, u32[]{:S(2)}) copy-start(bf16[768,1000]{0,1:T(8,128)(2,1)} %param.6) | copy-start | bytes 4608004
Sparse Core Ops, SparseCore 0:
  159.1 47.1 all-gather.3

commit v4 on v3

--- a/solution.py
+++ b/solution.py
@@ -35,7 +35,9 @@
     embedding_tiles = embeds.reshape(blocks_here, BLOCK, width)
     send_emb = embedding_tiles[lax.dynamic_index_in_dim(requested, row_pos, 1, keepdims=False)]
     my_labels = lax.dynamic_slice_in_dim(labels, row_pos * per_device, per_device, 1)
-    lab_blocks = my_labels.reshape(blocks_here, BLOCK, per_device)
+    lanes = -(-per_device // 128) * 128
+    padded_labels = jnp.pad(my_labels, ((0, 0), (0, lanes - per_device)))
+    lab_blocks = padded_labels.reshape(blocks_here, BLOCK, lanes)
     send_lab = lab_blocks[requested]
     shifted = mask_pos - row_pos * span
     shifted = jnp.where((shifted >= 0) & (shifted < span), shifted, span)
@@ -64,17 +66,17 @@
 
     def propagate_using(fetched, seed):
         candidates = fetched[owners, group_ids[None, :]]
-        candidates = candidates.reshape(blocks_here, n_row, span, per_device)
+        candidates = candidates.reshape(blocks_here, n_row, span, lanes)
         pieces = jnp.einsum(
             "gtmk,tgkc->gtmc", all_weights, candidates, preferred_element_type=jnp.float32
         ).astype(jnp.bfloat16)
-        summed = jnp.sum(pieces.astype(jnp.float32), axis=0).reshape(rows_here, per_device)
+        summed = jnp.sum(pieces.astype(jnp.float32), axis=0).reshape(rows_here, lanes)
         return (mixing * summed + (1.0 - mixing) * seed.astype(jnp.float32)).astype(jnp.bfloat16)
 
-    spread = propagate_using(fetched_lab, my_labels)
-    send_spread = spread.reshape(blocks_here, BLOCK, per_device)[requested]
+    spread = propagate_using(fetched_lab, padded_labels)
+    send_spread = spread.reshape(blocks_here, BLOCK, lanes)[requested]
     fetched_spread = lax.all_to_all(send_spread, "col", split_axis=0, concat_axis=0, tiled=True)
-    return propagate_using(fetched_spread, my_labels)
+    return propagate_using(fetched_spread, padded_labels)[:, :per_device]
 
 
 def solution(mesh):

time: 394 us -> 362 us (0.919)
  local copies, waits for them, and re-layouts: 90.6 us -> 53.5 us
  waiting for transfers between devices: 116 us -> 120 us
    all_to_all x2 -> x0, local copies, waits for them, and re-layouts: 23.7 us -> none  [the longest x1 11.9 us: body(): lax.all_to_all(send_lab, 'col', split_axis=0, concat_axis=0, tiled=True)]
    gather x2 -> x1, local copies, waits for them, and re-layouts: 20.2 us -> 8.34 us  [body(): send_spread = spread.reshape(blocks_here, BLOCK, lanes)[requested]]
  transfers between devices with their start and end apart: 4 -> 4, of which waited for: 3 -> 3; matrix products, arithmetic and copies ran while one was open for 14% -> 12% of each run, Pallas kernels for 0% -> 0%
where the time goes in v4:
time: 362 us; the launch traced here: 361 us
  blocking collectives  131 us (36%)
  waiting for transfers between devices  120 us (33%)
  local copies, waits for them, and re-layouts  53.5 us (15%)
  starting transfers between devices  23.3 us (6%)
  between operations  13.6 us (4%)
  matrix products  10.2 us (3%)
  other arithmetic  9.6 us (3%)
    all_to_all x1, blocking collectives, body(): lax.all_to_all(send_spread, 'col', split_axis=0, concat_axis=0, tiled=True)  106 us
    all_to_all x1, waiting for transfers between devices, body(): lax.all_to_all(send_lab, 'col', split_axis=0, concat_axis=0, tiled=True)  59.2 us
    all_to_all x1, waiting for transfers between devices, body(): lax.all_to_all(send_emb, 'col', split_axis=0, concat_axis=0, tiled=True)  54.1 us
    all_gather x1, blocking collectives, body(): stats = lax.all_gather(jnp.stack([local_max, local_sum]), 'row')  24.7 us
    gather x2, local copies, waits for them, and re-layouts, body(): send_lab = lab_blocks[requested]  18.8 us
    gather x2, local copies, waits for them, and re-layouts, propagate_using(): candidates = fetched[owners, group_ids[None, :]]  13 us
    all_to_all x1, starting transfers between devices, body(): lax.all_to_all(send_lab, 'col', split_axis=0, concat_axis=0, tiled=True)  9.53 us
    all_to_all x1, starting transfers between devices, body(): lax.all_to_all(wanted.T, 'col', split_axis=0, concat_axis=0, tiled=True)  8.58 us
  transfers between devices with their start and end apart: 4, of which 3 were waited for; matrix products, arithmetic and copies ran while one was open for 12% of the time, Pallas kernels for 0%

profile of v4, /device:TPU:1, one launch (start us, length us, event | category | flops | bytes accessed | tf_op | source)
XLA Modules:
  0.0 361.3 jit_solution(9340094371633917855)
XLA Ops:
  6.5 0.0 copy-start
  6.5 0.8 add_select_fusion.1
  7.4 0.1 copy.84
  7.4 0.1 copy.85
  7.5 0.1 copy.86
  7.6 0.1 copy.87
  7.7 0.1 select_reduce_fusion.2
  7.8 0.7 copy.88
  8.5 8.6 %all-to-all-start = ((s32[32,1,8]{2,1,0:T(1,128)}), s32[32,1,8]{2,1,0:T(1,128)S(1)}, u32[]{:S(2)}, u32[]{:S(2)}) async-start(s32[32,1,8]{2,1,0:T(1,128)} %copy.88), calls=%async_computation | async-start | bytes 32768 | tf_op jit(solution)/shard_map/all_to_all | solution.py:34
  17.1 6.9 %all-to-all-done = s32[32,1,8]{2,1,0:T(1,128)S(1)} async-done(((s32[32,1,8]{2,1,0:T(1,128)}), s32[32,1,8]{2,1,0:T(1,128)S(1)}, u32[]{:S(2)}, u32[]{:S(2)}) %all-to-all-start) | async-done | bytes 1056 | tf_op jit(solution)/shard_map/all_to_all | solution.py:34
  24.0 0.7 dynamic-slice_reduce_fusion
  24.7 4.9 %gather_fusion = bf16[32,128,768]{2,1,0:T(8,128)(2,1)} fusion(bf16[6,128,768]{2,1,0:T(8,128)(2,1)} %bitcast.63, s32[1024]{0:T(1024)S(1)} %pad_clamp_fusion.2), kind=kCustom, calls=%fused_computation | custom fusion | bytes 12583040 | tf_op jit(solution)/shard_map/gather | solution.py:36
  29.6 5.1 %all-to-all-start.1 = ((bf16[32,128,768]{2,1,0:T(8,128)(2,1)}), bf16[32,128,768]{2,1,0:T(8,128)(2,1)}, u32[]{:S(2)}, u32[]{:S(2)}) async-start(bf16[32,128,768]{2,1,0:T(8,128)(2,1)} %gather_fusion), calls=%async_computation.1 | async-start | bytes 12582912 | tf_op jit(solution)/shard_map/all_to_all | solution.py:49
  34.8 0.0 copy-done
  34.8 0.1 constant_dynamic-slice_fusion
  34.8 0.2 copy.98
  35.0 0.1 reshape.127
  35.1 8.3 %gather_fusion.2 = bf16[256,128,125]{2,1,0:T(8,128)(2,1)} fusion(bf16[6,128,125]{2,1,0:T(8,128)(2,1)S(1)} %bitcast.59, s32[1024]{0:T(1024)S(1)} %pad_clamp_fusion), kind=kCustom, calls=%fused_computation.2 | custom fusion | bytes 16385024 | tf_op jit(solution)/shard_map/gather | solution.py:41
  43.5 10.5 %gather.27 = bf16[32,8,128,128]{3,2,1,0:T(8,128)(2,1)} pad(bf16[32,8,128,125]{3,2,1,0:T(8,128)(2,1)} %bitcast.61, bf16[]{:T(256)} %constant.84.clone.1), padding=0_0x0_0x0_0x0_3 | pad | bytes 16580610 | tf_op jit(solution)/shard_map/gather | solution.py:41
  53.9 0.0 copy-start.3
  53.9 0.0 copy-start.5
  53.9 54.1 %all-to-all-done.1 = bf16[32,128,768]{2,1,0:T(8,128)(2,1)} async-done(((bf16[32,128,768]{2,1,0:T(8,128)(2,1)}), bf16[32,128,768]{2,1,0:T(8,128)(2,1)}, u32[]{:S(2)}, u32[]{:S(2)}) %all-to-all-start.1) | async-done | bytes 6291488 | tf_op jit(solution)/shard_map/all_to_all | solution.py:49
  108.1 9.5 %all-to-all-start.2 = ((bf16[32,8,128,128]{3,2,1,0:T(8,128)(2,1)}), bf16[32,8,128,128]{3,2,1,0:T(8,128)(2,1)}, u32[]{:S(2)}, u32[]{:S(2)}) async-start(bf16[32,8,128,128]{3,2,1,0:T(8,128)(2,1)} %gather.27), calls=%async_computation.2 | async-start | bytes 16777216 | tf_op jit(solution)/shard_map/all_to_all | solution.py:50
  117.6 0.0 copy-start.2
  117.6 0.0 all-gather.4.cloned.1.call-start
  117.7 0.1 compare_select_fusion.2
  117.7 0.1 reshape.119
  117.8 0.0 copy-done.3
  117.9 7.2 %fusion = pred[768,256]{1,0:T(8,128)(4,1)S(1)} fusion(s32[768,50]{0,1:T(8,128)S(1)} %and_select_fusion), kind=kLoop, calls=%fused_computation.7 | loop fusion | flops 19464192 | bytes 350208 | tf_op jit(solution)/shard_map/reduce_or | solution.py:45
  125.1 0.3 copy.92
  125.4 0.0 copy-done.5
  125.4 5.0 %gather_fusion.1 = bf16[12,128,768]{2,1,0:T(8,128)(2,1)} fusion(bf16[32,128,768]{2,1,0:T(8,128)(2,1)} %all-to-all-done.1, s32[1024]{0:T(1024)S(1)} %pad_clamp_fusion.1), kind=kCustom, calls=%fused_computation.1 | custom fusion | bytes 4718640 | tf_op jit(solution)/shard_map/gather | solution.py:51
  130.4 0.0 copy-done.2
  130.4 0.0 copy-start.4
  130.4 2.5 select_reduce_fusion.1
  132.9 0.2 select_reduce_fusion
  133.1 24.7 %all-gather = f32[16,6,128]{2,1,0:T(8,128)S(1)} all-gather(f32[2,6,128]{2,1,0:T(8,128)S(1)} %pad_maximum_fusion), channel_id=2, replica_groups=mesh['row'=8,'col'=32] {'row'}, dimensions={0}, use_global_device_ids=true | all-gather | bytes 55296 | tf_op jit(solution)/shard_map/all_gather | solution.py:58
  157.8 0.2 select_convert_fusion
  158.0 0.9 copy.93
  159.0 0.0 all-gather.4.cloned.1.call-update
  159.0 0.0 copy-done.4
  159.0 0.1 reshape.133
  159.1 59.2 %all-to-all-done.2 = bf16[32,8,128,128]{3,2,1,0:T(8,128)(2,1)} async-done(((bf16[32,8,128,128]{3,2,1,0:T(8,128)(2,1)}), bf16[32,8,128,128]{3,2,1,0:T(8,128)(2,1)}, u32[]{:S(2)}, u32[]{:S(2)}) %all-to-all-start.2) | async-done | bytes 8388640 | tf_op jit(solution)/shard_map/all_to_all | solution.py:50
  218.3 6.5 %gather_fusion.3 = bf16[96,128,128]{2,1,0:T(8,128)(2,1)} fusion(bf16[32,8,128,128]{3,2,1,0:T(8,128)(2,1)} %all-to-all-done.2, s32[96]{0:T(128)S(1)} %reshape.133), kind=kCustom, calls=%fused_computation.3 | custom fusion | bytes 6292224 | tf_op jit(solution)/shard_map/gather | solution.py:68
  224.8 0.0 all-gather.4.cloned.1.call-done
  224.8 3.8 %convert_reduce_fusion.1 = f32[6,128,128]{2,1,0:T(8,128)S(1)} fusion(bf16[8,6,128,256]{3,2,1,0:T(8,128)(2,1)} %bitcast.78, bf16[6,8,256,128]{3,2,1,0:T(8,128)(2,1)} %bitcast.65), kind=kOutput, calls=%fused_computation.13 | convolution fusion | flops 404914176 | bytes 6684672 | tf_op jit(solution)/shard_map/gtmk,tgkc->gtmc/dot_general | solution.py:70
  228.7 0.1 fusion.17
  228.7 8.3 %gather_fusion.4 = bf16[256,128,128]{2,1,0:T(8,128)(2,1)} fusion(bf16[6,128,128]{2,1,0:T(8,128)(2,1)S(1)} %bitcast.60, s32[1024]{0:T(1024)S(1)} %pad_clamp_fusion), kind=kCustom, calls=%fused_computation.4 | custom fusion | bytes 16778240 | tf_op jit(solution)/shard_map/gather | solution.py:77
  237.1 106.1 %all_to_all.27 = bf16[32,8,128,128]{3,2,1,0:T(8,128)(2,1)} all-to-all(bf16[32,8,128,128]{3,2,1,0:T(8,128)(2,1)} %bitcast.62), channel_id=1, replica_groups=mesh['row'=8,'col'=32] {'col'}, dimensions={0} | all-to-all | bytes 16777216 | tf_op jit(solution)/shard_map/all_to_all | solution.py:78
  343.2 6.5 %gather_fusion.5 = bf16[96,128,128]{2,1,0:T(8,128)(2,1)} fusion(bf16[32,8,128,128]{3,2,1,0:T(8,128)(2,1)} %all_to_all.27, s32[96]{0:T(128)S(1)} %reshape.133), kind=kCustom, calls=%fused_computation.5 | custom fusion | bytes 6292224 | tf_op jit(solution)/shard_map/gather | solution.py:68
  349.7 0.0 copy-start.1
  349.7 3.9 %convert_reduce_fusion = f32[6,128,128]{2,1,0:T(8,128)S(1)} fusion(bf16[8,6,128,256]{3,2,1,0:T(8,128)(2,1)} %bitcast.79, bf16[6,8,256,128]{3,2,1,0:T(8,128)(2,1)} %bitcast.66), kind=kOutput, calls=%fused_computation.12 | convolution fusion | flops 404914176 | bytes 6684672 | tf_op jit(solution)/shard_map/gtmk,tgkc->gtmc/dot_general | solution.py:70
  353.7 0.7 fusion.16
  354.4 0.0 copy-done.1
  (14 shorter events, 0.2 us)
Async XLA Ops:
  6.5 28.2 %copy-start = (bf16[768,1000]{0,1:T(8,128)(2,1)S(1)}, bf16[768,1000]{0,1:T(8,128)(2,1)}, u32[]{:S(2)}) copy-start(bf16[768,1000]{0,1:T(8,128)(2,1)} %param.6) | copy-start | bytes 4608004
  8.5 15.5 %all-to-all-start = ((s32[32,1,8]{2,1,0:T(1,128)}), s32[32,1,8]{2,1,0:T(1,128)S(1)}, u32[]{:S(2)}, u32[]{:S(2)}) async-start(s32[32,1,8]{2,1,0:T(1,128)} %copy.88), calls=%async_computation | async-start | bytes 32768 | tf_op jit(solution)/shard_map/all_to_all | solution.py:34
  29.6 78.5 %all-to-all-start.1 = ((bf16[32,128,768]{2,1,0:T(8,128)(2,1)}), bf16[32,128,768]{2,1,0:T(8,128)(2,1)}, u32[]{:S(2)}, u32[]{:S(2)}) async-start(bf16[32,128,768]{2,1,0:T(8,128)(2,1)} %gather_fusion), calls=%async_computation.1 | async-start | bytes 12582912 | tf_op jit(solution)/shard_map/all_to_all | solution.py:49
  53.9 63.9 %copy-start.3 = (s32[768,50]{0,1:T(8,128)S(1)}, s32[768,50]{0,1:T(8,128)}, u32[]{:S(2)}) copy-start(s32[768,50]{0,1:T(8,128)} %param.9) | copy-start | bytes 460804
  53.9 71.5 %copy-start.5 = (f32[768]{0:T(1024)S(1)}, f32[768]{0:T(1024)}, u32[]{:S(2)}) copy-start(f32[768]{0:T(1024)} %param.7) | copy-start | bytes 9220
  108.1 110.2 %all-to-all-start.2 = ((bf16[32,8,128,128]{3,2,1,0:T(8,128)(2,1)}), bf16[32,8,128,128]{3,2,1,0:T(8,128)(2,1)}, u32[]{:S(2)}, u32[]{:S(2)}) async-start(bf16[32,8,128,128]{3,2,1,0:T(8,128)(2,1)} %gather.27), calls=%async_computation.2 | async-start | bytes 16777216 | tf_op jit(solution)/shard_map/all_to_all | solution.py:50
  117.6 12.8 %copy-start.2 = (bf16[768,768]{1,0:T(8,128)(2,1)S(1)}, bf16[768,768]{1,0:T(8,128)(2,1)}, u32[]{:S(2)}) copy-start(bf16[768,768]{1,0:T(8,128)(2,1)} %param.5) | copy-start | bytes 3538948
  117.6 107.2 %all-gather.4.cloned.1.call-start = ((), (), s32[]{:S(2)}) async-start(), calls=%async_computation.4 | async-start | bytes 3538944 | tf_op jit(solution)/shard_map/all_gather | solution.py:64
  130.4 28.6 %copy-start.4 = (s32[6,16]{1,0:T(8,128)S(1)}, s32[6,16]{1,0:T(8,128)}, u32[]{:S(2)}) copy-start(s32[6,16]{1,0:T(8,128)} %param.8) | copy-start | bytes 1156
  349.7 4.7 %copy-start.1 = (bf16[768,1000]{0,1:T(8,128)(2,1)S(1)}, bf16[768,1000]{0,1:T(8,128)(2,1)}, u32[]{:S(2)}) copy-start(bf16[768,1000]{0,1:T(8,128)(2,1)} %param.6) | copy-start | bytes 4608004
Sparse Core Ops, SparseCore 0:
  159.1 47.1 all-gather.3

commit v5 on v3

v5 whole, which is shorter than its diff:
```python
import math

import jax
import jax.numpy as jnp
from jax import lax
from jax.sharding import PartitionSpec as P

BLOCK = 128
SLOTS = 16


mixing = 0.75
lowest_logit = -1e30


def body(embeds, labels, sharpness, pattern, mask_pos):
    rows_here, width = embeds.shape
    classes = labels.shape[1]
    n_col = lax.axis_size("col")
    n_row = lax.axis_size("row")
    row_pos = lax.axis_index("row")
    blocks_here = rows_here // BLOCK
    slots_here = SLOTS // n_row
    span = slots_here * BLOCK
    per_device = classes // n_row
    owners = pattern // blocks_here
    local_ids = pattern % blocks_here
    my_owners = lax.dynamic_slice_in_dim(owners, row_pos * slots_here, slots_here, 1)
    my_ids = lax.dynamic_slice_in_dim(local_ids, row_pos * slots_here, slots_here, 1)
    peers = jnp.arange(n_col, dtype=jnp.int32)
    wanted = jnp.max(jnp.where(my_owners[..., None] == peers, my_ids[..., None], 0), axis=(0, 1))
    requested = lax.all_to_all(wanted, "col", split_axis=0, concat_axis=0, tiled=True)
    embedding_tiles = embeds.reshape(blocks_here, BLOCK, width)
    send_emb = embedding_tiles[requested]
    my_labels = lax.dynamic_slice_in_dim(labels, row_pos * per_device, per_device, 1)
    all_labels = lax.all_gather(my_labels, "col", tiled=True)
    shifted = mask_pos - row_pos * span
    shifted = jnp.where((shifted >= 0) & (shifted < span), shifted, span)
    positions = jnp.arange(span, dtype=jnp.int32)
    in_mask = jnp.any(shifted[:, :, None] == positions[None, None, :], axis=1)
    in_mask = in_mask.reshape(blocks_here, BLOCK, span)

    fetched_emb = lax.all_to_all(send_emb, "col", split_axis=0, concat_axis=0, tiled=True)
    candidate_ids = fetched_emb[my_owners].reshape(blocks_here, span, width)
    scores = jnp.einsum(
        "evg,erg->evr", embedding_tiles, candidate_ids, preferred_element_type=jnp.float32
    ) / math.sqrt(width)
    logits = scores * sharpness.reshape(blocks_here, BLOCK, 1)
    local_max = jnp.max(jnp.where(in_mask, logits, lowest_logit), axis=2)
    local_sum = jnp.sum(jnp.where(in_mask, jnp.exp(logits - local_max[..., None]), 0.0), axis=2)
    stats = lax.all_gather(jnp.stack([local_max, local_sum]), "row")
    top = jnp.max(stats[:, 0], axis=0)
    totals = jnp.sum(stats[:, 1] * jnp.exp(stats[:, 0] - top), axis=0)
    weight_matrix = jnp.where(
        in_mask, jnp.exp(logits - top[..., None]) / totals[..., None], 0.0
    ).astype(jnp.bfloat16)
    all_weights = lax.all_gather(weight_matrix, "row")

    def propagate_using(gathered, seed):
        candidates = gathered.reshape(-1, BLOCK, per_device)[pattern]
        candidates = candidates.reshape(blocks_here, n_row, span, per_device)
        pieces = jnp.einsum(
            "gtmk,tgkc->gtmc", all_weights, candidates, preferred_element_type=jnp.float32
        ).astype(jnp.bfloat16)
        summed = jnp.sum(pieces.astype(jnp.float32), axis=0).reshape(rows_here, per_device)
        return (mixing * summed + (1.0 - mixing) * seed.astype(jnp.float32)).astype(jnp.bfloat16)

    spread = propagate_using(all_labels, my_labels)
    all_spread = lax.all_gather(spread, "col", tiled=True)
    return propagate_using(all_spread, my_labels)


def solution(mesh):
    placed = (P("col", None), P("col", None), P("col"), P("col", None), P("col", None))
    return jax.shard_map(
        body, mesh=mesh, in_specs=placed, out_specs=P("col", "row"), check_vma=False
    )
```

time: 394 us -> 278 us (0.71)
  blocking collectives: 128 us -> 37.6 us
  local copies, waits for them, and re-layouts: 90.6 us -> 24.6 us
  waiting for transfers between devices: 116 us -> 175 us
  starting transfers between devices: 23.3 us -> 5.35 us
    all_to_all x1, blocking collectives: 104 us -> 15.3 us  [body(): lax.all_to_all(wanted, 'col', split_axis=0, concat_axis=0, tiled=True)]
    all_to_all x2 -> x0, waiting for transfers between devices: 63.6 us -> none  [the longest x1 56.8 us: body(): lax.all_to_all(send_lab, 'col', split_axis=0, concat_axis=0, tiled=True)]
    all_gather x0 -> x2, waiting for transfers between devices: none -> 53.7 us  [the longest x1 53.7 us: body(): all_spread = lax.all_gather(spread, 'col', tiled=True)]
    all_gather x1, waiting for transfers between devices: 0.01 us -> 43.6 us  [body(): all_weights = lax.all_gather(weight_matrix, 'row')]
    gather x7 -> x3, local copies, waits for them, and re-layouts: 58.5 us -> 15.8 us  [the longest x2 10.9 us: propagate_using(): candidates = gathered.reshape(-1, BLOCK, per_device)[pattern]]
    all_to_all x1, waiting for transfers between devices: 52.7 us -> 77.9 us  [body(): lax.all_to_all(send_emb, 'col', split_axis=0, concat_axis=0, tiled=True)]
    all_to_all x3 -> x1, local copies, waits for them, and re-layouts: 24.4 us -> 0.09 us  [body(): lax.all_to_all(wanted, 'col', split_axis=0, concat_axis=0, tiled=True)]
    all_to_all x2 -> x0, starting transfers between devices: 18.1 us -> none  [the longest x1 9.54 us: body(): lax.all_to_all(send_lab, 'col', split_axis=0, concat_axis=0, tiled=True)]
  transfers between devices with their start and end apart: 4 -> 4, of which waited for: 3 -> 3; matrix products, arithmetic and copies ran while one was open for 14% -> 10% of each run, Pallas kernels for 0% -> 0%
where the time goes in v5:
time: 278 us; the launch traced here: 277 us
  waiting for transfers between devices  175 us (63%)
  blocking collectives  37.6 us (14%)
  local copies, waits for them, and re-layouts  24.6 us (9%)
  between operations  13.3 us (5%)
  other arithmetic  10.8 us (4%)
  matrix products  10.2 us (4%)
  starting transfers between devices  5.35 us (2%)
    all_to_all x1, waiting for transfers between devices, body(): lax.all_to_all(send_emb, 'col', split_axis=0, concat_axis=0, tiled=True)  77.9 us
    all_gather x1, waiting for transfers between devices, body(): all_spread = lax.all_gather(spread, 'col', tiled=True)  53.7 us
    all_gather x1, waiting for transfers between devices, body(): all_weights = lax.all_gather(weight_matrix, 'row')  43.6 us
    all_gather x1, blocking collectives, body(): stats = lax.all_gather(jnp.stack([local_max, local_sum]), 'row')  22.3 us
    all_to_all x1, blocking collectives, body(): lax.all_to_all(wanted, 'col', split_axis=0, concat_axis=0, tiled=True)  15.3 us
    gather x2, local copies, waits for them, and re-layouts, propagate_using(): candidates = gathered.reshape(-1, BLOCK, per_device)[pattern]  10.9 us
    dot_general x2, matrix products, propagate_using(): jnp.einsum('gtmk,tgkc->gtmc', all_weights, candidates, preferred_element_...  7.72 us
    reduce_or x1, other arithmetic, body(): in_mask = jnp.any(shifted[:, :, None] == positions[None, None, :], axis=1)  7.22 us
  transfers between devices with their start and end apart: 4, of which 3 were waited for; matrix products, arithmetic and copies ran while one was open for 10% of the time, Pallas kernels for 0%

profile of v5, /device:TPU:1, one launch (start us, length us, event | category | flops | bytes accessed | tf_op | source)
XLA Modules:
  0.0 277.1 jit_solution(4000014015893314720)
XLA Ops:
  6.5 0.0 copy-start
  6.5 0.0 all-gather.6.cloned.1.call-start
  6.5 1.4 copy-done
  7.9 0.1 constant_dynamic-slice_fusion
  8.0 0.8 copy.51
  8.8 0.0 all-gather.6.cloned.1.call-update
  8.8 0.7 compare_select_fusion.1
  9.5 0.1 compare_select_fusion.2
  9.6 0.1 fusion.21
  9.7 0.1 copy.41
  9.8 15.3 %all_to_all.17 = s32[32,1,1]{2,1,0:T(1,128)S(1)} all-to-all(s32[32,1,1]{2,1,0:T(1,128)S(1)} %copy.41), channel_id=1, replica_groups=mesh['row'=8,'col'=32] {'col'}, dimensions={0} | all-to-all | bytes 256 | tf_op jit(solution)/shard_map/all_to_all | solution.py:32
  25.1 0.7 reduce.1
  25.8 4.9 %gather_fusion = bf16[32,128,768]{2,1,0:T(8,128)(2,1)} fusion(bf16[6,128,768]{2,1,0:T(8,128)(2,1)} %bitcast.47, s32[1024]{0:T(1024)S(1)} %pad_clamp_fusion.2), kind=kCustom, calls=%fused_computation | custom fusion | bytes 12583040 | tf_op jit(solution)/shard_map/gather | solution.py:34
  30.7 0.0 copy-start.3
  30.7 0.0 copy-start.4
  30.7 5.3 %all-to-all-start.1 = ((bf16[32,128,768]{2,1,0:T(8,128)(2,1)}), bf16[32,128,768]{2,1,0:T(8,128)(2,1)}, u32[]{:S(2)}, u32[]{:S(2)}) async-start(bf16[32,128,768]{2,1,0:T(8,128)(2,1)} %gather_fusion), calls=%async_computation.1 | async-start | bytes 12582912 | tf_op jit(solution)/shard_map/all_to_all | solution.py:43
  36.0 0.0 copy-start.1
  36.0 0.0 all-gather.10.cloned.1.call-start
  36.0 0.1 reshape.85
  36.1 0.0 copy-done.3
  36.2 7.2 %fusion = pred[768,256]{1,0:T(8,128)(4,1)S(1)} fusion(s32[768,50]{0,1:T(8,128)S(1)} %and_select_fusion), kind=kLoop, calls=%fused_computation.5 | loop fusion | flops 19464192 | bytes 350208 | tf_op jit(solution)/shard_map/reduce_or | solution.py:40
  43.4 0.3 copy.45
  43.7 0.0 copy-done.4
  43.7 77.9 %all-to-all-done.1 = bf16[32,128,768]{2,1,0:T(8,128)(2,1)} async-done(((bf16[32,128,768]{2,1,0:T(8,128)(2,1)}), bf16[32,128,768]{2,1,0:T(8,128)(2,1)}, u32[]{:S(2)}, u32[]{:S(2)}) %all-to-all-start.1) | async-done | bytes 6291488 | tf_op jit(solution)/shard_map/all_to_all | solution.py:43
  121.6 5.0 %gather_fusion.1 = bf16[12,128,768]{2,1,0:T(8,128)(2,1)} fusion(bf16[32,128,768]{2,1,0:T(8,128)(2,1)} %all-to-all-done.1, s32[1024]{0:T(1024)S(1)} %pad_clamp_fusion.1), kind=kCustom, calls=%fused_computation.1 | custom fusion | bytes 4718640 | tf_op jit(solution)/shard_map/gather | solution.py:44
  126.6 0.0 copy-done.1
  126.6 2.5 select_reduce_fusion.1
  129.1 0.2 select_reduce_fusion
  129.3 22.3 %all-gather = f32[16,6,128]{2,1,0:T(8,128)S(1)} all-gather(f32[2,6,128]{2,1,0:T(8,128)S(1)} %pad_maximum_fusion), channel_id=2, replica_groups=mesh['row'=8,'col'=32] {'row'}, dimensions={0}, use_global_device_ids=true | all-gather | bytes 55296 | tf_op jit(solution)/shard_map/all_gather | solution.py:51
  151.6 0.2 select_convert_fusion
  151.9 1.0 copy.46
  152.8 0.0 all-gather.10.cloned.1.call-update
  152.8 0.0 all-gather.8.cloned.1.call-start
  152.9 0.1 reshape.93
  153.0 0.0 all-gather.6.cloned.1.call-done
  153.0 5.5 %gather_fusion.2 = bf16[96,128,125]{2,1,0:T(8,128)(2,1)} fusion(bf16[192,128,125]{2,1,0:T(8,128)(2,1)} %bitcast.52, s32[1024]{0:T(1024)S(1)} %pad_clamp_fusion), kind=kCustom, calls=%fused_computation.2 | custom fusion | bytes 6144384 | tf_op jit(solution)/shard_map/gather | solution.py:60
  158.5 43.6 %all-gather.10.cloned.1.call-done = bf16[48,128,256]{2,1,0:T(8,128)(2,1)} async-done(((bf16[6,128,256]{2,1,0:T(8,128)(2,1)}), bf16[48,128,256]{2,1,0:T(8,128)(2,1)}) %all-gather.10.cloned.1.call-update) | async-done | bytes 3145744 | tf_op jit(solution)/shard_map/all_gather | solution.py:57
  202.0 0.0 copy-start.2
  202.1 3.9 %convert_reduce_fusion.1 = f32[6,128,125]{2,1,0:T(8,128)S(1)} fusion(bf16[8,6,128,256]{3,2,1,0:T(8,128)(2,1)} %bitcast.60, bf16[6,8,256,125]{3,2,1,0:T(8,128)(2,1)} %bitcast.49), kind=kOutput, calls=%fused_computation.11 | convolution fusion | flops 395424000 | bytes 6601728 | tf_op jit(solution)/shard_map/gtmk,tgkc->gtmc/dot_general | solution.py:62
  206.0 0.0 copy-done.2
  206.0 0.7 fusion.17
  206.7 0.0 all-gather.8.cloned.1.call-update
  206.7 53.7 %all-gather.8.cloned.1.call-done = bf16[24576,125]{1,0:T(8,128)(2,1)} async-done(((bf16[768,125]{1,0:T(8,128)(2,1)}), bf16[24576,125]{1,0:T(8,128)(2,1)}) %all-gather.8.cloned.1.call-update) | async-done | bytes 6144016 | tf_op jit(solution)/shard_map/all_gather | solution.py:69
  260.5 5.5 %gather_fusion.3 = bf16[96,128,125]{2,1,0:T(8,128)(2,1)} fusion(bf16[192,128,125]{2,1,0:T(8,128)(2,1)} %bitcast.53, s32[1024]{0:T(1024)S(1)} %pad_clamp_fusion), kind=kCustom, calls=%fused_computation.3 | custom fusion | bytes 6144384 | tf_op jit(solution)/shard_map/gather | solution.py:60
  265.9 3.8 %convert_reduce_fusion = f32[6,128,125]{2,1,0:T(8,128)S(1)} fusion(bf16[8,6,128,256]{3,2,1,0:T(8,128)(2,1)} %bitcast.61, bf16[6,8,256,125]{3,2,1,0:T(8,128)(2,1)} %bitcast.50), kind=kOutput, calls=%fused_computation.10 | convolution fusion | flops 395424000 | bytes 6601728 | tf_op jit(solution)/shard_map/gtmk,tgkc->gtmc/dot_general | solution.py:62
  269.8 0.7 fusion.16
  (11 shorter events, 0.2 us)
Async XLA Ops:
  6.5 1.4 copy-start
  6.5 146.5 %all-gather.6.cloned.1.call-start = ((), (), s32[]{:S(2)}) async-start(), calls=%async_computation.2 | async-start | bytes 6488064 | tf_op jit(solution)/shard_map/all_gather | solution.py:36
  30.7 5.4 %copy-start.3 = (s32[768,50]{0,1:T(8,128)S(1)}, s32[768,50]{0,1:T(8,128)}, u32[]{:S(2)}) copy-start(s32[768,50]{0,1:T(8,128)} %param.9) | copy-start | bytes 460804
  30.7 13.0 %copy-start.4 = (f32[768]{0:T(1024)S(1)}, f32[768]{0:T(1024)}, u32[]{:S(2)}) copy-start(f32[768]{0:T(1024)} %param.7) | copy-start | bytes 9220
  30.7 90.9 %all-to-all-start.1 = ((bf16[32,128,768]{2,1,0:T(8,128)(2,1)}), bf16[32,128,768]{2,1,0:T(8,128)(2,1)}, u32[]{:S(2)}, u32[]{:S(2)}) async-start(bf16[32,128,768]{2,1,0:T(8,128)(2,1)} %gather_fusion), calls=%async_computation.1 | async-start | bytes 12582912 | tf_op jit(solution)/shard_map/all_to_all | solution.py:43
  36.0 90.6 %copy-start.1 = (bf16[768,768]{1,0:T(8,128)(2,1)S(1)}, bf16[768,768]{1,0:T(8,128)(2,1)}, u32[]{:S(2)}) copy-start(bf16[768,768]{1,0:T(8,128)(2,1)} %param.5) | copy-start | bytes 3538948
  36.0 166.1 %all-gather.10.cloned.1.call-start = ((), (), s32[]{:S(2)}) async-start(), calls=%async_computation.4 | async-start | bytes 3538944 | tf_op jit(solution)/shard_map/all_gather | solution.py:57
  152.8 107.6 %all-gather.8.cloned.1.call-start = ((), (), s32[]{:S(2)}) async-start(), calls=%async_computation.3 | async-start | bytes 6488064 | tf_op jit(solution)/shard_map/all_gather | solution.py:69
  202.0 3.9 %copy-start.2 = (bf16[768,125]{1,0:T(8,128)(2,1)S(1)}, bf16[768,125]{1,0:T(8,128)(2,1)}, u32[]{:S(2)}) copy-start(bf16[768,125]{1,0:T(8,128)(2,1)} %copy.51) | copy-start | bytes 576004
Sparse Core Ops, SparseCore 0:
  9.9 110.2 all-gather.5
  153.0 49.0 all-gather.9
  206.9 53.5 all-gather.7

commit v6 on v5

v6 whole, which is shorter than its diff:
```python
import math

import jax
import jax.numpy as jnp
from jax import lax
from jax.sharding import PartitionSpec as P

BLOCK = 128
SLOTS = 16


mixing = 0.75
lowest_logit = -1e30


COL = ("chip", "core")


def gather_columns(x):
    rows_here, width = x.shape
    same_core = lax.all_gather(x, "chip", tiled=True).reshape(-1, BLOCK, width)
    other_core = lax.ppermute(same_core, "core", [(0, 1), (1, 0)])
    return same_core, other_core


def body(embeds, labels, sharpness, pattern, mask_pos):
    rows_here, width = embeds.shape
    classes = labels.shape[1]
    n_col = lax.axis_size(COL)
    n_row = lax.axis_size("row")
    row_pos = lax.axis_index("row")
    blocks_here = rows_here // BLOCK
    slots_here = SLOTS // n_row
    span = slots_here * BLOCK
    per_device = classes // n_row
    owners = pattern // blocks_here
    local_ids = pattern % blocks_here
    my_owners = lax.dynamic_slice_in_dim(owners, row_pos * slots_here, slots_here, 1)
    my_ids = lax.dynamic_slice_in_dim(local_ids, row_pos * slots_here, slots_here, 1)
    peers = jnp.arange(n_col, dtype=jnp.int32)
    wanted = jnp.max(jnp.where(my_owners[..., None] == peers, my_ids[..., None], 0), axis=(0, 1))
    requested = lax.all_to_all(wanted, COL, split_axis=0, concat_axis=0, tiled=True)
    embedding_tiles = embeds.reshape(blocks_here, BLOCK, width)
    send_emb = embedding_tiles[requested]
    my_labels = lax.dynamic_slice_in_dim(labels, row_pos * per_device, per_device, 1)
    lanes = -(-per_device // 128) * 128
    my_labels = jnp.pad(my_labels, ((0, 0), (0, lanes - per_device)))
    all_labels = gather_columns(my_labels)
    shifted = mask_pos - row_pos * span
    shifted = jnp.where((shifted >= 0) & (shifted < span), shifted, span)
    positions = jnp.arange(span, dtype=jnp.int32)
    in_mask = jnp.any(shifted[:, :, None] == positions[None, None, :], axis=1)
    in_mask = in_mask.reshape(blocks_here, BLOCK, span)

    fetched_emb = lax.all_to_all(send_emb, COL, split_axis=0, concat_axis=0, tiled=True)
    candidate_ids = fetched_emb[my_owners].reshape(blocks_here, span, width)
    scores = jnp.einsum(
        "evg,erg->evr", embedding_tiles, candidate_ids, preferred_element_type=jnp.float32
    ) / math.sqrt(width)
    logits = scores * sharpness.reshape(blocks_here, BLOCK, 1)
    local_max = jnp.max(jnp.where(in_mask, logits, lowest_logit), axis=2)
    local_sum = jnp.sum(jnp.where(in_mask, jnp.exp(logits - local_max[..., None]), 0.0), axis=2)
    stats = lax.all_gather(jnp.stack([local_max, local_sum]), "row")
    top = jnp.max(stats[:, 0], axis=0)
    totals = jnp.sum(stats[:, 1] * jnp.exp(stats[:, 0] - top), axis=0)
    weight_matrix = jnp.where(
        in_mask, jnp.exp(logits - top[..., None]) / totals[..., None], 0.0
    ).astype(jnp.bfloat16)
    all_weights = lax.all_gather(weight_matrix, "row")

    shard_of = pattern // blocks_here
    on_this_core = (shard_of % 2 == lax.axis_index("core"))[..., None, None]
    pair_ids = (shard_of // 2) * blocks_here + pattern % blocks_here

    def propagate_using(gathered, seed):
        same_core, other_core = gathered
        candidates = jnp.where(on_this_core, same_core[pair_ids], other_core[pair_ids])
        candidates = candidates.reshape(blocks_here, n_row, span, lanes)
        pieces = jnp.einsum(
            "gtmk,tgkc->gtmc", all_weights, candidates, preferred_element_type=jnp.float32
        ).astype(jnp.bfloat16)
        summed = jnp.sum(pieces.astype(jnp.float32), axis=0).reshape(rows_here, lanes)
        return (mixing * summed + (1.0 - mixing) * seed.astype(jnp.float32)).astype(jnp.bfloat16)

    spread = propagate_using(all_labels, my_labels)
    all_spread = gather_columns(spread)
    return propagate_using(all_spread, my_labels)[:, :per_device]


def solution(mesh):
    devices = mesh.devices
    fine = jax.sharding.Mesh(
        devices.reshape(devices.shape[0], devices.shape[1] // 2, 2), ("row", "chip", "core")
    )
    placed = (P(COL, None), P(COL, None), P(COL), P(COL, None), P(COL, None))
    return jax.shard_map(
        body, mesh=fine, in_specs=placed, out_specs=P(COL, "row"), check_vma=False
    )
```

time: 278 us -> 275 us (0.989)
  waiting for transfers between devices: 175 us -> 149 us
  starting transfers between devices: 5.35 us -> 17.8 us
  local copies, waits for them, and re-layouts: 24.6 us -> 31.1 us
  matrix products: 10.2 us -> 13.5 us
    all_gather x1, waiting for transfers between devices: 43.6 us -> 27.3 us  [body(): all_weights = lax.all_gather(weight_matrix, 'row')]
    ppermute x0 -> x2, starting transfers between devices: none -> 12.4 us  [gather_columns(): other_core = lax.ppermute(same_core, 'core', [(0, 1), (1, 0)])]
    all_to_all x1, waiting for transfers between devices: 77.9 us -> 68.2 us  [body(): lax.all_to_all(send_emb, COL, split_axis=0, concat_axis=0, tiled=True)]
    gather x2 -> x4, local copies, waits for them, and re-layouts: 10.9 us -> 18.4 us  [the longest x2 9.28 us: propagate_using(): same_core[pair_ids]]
    dot_general x2, matrix products: 7.72 us -> 11 us  [propagate_using(): jnp.einsum('gtmk,tgkc->gtmc', all_weights, candidates, preferred_element_...]
  transfers between devices with their start and end apart: 4 -> 6, of which waited for: 3 -> 5; matrix products, arithmetic and copies ran while one was open for 10% -> 12% of each run, Pallas kernels for 0% -> 0%
where the time goes in v6:
time: 275 us
  waiting for transfers between devices  149 us (54%)
  blocking collectives  38.6 us (14%)
  local copies, waits for them, and re-layouts  31.1 us (11%)
  starting transfers between devices  17.8 us (6%)
  matrix products  13.5 us (5%)
  between operations  13.3 us (5%)
  other arithmetic  11.6 us (4%)
    all_to_all x1, waiting for transfers between devices, body(): lax.all_to_all(send_emb, COL, split_axis=0, concat_axis=0, tiled=True)  68.2 us
    all_gather x2, waiting for transfers between devices, gather_columns(): same_core = lax.all_gather(x, 'chip', tiled=True).reshape(-1, BLOCK, width)  51.5 us
    all_gather x1, waiting for transfers between devices, body(): all_weights = lax.all_gather(weight_matrix, 'row')  27.3 us
    all_gather x1, blocking collectives, body(): stats = lax.all_gather(jnp.stack([local_max, local_sum]), 'row')  23.3 us
    all_to_all x1, blocking collectives, body(): lax.all_to_all(wanted, COL, split_axis=0, concat_axis=0, tiled=True)  15.3 us
    ppermute x2, starting transfers between devices, gather_columns(): other_core = lax.ppermute(same_core, 'core', [(0, 1), (1, 0)])  12.4 us
    dot_general x2, matrix products, propagate_using(): jnp.einsum('gtmk,tgkc->gtmc', all_weights, candidates, preferred_element_...  11 us
    gather x2, local copies, waits for them, and re-layouts, propagate_using(): same_core[pair_ids]  9.28 us
  transfers between devices with their start and end apart: 6, of which 5 were waited for; matrix products, arithmetic and copies ran while one was open for 12% of the time, Pallas kernels for 0%

profile of v6, /device:TPU:1, one launch (start us, length us, event | category | flops | bytes accessed | tf_op | source)
XLA Modules:
  0.0 274.8 jit_solution(12383164933250305799)
XLA Ops:
  6.5 0.0 copy-start
  6.5 0.8 fusion.22
  7.4 0.7 compare_select_fusion.1
  8.1 0.1 compare_select_fusion.2
  8.1 0.1 fusion.21
  8.2 0.1 copy.41
  8.3 15.3 %all_to_all.17 = s32[32,1,1]{2,1,0:T(1,128)S(1)} all-to-all(s32[32,1,1]{2,1,0:T(1,128)S(1)} %copy.41), channel_id=1, replica_groups=mesh['row'=8,'chip'=16,'core'=2] {'chip','core'}, dimensions={0} | all-to-all | bytes 256 | tf_op jit(solution)/shard_map/all_to_all | solution.py:42
  23.7 0.7 reduce.1
  24.4 4.9 %gather_fusion = bf16[32,128,768]{2,1,0:T(8,128)(2,1)} fusion(bf16[6,128,768]{2,1,0:T(8,128)(2,1)} %bitcast.46, s32[1024]{0:T(1024)S(1)} %pad_clamp_fusion.2), kind=kCustom, calls=%fused_computation | custom fusion | bytes 12583040 | tf_op jit(solution)/shard_map/gather | solution.py:44
  29.2 0.0 copy-start.2
  29.2 0.0 copy-start.3
  29.2 5.3 %all-to-all-start.1 = ((bf16[32,128,768]{2,1,0:T(8,128)(2,1)}), bf16[32,128,768]{2,1,0:T(8,128)(2,1)}, u32[]{:S(2)}, u32[]{:S(2)}) async-start(bf16[32,128,768]{2,1,0:T(8,128)(2,1)} %gather_fusion), calls=%async_computation.1 | async-start | bytes 12582912 | tf_op jit(solution)/shard_map/all_to_all | solution.py:55
  34.5 0.0 all-gather.6.cloned.1.call-start
  34.6 0.0 copy-done
  34.6 0.1 constant_dynamic-slice_fusion
  34.6 0.2 copy.51
  34.8 0.0 copy-start.1
  34.8 0.7 pad.4
  35.5 0.0 all-gather.6.cloned.1.call-update
  35.6 0.0 all-gather.10.cloned.1.call-start
  35.6 0.1 reshape.86
  35.7 0.0 copy-done.2
  35.7 7.2 %fusion = pred[768,256]{1,0:T(8,128)(4,1)S(1)} fusion(s32[768,50]{0,1:T(8,128)S(1)} %and_select_fusion), kind=kLoop, calls=%fused_computation.7 | loop fusion | flops 19464192 | bytes 350208 | tf_op jit(solution)/shard_map/reduce_or | solution.py:52
  43.0 0.3 copy.45
  43.3 0.0 copy-done.3
  43.3 68.2 %all-to-all-done.1 = bf16[32,128,768]{2,1,0:T(8,128)(2,1)} async-done(((bf16[32,128,768]{2,1,0:T(8,128)(2,1)}), bf16[32,128,768]{2,1,0:T(8,128)(2,1)}, u32[]{:S(2)}, u32[]{:S(2)}) %all-to-all-start.1) | async-done | bytes 6291488 | tf_op jit(solution)/shard_map/all_to_all | solution.py:55
  111.5 5.2 %gather_fusion.1 = bf16[12,128,768]{2,1,0:T(8,128)(2,1)} fusion(bf16[32,128,768]{2,1,0:T(8,128)(2,1)} %all-to-all-done.1, s32[1024]{0:T(1024)S(1)} %pad_clamp_fusion.1), kind=kCustom, calls=%fused_computation.1 | custom fusion | bytes 4718640 | tf_op jit(solution)/shard_map/gather | solution.py:56
  116.8 0.0 copy-done.1
  116.8 2.5 select_reduce_fusion.1
  119.3 0.2 select_reduce_fusion
  119.5 23.3 %all-gather = f32[16,6,128]{2,1,0:T(8,128)S(1)} all-gather(f32[2,6,128]{2,1,0:T(8,128)S(1)} %pad_maximum_fusion), channel_id=2, replica_groups=mesh['row'=8,'chip'=16,'core'=2] {'row'}, dimensions={0}, use_global_device_ids=true | all-gather | bytes 55296 | tf_op jit(solution)/shard_map/all_gather | solution.py:63
  142.8 0.2 select_convert_fusion
  143.0 1.0 copy.46
  143.9 0.0 all-gather.10.cloned.1.call-update
  144.0 0.0 all-gather.8.cloned.1.call-start
  144.0 0.0 all-gather.6.cloned.1.call-done
  144.0 11.1 %collective-permute-start = (bf16[96,128,128]{2,1,0:T(8,128)(2,1)}, bf16[96,128,128]{2,1,0:T(8,128)(2,1)}, u32[]{:S(2)}, u32[]{:S(2)}) collective-permute-start(bf16[96,128,128]{2,1,0:T(8,128)(2,1)} %bitcast.48), channel_id=1, source_target_pairs={{0,1},{1,0},{2,3},{3,2},{4,5},{5,4},{6,7},{7,6},{8,9},{9,8},{10,11... | collective-permute-start | bytes 9437192 | tf_op jit(solution)/shard_map/ppermute | solution.py:22
  155.1 0.1 reshape.94
  155.2 0.1 broadcast_in_dim.62
  155.3 4.6 %gather_fusion.2 = bf16[96,128,128]{2,1,0:T(8,128)(2,1)} fusion(bf16[96,128,128]{2,1,0:T(8,128)(2,1)} %bitcast.49, s32[1024]{0:T(1024)S(1)} %pad_clamp_fusion), kind=kCustom, calls=%fused_computation.2 | custom fusion | bytes 6291840 | tf_op jit(solution)/shard_map/gather | solution.py:77
  160.0 0.8 collective-permute-done
  160.8 4.6 %gather_fusion.3 = bf16[96,128,128]{2,1,0:T(8,128)(2,1)} fusion(bf16[96,128,128]{2,1,0:T(8,128)(2,1)} %collective-permute-done, s32[1024]{0:T(1024)S(1)} %pad_clamp_fusion), kind=kCustom, calls=%fused_computation.3 | custom fusion | bytes 6291840 | tf_op jit(solution)/shard_map/gather | solution.py:77
  165.3 27.3 %all-gather.10.cloned.1.call-done = bf16[48,128,256]{2,1,0:T(8,128)(2,1)} async-done(((bf16[6,128,256]{2,1,0:T(8,128)(2,1)}), bf16[48,128,256]{2,1,0:T(8,128)(2,1)}) %all-gather.10.cloned.1.call-update) | async-done | bytes 3145744 | tf_op jit(solution)/shard_map/all_gather | solution.py:69
  192.6 5.5 %convert_reduce_fusion.1 = f32[6,128,128]{2,1,0:T(8,128)S(1)} fusion(bf16[8,6,128,256]{3,2,1,0:T(8,128)(2,1)} %bitcast.64, bf16[6,8,256,128]{3,2,1,0:T(8,128)(2,1)} %bitcast.52, bf16[6,8,256,128]{3,2,1,0:T(8,128)(2,1)} %bitcast.54, pred[6,8,256]{2,1,0:T(8,128)(4,1)S(1)} %broadcast_in_dim.63), kind=kOutput, calls=%fused_computation.13 | convolution fusion | flops 406487040 | bytes 9842688 | tf_op jit(solution)/shard_map/gtmk,tgkc->gtmc/dot_general | solution.py:79
  198.2 0.8 fusion.17
  198.9 0.0 all-gather.8.cloned.1.call-update
  199.0 51.5 %all-gather.8.cloned.1.call-done = bf16[12288,128]{1,0:T(8,128)(2,1)} async-done(((bf16[768,128]{1,0:T(8,128)(2,1)}), bf16[12288,128]{1,0:T(8,128)(2,1)}) %all-gather.8.cloned.1.call-update) | async-done | bytes 3145744 | tf_op jit(solution)/shard_map/all_gather | solution.py:21
  250.5 1.3 collective-permute-start.1
  251.8 4.6 %gather_fusion.4 = bf16[96,128,128]{2,1,0:T(8,128)(2,1)} fusion(bf16[96,128,128]{2,1,0:T(8,128)(2,1)} %bitcast.51, s32[1024]{0:T(1024)S(1)} %pad_clamp_fusion), kind=kCustom, calls=%fused_computation.4 | custom fusion | bytes 6291840 | tf_op jit(solution)/shard_map/gather | solution.py:77
  256.4 1.0 collective-permute-done.1
  257.4 4.6 %gather_fusion.5 = bf16[96,128,128]{2,1,0:T(8,128)(2,1)} fusion(bf16[96,128,128]{2,1,0:T(8,128)(2,1)} %collective-permute-done.1, s32[1024]{0:T(1024)S(1)} %pad_clamp_fusion), kind=kCustom, calls=%fused_computation.5 | custom fusion | bytes 6291840 | tf_op jit(solution)/shard_map/gather | solution.py:77
  262.0 5.5 %convert_reduce_fusion = f32[6,128,128]{2,1,0:T(8,128)S(1)} fusion(bf16[8,6,128,256]{3,2,1,0:T(8,128)(2,1)} %bitcast.65, bf16[6,8,256,128]{3,2,1,0:T(8,128)(2,1)} %bitcast.53, bf16[6,8,256,128]{3,2,1,0:T(8,128)(2,1)} %bitcast.55, pred[6,8,256]{2,1,0:T(8,128)(4,1)S(1)} %broadcast_in_dim.63), kind=kOutput, calls=%fused_computation.12 | convolution fusion | flops 406487040 | bytes 9842688 | tf_op jit(solution)/shard_map/gtmk,tgkc->gtmc/dot_general | solution.py:79
  267.5 0.7 fusion.16
  (12 shorter events, 0.2 us)
Async XLA Ops:
  6.5 28.0 %copy-start = (bf16[768,1000]{0,1:T(8,128)(2,1)S(1)}, bf16[768,1000]{0,1:T(8,128)(2,1)}, u32[]{:S(2)}) copy-start(bf16[768,1000]{0,1:T(8,128)(2,1)} %param.6) | copy-start | bytes 4608004
  29.2 6.5 %copy-start.2 = (s32[768,50]{0,1:T(8,128)S(1)}, s32[768,50]{0,1:T(8,128)}, u32[]{:S(2)}) copy-start(s32[768,50]{0,1:T(8,128)} %param.9) | copy-start | bytes 460804
  29.2 14.0 %copy-start.3 = (f32[768]{0:T(1024)S(1)}, f32[768]{0:T(1024)}, u32[]{:S(2)}) copy-start(f32[768]{0:T(1024)} %param.7) | copy-start | bytes 9220
  29.2 82.3 %all-to-all-start.1 = ((bf16[32,128,768]{2,1,0:T(8,128)(2,1)}), bf16[32,128,768]{2,1,0:T(8,128)(2,1)}, u32[]{:S(2)}, u32[]{:S(2)}) async-start(bf16[32,128,768]{2,1,0:T(8,128)(2,1)} %gather_fusion), calls=%async_computation.1 | async-start | bytes 12582912 | tf_op jit(solution)/shard_map/all_to_all | solution.py:55
  34.5 109.5 %all-gather.6.cloned.1.call-start = ((), (), s32[]{:S(2)}) async-start(), calls=%async_computation.2 | async-start | bytes 3342336 | tf_op jit(solution)/shard_map/all_gather | solution.py:21
  34.8 82.0 %copy-start.1 = (bf16[768,768]{1,0:T(8,128)(2,1)S(1)}, bf16[768,768]{1,0:T(8,128)(2,1)}, u32[]{:S(2)}) copy-start(bf16[768,768]{1,0:T(8,128)(2,1)} %param.5) | copy-start | bytes 3538948
  35.6 157.1 %all-gather.10.cloned.1.call-start = ((), (), s32[]{:S(2)}) async-start(), calls=%async_computation.4 | async-start | bytes 3538944 | tf_op jit(solution)/shard_map/all_gather | solution.py:69
  144.0 106.5 %all-gather.8.cloned.1.call-start = ((), (), s32[]{:S(2)}) async-start(), calls=%async_computation.3 | async-start | bytes 3342336 | tf_op jit(solution)/shard_map/all_gather | solution.py:21
  144.0 16.7 %collective-permute-start = (bf16[96,128,128]{2,1,0:T(8,128)(2,1)}, bf16[96,128,128]{2,1,0:T(8,128)(2,1)}, u32[]{:S(2)}, u32[]{:S(2)}) collective-permute-start(bf16[96,128,128]{2,1,0:T(8,128)(2,1)} %bitcast.48), channel_id=1, source_target_pairs={{0,1},{1,0},{2,3},{3,2},{4,5},{5,4},{6,7},{7,6},{8,9},{9,8},{10,11... | collective-permute-start | bytes 9437192 | tf_op jit(solution)/shard_map/ppermute | solution.py:22
  250.5 6.9 %collective-permute-start.1 = (bf16[96,128,128]{2,1,0:T(8,128)(2,1)}, bf16[96,128,128]{2,1,0:T(8,128)(2,1)}, u32[]{:S(2)}, u32[]{:S(2)}) collective-permute-start(bf16[96,128,128]{2,1,0:T(8,128)(2,1)} %bitcast.50), channel_id=1, source_target_pairs={{0,1},{1,0},{2,3},{3,2},{4,5},{5,4},{6,7},{7,6},{8,9},{9,8},{10,11... | collective-permute-start | bytes 9437192 | tf_op jit(solution)/shard_map/ppermute | solution.py:22
Sparse Core Ops, SparseCore 0:
  37.7 91.3 all-gather.5
  144.1 48.5 all-gather.9
  199.1 51.3 all-gather.7

commit v7 on v6

--- a/solution.py
+++ b/solution.py
@@ -60,13 +60,14 @@
     logits = scores * sharpness.reshape(blocks_here, BLOCK, 1)
     local_max = jnp.max(jnp.where(in_mask, logits, lowest_logit), axis=2)
     local_sum = jnp.sum(jnp.where(in_mask, jnp.exp(logits - local_max[..., None]), 0.0), axis=2)
+    local_weights = jnp.where(
+        in_mask, jnp.exp(logits - local_max[..., None]), 0.0
+    ).astype(jnp.bfloat16)
     stats = lax.all_gather(jnp.stack([local_max, local_sum]), "row")
+    all_weights = lax.all_gather(local_weights, "row")
     top = jnp.max(stats[:, 0], axis=0)
     totals = jnp.sum(stats[:, 1] * jnp.exp(stats[:, 0] - top), axis=0)
-    weight_matrix = jnp.where(
-        in_mask, jnp.exp(logits - top[..., None]) / totals[..., None], 0.0
-    ).astype(jnp.bfloat16)
-    all_weights = lax.all_gather(weight_matrix, "row")
+    factors = jnp.exp(stats[:, 0] - top) / totals
 
     shard_of = pattern // blocks_here
     on_this_core = (shard_of % 2 == lax.axis_index("core"))[..., None, None]
@@ -78,7 +79,8 @@
         candidates = candidates.reshape(blocks_here, n_row, span, lanes)
         pieces = jnp.einsum(
             "gtmk,tgkc->gtmc", all_weights, candidates, preferred_element_type=jnp.float32
-        ).astype(jnp.bfloat16)
+        )
+        pieces = (pieces * factors[..., None]).astype(jnp.bfloat16)
         summed = jnp.sum(pieces.astype(jnp.float32), axis=0).reshape(rows_here, lanes)
         return (mixing * summed + (1.0 - mixing) * seed.astype(jnp.float32)).astype(jnp.bfloat16)
 

time: 275 us -> 259 us (0.942)
  starting transfers between devices: 17.8 us -> 7.98 us
  waiting for transfers between devices: 149 us -> 142 us
    all_gather x1, waiting for transfers between devices: 27.3 us -> 13.2 us  [body(): all_weights = lax.all_gather(local_weights, 'row')]
    ppermute x2, starting transfers between devices: 12.4 us -> 2.6 us  [gather_columns(): other_core = lax.ppermute(same_core, 'core', [(0, 1), (1, 0)])]
    all_gather x2, waiting for transfers between devices: 51.5 us -> 59.8 us  [gather_columns(): same_core = lax.all_gather(x, 'chip', tiled=True).reshape(-1, BLOCK, width)]
where the time goes in v7:
time: 259 us; the launch traced here: 258 us
  waiting for transfers between devices  142 us (55%)
  blocking collectives  37.7 us (15%)
  local copies, waits for them, and re-layouts  31.1 us (12%)
  matrix products  14.2 us (5%)
  between operations  13.3 us (5%)
  other arithmetic  11.4 us (4%)
  starting transfers between devices  7.98 us (3%)
    all_to_all x1, waiting for transfers between devices, body(): lax.all_to_all(send_emb, COL, split_axis=0, concat_axis=0, tiled=True)  68.2 us
    all_gather x2, waiting for transfers between devices, gather_columns(): same_core = lax.all_gather(x, 'chip', tiled=True).reshape(-1, BLOCK, width)  59.8 us
    all_gather x1, blocking collectives, body(): stats = lax.all_gather(jnp.stack([local_max, local_sum]), 'row')  22.3 us
    all_to_all x1, blocking collectives, body(): lax.all_to_all(wanted, COL, split_axis=0, concat_axis=0, tiled=True)  15.3 us
    all_gather x1, waiting for transfers between devices, body(): all_weights = lax.all_gather(local_weights, 'row')  13.2 us
    dot_general x2, matrix products, propagate_using(): jnp.einsum('gtmk,tgkc->gtmc', all_weights, candidates, preferred_element_...  11.7 us
    gather x2, local copies, waits for them, and re-layouts, propagate_using(): same_core[pair_ids]  9.28 us
    gather x2, local copies, waits for them, and re-layouts, propagate_using(): other_core[pair_ids]  9.16 us
  transfers between devices with their start and end apart: 6, of which 5 were waited for; matrix products, arithmetic and copies ran while one was open for 12% of the time, Pallas kernels for 0%

profile of v7, /device:TPU:1, one launch (start us, length us, event | category | flops | bytes accessed | tf_op | source)
XLA Modules:
  0.0 258.0 jit_solution(13602397430212546452)
XLA Ops:
  6.5 0.0 copy-start
  6.5 0.8 fusion.23
  7.4 0.7 compare_select_fusion.1
  8.1 0.1 compare_select_fusion.2
  8.1 0.1 fusion.22
  8.2 0.1 copy.42
  8.3 15.3 %all_to_all.17 = s32[32,1,1]{2,1,0:T(1,128)S(1)} all-to-all(s32[32,1,1]{2,1,0:T(1,128)S(1)} %copy.42), channel_id=1, replica_groups=mesh['row'=8,'chip'=16,'core'=2] {'chip','core'}, dimensions={0} | all-to-all | bytes 256 | tf_op jit(solution)/shard_map/all_to_all | solution.py:42
  23.7 0.7 reduce.1
  24.4 4.9 %gather_fusion = bf16[32,128,768]{2,1,0:T(8,128)(2,1)} fusion(bf16[6,128,768]{2,1,0:T(8,128)(2,1)} %bitcast.50, s32[1024]{0:T(1024)S(1)} %pad_clamp_fusion.2), kind=kCustom, calls=%fused_computation | custom fusion | bytes 12583040 | tf_op jit(solution)/shard_map/gather | solution.py:44
  29.2 0.0 copy-start.2
  29.2 0.0 copy-start.3
  29.2 5.3 %all-to-all-start.1 = ((bf16[32,128,768]{2,1,0:T(8,128)(2,1)}), bf16[32,128,768]{2,1,0:T(8,128)(2,1)}, u32[]{:S(2)}, u32[]{:S(2)}) async-start(bf16[32,128,768]{2,1,0:T(8,128)(2,1)} %gather_fusion), calls=%async_computation.1 | async-start | bytes 12582912 | tf_op jit(solution)/shard_map/all_to_all | solution.py:55
  34.5 0.0 all-gather.6.cloned.1.call-start
  34.6 0.0 copy-done
  34.6 0.1 constant_dynamic-slice_fusion
  34.6 0.2 copy.51
  34.8 0.0 copy-start.1
  34.8 0.7 pad.4
  35.5 0.0 all-gather.6.cloned.1.call-update
  35.6 0.0 all-gather.10.cloned.1.call-start
  35.6 0.1 reshape.92
  35.7 0.0 copy-done.2
  35.7 7.2 %fusion = pred[768,256]{1,0:T(8,128)(4,1)S(1)} fusion(s32[768,50]{0,1:T(8,128)S(1)} %and_select_fusion), kind=kLoop, calls=%fused_computation.7 | loop fusion | flops 19464192 | bytes 350208 | tf_op jit(solution)/shard_map/reduce_or | solution.py:52
  43.0 0.3 copy.44
  43.3 0.0 copy-done.3
  43.3 68.2 %all-to-all-done.1 = bf16[32,128,768]{2,1,0:T(8,128)(2,1)} async-done(((bf16[32,128,768]{2,1,0:T(8,128)(2,1)}), bf16[32,128,768]{2,1,0:T(8,128)(2,1)}, u32[]{:S(2)}, u32[]{:S(2)}) %all-to-all-start.1) | async-done | bytes 6291488 | tf_op jit(solution)/shard_map/all_to_all | solution.py:55
  111.5 5.2 %gather_fusion.1 = bf16[12,128,768]{2,1,0:T(8,128)(2,1)} fusion(bf16[32,128,768]{2,1,0:T(8,128)(2,1)} %all-to-all-done.1, s32[1024]{0:T(1024)S(1)} %pad_clamp_fusion.1), kind=kCustom, calls=%fused_computation.1 | custom fusion | bytes 4718640 | tf_op jit(solution)/shard_map/gather | solution.py:56
  116.8 0.0 copy-done.1
  116.8 2.5 select_reduce_fusion
  119.3 0.2 fusion.15
  119.5 1.0 copy.45
  120.4 0.0 all-gather.10.cloned.1.call-update
  120.5 0.0 all-gather.8.cloned.1.call-start
  120.5 8.6 %all-gather.6.cloned.1.call-done = bf16[12288,128]{1,0:T(8,128)(2,1)} async-done(((bf16[768,128]{1,0:T(8,128)(2,1)}), bf16[12288,128]{1,0:T(8,128)(2,1)}) %all-gather.6.cloned.1.call-update) | async-done | bytes 3145744 | tf_op jit(solution)/shard_map/all_gather | solution.py:21
  129.1 1.3 collective-permute-start
  130.4 0.1 reshape.100
  130.5 0.1 broadcast_in_dim.65
  130.6 4.6 %gather_fusion.2 = bf16[96,128,128]{2,1,0:T(8,128)(2,1)} fusion(bf16[96,128,128]{2,1,0:T(8,128)(2,1)} %bitcast.53, s32[1024]{0:T(1024)S(1)} %pad_clamp_fusion), kind=kCustom, calls=%fused_computation.2 | custom fusion | bytes 6291840 | tf_op jit(solution)/shard_map/gather | solution.py:78
  135.3 22.3 %all-gather.1 = f32[16,6,128]{2,1,0:T(8,128)S(1)} all-gather(f32[2,6,128]{2,1,0:T(8,128)S(1)} %pad_maximum_fusion), channel_id=3, replica_groups=mesh['row'=8,'chip'=16,'core'=2] {'row'}, dimensions={0}, use_global_device_ids=true | all-gather | bytes 55296 | tf_op jit(solution)/shard_map/all_gather | solution.py:66
  157.6 0.0 collective-permute-done
  157.7 4.6 %gather_fusion.3 = bf16[96,128,128]{2,1,0:T(8,128)(2,1)} fusion(bf16[96,128,128]{2,1,0:T(8,128)(2,1)} %collective-permute-done, s32[1024]{0:T(1024)S(1)} %pad_clamp_fusion), kind=kCustom, calls=%fused_computation.3 | custom fusion | bytes 6291840 | tf_op jit(solution)/shard_map/gather | solution.py:78
  162.3 13.2 %all-gather.10.cloned.1.call-done = bf16[48,128,256]{2,1,0:T(8,128)(2,1)} async-done(((bf16[6,128,256]{2,1,0:T(8,128)(2,1)}), bf16[48,128,256]{2,1,0:T(8,128)(2,1)}) %all-gather.10.cloned.1.call-update) | async-done | bytes 3145744 | tf_op jit(solution)/shard_map/all_gather | solution.py:67
  175.5 5.9 %convert_reduce_fusion.1 = f32[6,128,128]{2,1,0:T(8,128)S(1)} fusion(f32[8,6,128]{2,1,0:T(8,128)S(1)} %fusion.21, bf16[8,6,128,256]{3,2,1,0:T(8,128)(2,1)} %bitcast.69, bf16[6,8,256,128]{3,2,1,0:T(8,128)(2,1)} %bitcast.54, bf16[6,8,256,128]{3,2,1,0:T(8,128)(2,1)} %bitcast.58, pred[6,8,256]{2,1,0:T(8,128)(4,1)S(1)} %broadcast_in_dim.66), kind=kOutput, calls=%fused_computation.14 | convolution fusion | flops 407273472 | bytes 9867264 | tf_op jit(solution)/shard_map/gtmk,tgkc->gtmc/dot_general | solution.py:80
  181.4 0.8 fusion.17
  182.2 0.0 all-gather.8.cloned.1.call-update
  182.2 51.2 %all-gather.8.cloned.1.call-done = bf16[12288,128]{1,0:T(8,128)(2,1)} async-done(((bf16[768,128]{1,0:T(8,128)(2,1)}), bf16[12288,128]{1,0:T(8,128)(2,1)}) %all-gather.8.cloned.1.call-update) | async-done | bytes 3145744 | tf_op jit(solution)/shard_map/all_gather | solution.py:21
  233.3 1.3 collective-permute-start.1
  234.6 4.6 %gather_fusion.4 = bf16[96,128,128]{2,1,0:T(8,128)(2,1)} fusion(bf16[96,128,128]{2,1,0:T(8,128)(2,1)} %bitcast.56, s32[1024]{0:T(1024)S(1)} %pad_clamp_fusion), kind=kCustom, calls=%fused_computation.4 | custom fusion | bytes 6291840 | tf_op jit(solution)/shard_map/gather | solution.py:78
  239.3 1.0 collective-permute-done.1
  240.3 4.6 %gather_fusion.5 = bf16[96,128,128]{2,1,0:T(8,128)(2,1)} fusion(bf16[96,128,128]{2,1,0:T(8,128)(2,1)} %collective-permute-done.1, s32[1024]{0:T(1024)S(1)} %pad_clamp_fusion), kind=kCustom, calls=%fused_computation.5 | custom fusion | bytes 6291840 | tf_op jit(solution)/shard_map/gather | solution.py:78
  244.8 5.9 %convert_reduce_fusion = f32[6,128,128]{2,1,0:T(8,128)S(1)} fusion(f32[8,6,128]{2,1,0:T(8,128)S(1)} %fusion.21, bf16[8,6,128,256]{3,2,1,0:T(8,128)(2,1)} %bitcast.70, bf16[6,8,256,128]{3,2,1,0:T(8,128)(2,1)} %bitcast.57, bf16[6,8,256,128]{3,2,1,0:T(8,128)(2,1)} %bitcast.59, pred[6,8,256]{2,1,0:T(8,128)(4,1)S(1)} %broadcast_in_dim.66), kind=kOutput, calls=%fused_computation.12 | convolution fusion | flops 407273472 | bytes 9867264 | tf_op jit(solution)/shard_map/gtmk,tgkc->gtmc/dot_general | solution.py:80
  250.8 0.7 fusion.16
  (13 shorter events, 0.2 us)
Async XLA Ops:
  6.5 28.0 %copy-start = (bf16[768,1000]{0,1:T(8,128)(2,1)S(1)}, bf16[768,1000]{0,1:T(8,128)(2,1)}, u32[]{:S(2)}) copy-start(bf16[768,1000]{0,1:T(8,128)(2,1)} %param.6) | copy-start | bytes 4608004
  29.2 6.5 %copy-start.2 = (s32[768,50]{0,1:T(8,128)S(1)}, s32[768,50]{0,1:T(8,128)}, u32[]{:S(2)}) copy-start(s32[768,50]{0,1:T(8,128)} %param.9) | copy-start | bytes 460804
  29.2 14.0 %copy-start.3 = (f32[768]{0:T(1024)S(1)}, f32[768]{0:T(1024)}, u32[]{:S(2)}) copy-start(f32[768]{0:T(1024)} %param.7) | copy-start | bytes 9220
  29.2 82.3 %all-to-all-start.1 = ((bf16[32,128,768]{2,1,0:T(8,128)(2,1)}), bf16[32,128,768]{2,1,0:T(8,128)(2,1)}, u32[]{:S(2)}, u32[]{:S(2)}) async-start(bf16[32,128,768]{2,1,0:T(8,128)(2,1)} %gather_fusion), calls=%async_computation.1 | async-start | bytes 12582912 | tf_op jit(solution)/shard_map/all_to_all | solution.py:55
  34.5 94.6 %all-gather.6.cloned.1.call-start = ((), (), s32[]{:S(2)}) async-start(), calls=%async_computation.2 | async-start | bytes 3342336 | tf_op jit(solution)/shard_map/all_gather | solution.py:21
  34.8 82.0 %copy-start.1 = (bf16[768,768]{1,0:T(8,128)(2,1)S(1)}, bf16[768,768]{1,0:T(8,128)(2,1)}, u32[]{:S(2)}) copy-start(bf16[768,768]{1,0:T(8,128)(2,1)} %param.5) | copy-start | bytes 3538948
  35.6 139.9 %all-gather.10.cloned.1.call-start = ((), (), s32[]{:S(2)}) async-start(), calls=%async_computation.4 | async-start | bytes 3538944 | tf_op jit(solution)/shard_map/all_gather | solution.py:67
  120.5 112.9 %all-gather.8.cloned.1.call-start = ((), (), s32[]{:S(2)}) async-start(), calls=%async_computation.3 | async-start | bytes 3342336 | tf_op jit(solution)/shard_map/all_gather | solution.py:21
  129.1 28.5 %collective-permute-start = (bf16[96,128,128]{2,1,0:T(8,128)(2,1)}, bf16[96,128,128]{2,1,0:T(8,128)(2,1)}, u32[]{:S(2)}, u32[]{:S(2)}) collective-permute-start(bf16[96,128,128]{2,1,0:T(8,128)(2,1)} %bitcast.52), channel_id=1, source_target_pairs={{0,1},{1,0},{2,3},{3,2},{4,5},{5,4},{6,7},{7,6},{8,9},{9,8},{10,11... | collective-permute-start | bytes 9437192 | tf_op jit(solution)/shard_map/ppermute | solution.py:22
  233.3 6.9 %collective-permute-start.1 = (bf16[96,128,128]{2,1,0:T(8,128)(2,1)}, bf16[96,128,128]{2,1,0:T(8,128)(2,1)}, u32[]{:S(2)}, u32[]{:S(2)}) collective-permute-start(bf16[96,128,128]{2,1,0:T(8,128)(2,1)} %bitcast.55), channel_id=1, source_target_pairs={{0,1},{1,0},{2,3},{3,2},{4,5},{5,4},{6,7},{7,6},{8,9},{9,8},{10,11... | collective-permute-start | bytes 9437192 | tf_op jit(solution)/shard_map/ppermute | solution.py:22
Sparse Core Ops, SparseCore 0:
  37.7 91.3 all-gather.5
  130.9 44.5 all-gather.9
  182.3 50.9 all-gather.7

commit v8 on v7

--- a/solution.py
+++ b/solution.py
@@ -13,12 +13,26 @@
 lowest_logit = -1e30
 
 
-COL = ("chip", "core")
+COL = ("y", "x", "core")
+
+
+def ring_gather(x, axis):
+    n = lax.axis_size(axis)
+    ahead, behind = [], []
+    cur_f, cur_b = x, x
+    for step in range(1, n // 2 + 1):
+        cur_f = lax.ppermute(cur_f, axis, [(i, (i + 1) % n) for i in range(n)])
+        behind.append(cur_f)
+    for step in range(1, (n - 1) // 2 + 1):
+        cur_b = lax.ppermute(cur_b, axis, [(i, (i - 1) % n) for i in range(n)])
+        ahead.append(cur_b)
+    return jnp.stack([x] + ahead + behind[::-1])
 
 
 def gather_columns(x):
     rows_here, width = x.shape
-    same_core = lax.all_gather(x, "chip", tiled=True).reshape(-1, BLOCK, width)
+    along_x = ring_gather(x.reshape(rows_here // BLOCK, BLOCK, width), "x")
+    same_core = ring_gather(along_x, "y")
     other_core = lax.ppermute(same_core, "core", [(0, 1), (1, 0)])
     return same_core, other_core
 
@@ -63,15 +77,25 @@
     local_weights = jnp.where(
         in_mask, jnp.exp(logits - local_max[..., None]), 0.0
     ).astype(jnp.bfloat16)
-    stats = lax.all_gather(jnp.stack([local_max, local_sum]), "row")
-    all_weights = lax.all_gather(local_weights, "row")
+    stats = ring_gather(jnp.stack([local_max, local_sum]), "row")
+    all_weights = ring_gather(local_weights, "row")
     top = jnp.max(stats[:, 0], axis=0)
     totals = jnp.sum(stats[:, 1] * jnp.exp(stats[:, 0] - top), axis=0)
     factors = jnp.exp(stats[:, 0] - top) / totals
 
+    ring_groups = (row_pos + jnp.arange(n_row, dtype=jnp.int32)) % n_row
+    slot_order = (ring_groups[:, None] * slots_here + jnp.arange(slots_here, dtype=jnp.int32)).reshape(-1)
+    pattern = pattern[:, slot_order]
+    n_core = lax.axis_size("core")
+    n_x = lax.axis_size("x")
+    n_y = lax.axis_size("y")
     shard_of = pattern // blocks_here
-    on_this_core = (shard_of % 2 == lax.axis_index("core"))[..., None, None]
-    pair_ids = (shard_of // 2) * blocks_here + pattern % blocks_here
+    on_this_core = (shard_of % n_core == lax.axis_index("core"))[..., None, None]
+    pair_ids = (
+        (shard_of // (n_core * n_x) - lax.axis_index("y")) % n_y,
+        (shard_of // n_core % n_x - lax.axis_index("x")) % n_x,
+        pattern % blocks_here,
+    )
 
     def propagate_using(gathered, seed):
         same_core, other_core = gathered
@@ -91,8 +115,10 @@
 
 def solution(mesh):
     devices = mesh.devices
+    n_x = len({d.coords[0] for d in devices.reshape(-1)})
     fine = jax.sharding.Mesh(
-        devices.reshape(devices.shape[0], devices.shape[1] // 2, 2), ("row", "chip", "core")
+        devices.reshape(devices.shape[0], devices.shape[1] // (2 * n_x), n_x, 2),
+        ("row", "y", "x", "core"),
     )
     placed = (P(COL, None), P(COL, None), P(COL), P(COL, None), P(COL, None))
     return jax.shard_map(

time: 259 us -> 316 us (1.22)
  starting transfers between devices: 7.98 us -> 52 us
  waiting for transfers between devices: 142 us -> 186 us
  blocking collectives: 37.7 us -> 15.3 us
  between operations: 13.3 us -> 0.4 us
    ppermute x0 -> x26, waiting for transfers between devices: none -> 186 us  [the longest x16 179 us: ring_gather(): cur_f = lax.ppermute(cur_f, axis, [(i, (i + 1) % n) for i in range(n)])]
    all_gather x3 -> x0, waiting for transfers between devices: 73 us -> none  [the longest x2 59.8 us: gather_columns(): same_core = lax.all_gather(x, 'chip', tiled=True).reshape(-1, BLOCK, width)]
    all_to_all x1, waiting for transfers between devices: 68.2 us -> 0.01 us  [body(): lax.all_to_all(send_emb, COL, split_axis=0, concat_axis=0, tiled=True)]
    ppermute x0 -> x26, starting transfers between devices: none -> 31.6 us  [the longest x10 28.3 us: ring_gather(): cur_b = lax.ppermute(cur_b, axis, [(i, (i - 1) % n) for i in range(n)])]
    all_gather x1 -> x0, blocking collectives: 22.3 us -> none  [body(): stats = lax.all_gather(jnp.stack([local_max, local_sum]), 'row')]
    ppermute x2, starting transfers between devices: 2.6 us -> 15.3 us  [gather_columns(): other_core = lax.ppermute(same_core, 'core', [(0, 1), (1, 0)])]
    another operation x1 -> x5, other arithmetic: 0.01 us -> 4 us  [the longest x4 3.99 us: ring_gather(): return jnp.stack([x] + ahead + behind[::-1])]
  transfers between devices with their start and end apart: 6 -> 29, of which waited for: 5 -> 16; matrix products, arithmetic and copies ran while one was open for 12% -> 9% of each run, Pallas kernels for 0% -> 0%
where the time goes in v8:
time: 316 us
  waiting for transfers between devices  186 us (59%)
  starting transfers between devices  52 us (16%)
  local copies, waits for them, and re-layouts  32.9 us (10%)
  blocking collectives  15.3 us (5%)
  matrix products  14.9 us (5%)
  other arithmetic  14.4 us (5%)
    ppermute x16, waiting for transfers between devices, ring_gather(): cur_f = lax.ppermute(cur_f, axis, [(i, (i + 1) % n) for i in range(n)])  179 us
    ppermute x10, starting transfers between devices, ring_gather(): cur_b = lax.ppermute(cur_b, axis, [(i, (i - 1) % n) for i in range(n)])  28.3 us
    all_to_all x1, blocking collectives, body(): lax.all_to_all(wanted, COL, split_axis=0, concat_axis=0, tiled=True)  15.3 us
    ppermute x2, starting transfers between devices, gather_columns(): other_core = lax.ppermute(same_core, 'core', [(0, 1), (1, 0)])  15.3 us
    dot_general x2, matrix products, propagate_using(): jnp.einsum('gtmk,tgkc->gtmc', all_weights, candidates, preferred_element_...  12.5 us
    gather x2, local copies, waits for them, and re-layouts, propagate_using(): same_core[pair_ids]  10.4 us
    gather x2, local copies, waits for them, and re-layouts, propagate_using(): other_core[pair_ids]  10.4 us
    reduce_or x1, other arithmetic, body(): in_mask = jnp.any(shifted[:, :, None] == positions[None, None, :], axis=1)  7.22 us
  transfers between devices with their start and end apart: 29, of which 16 were waited for; matrix products, arithmetic and copies ran while one was open for 9% of the time, Pallas kernels for 0%

profile of v8, /device:TPU:1, one launch (start us, length us, event | category | flops | bytes accessed | tf_op | source)
XLA Modules:
  0.0 315.9 jit_solution(8060595198541497711)
XLA Ops:
  0.0 0.8 add_select_fusion.10
  0.9 0.1 fusion.22
  1.0 0.1 copy.104
  1.1 15.3 %all_to_all.17 = s32[32,1,1]{2,1,0:T(1,128)S(1)} all-to-all(s32[32,1,1]{2,1,0:T(1,128)S(1)} %copy.104), channel_id=1, replica_groups=mesh['row'=8,'y'=4,'x'=4,'core'=2] {'y','x','core'}, dimensions={0} | all-to-all | bytes 256 | tf_op jit(solution)/shard_map/all_to_all | solution.py:56
  16.4 0.7 reduce.1
  17.1 4.8 %gather_fusion = bf16[32,128,768]{2,1,0:T(8,128)(2,1)} fusion(bf16[6,128,768]{2,1,0:T(8,128)(2,1)} %bitcast.139, s32[1024]{0:T(1024)S(1)} %pad_clamp_fusion.2), kind=kCustom, calls=%fused_computation | custom fusion | bytes 12583040 | tf_op jit(solution)/shard_map/gather | solution.py:58
  22.0 5.2 %all-to-all-start.1 = ((bf16[32,128,768]{2,1,0:T(8,128)(2,1)}), bf16[32,128,768]{2,1,0:T(8,128)(2,1)}, u32[]{:S(2)}, u32[]{:S(2)}) async-start(bf16[32,128,768]{2,1,0:T(8,128)(2,1)} %gather_fusion), calls=%async_computation.1 | async-start | bytes 12582912 | tf_op jit(solution)/shard_map/all_to_all | solution.py:69
  27.2 0.2 copy.119
  27.4 1.4 collective-permute-start.8
  28.9 1.3 collective-permute-start.7
  30.2 73.8 %collective-permute-done.8 = bf16[6,128,128]{2,1,0:T(8,128)(2,1)S(1)} collective-permute-done((bf16[6,128,128]{2,1,0:T(8,128)(2,1)S(1)}, bf16[6,128,128]{2,1,0:T(8,128)(2,1)S(1)}, u32[]{:S(2)}, u32[]{:S(2)}) %collective-permute-start.8) | collective-permute-done | bytes 196640 | tf_op jit(solution)/shard_map/ppermute | solution.py:24
  104.0 0.2 collective-permute-start.9
  104.2 1.1 collective-permute-done.7
  105.3 6.4 %collective-permute-done.9 = bf16[6,128,128]{2,1,0:T(8,128)(2,1)S(1)} collective-permute-done((bf16[6,128,128]{2,1,0:T(8,128)(2,1)S(1)}, bf16[6,128,128]{2,1,0:T(8,128)(2,1)S(1)}, u32[]{:S(2)}, u32[]{:S(2)}) %collective-permute-start.9) | collective-permute-done | bytes 196640 | tf_op jit(solution)/shard_map/ppermute | solution.py:24
  111.6 0.1 fusion.50
  111.8 1.2 collective-permute-start.11
  113.0 1.5 collective-permute-start.10
  114.5 16.1 %collective-permute-done.11 = bf16[4,6,128,128]{3,2,1,0:T(8,128)(2,1)S(1)} collective-permute-done((bf16[4,6,128,128]{3,2,1,0:T(8,128)(2,1)S(1)}, bf16[4,6,128,128]{3,2,1,0:T(8,128)(2,1)S(1)}, u32[]{:S(2)}, u32[]{:S(2)}) %collective-permute-start.11) | collective-permute-done | bytes 786464 | tf_op jit(solution)/shard_map/ppermute | solution.py:24
  130.6 17.9 %collective-permute-done.12 = bf16[4,6,128,128]{3,2,1,0:T(8,128)(2,1)S(1)} collective-permute-done((bf16[4,6,128,128]{3,2,1,0:T(8,128)(2,1)S(1)}, bf16[4,6,128,128]{3,2,1,0:T(8,128)(2,1)S(1)}, u32[]{:S(2)}, u32[]{:S(2)}) %collective-permute-start.12) | collective-permute-done | bytes 786464 | tf_op jit(solution)/shard_map/ppermute | solution.py:24
  148.6 1.9 pad_maximum_fusion
  150.4 3.3 %collective-permute-start.13 = (bf16[4,4,6,128,128]{4,3,2,1,0:T(8,128)(2,1)}, bf16[4,4,6,128,128]{4,3,2,1,0:T(8,128)(2,1)}, u32[]{:S(2)}, u32[]{:S(2)}) collective-permute-start(bf16[4,4,6,128,128]{4,3,2,1,0:T(8,128)(2,1)} %pad_maximum_fusion), channel_id=1, source_target_pairs={{0,1},{1,0},{2,3},{3,2},{4,5},{5,4},{6,7},{7,6},{8,9},{9,8},{10,11... | collective-permute-start | bytes 9437192 | tf_op jit(solution)/shard_map/ppermute | solution.py:36
  153.7 0.1 copy.107
  153.8 7.2 %fusion = pred[768,256]{1,0:T(8,128)(4,1)S(1)} fusion(s32[768,50]{0,1:T(8,128)S(1)} %and_select_fusion), kind=kLoop, calls=%fused_computation.8 | loop fusion | flops 19464192 | bytes 350208 | tf_op jit(solution)/shard_map/reduce_or | solution.py:66
  161.0 0.3 copy.106
  161.5 0.1 add.226
  161.6 0.6 gather_fusion.2
  162.2 0.1 copy.108
  162.4 0.1 broadcast_in_dim.44
  162.5 5.2 %gather_fusion.3 = bf16[96,128,128]{2,1,0:T(8,128)(2,1)} fusion(bf16[4,4,6,128,128]{4,3,2,1,0:T(8,128)(2,1)} %pad_maximum_fusion, s32[96]{0:T(128)S(1)} %reshape.436), kind=kCustom, calls=%fused_computation.3 | custom fusion | bytes 6292608 | tf_op jit(solution)/shard_map/gather | solution.py:102
  167.7 5.2 %gather_fusion.4 = bf16[96,128,128]{2,1,0:T(8,128)(2,1)} fusion(bf16[4,4,6,128,128]{4,3,2,1,0:T(8,128)(2,1)} %collective-permute-done.13, s32[96]{0:T(128)S(1)} %reshape.436), kind=kCustom, calls=%fused_computation.4 | custom fusion | bytes 6292608 | tf_op jit(solution)/shard_map/gather | solution.py:102
  173.0 5.1 %gather_fusion.1 = bf16[12,128,768]{2,1,0:T(8,128)(2,1)} fusion(bf16[32,128,768]{2,1,0:T(8,128)(2,1)} %all-to-all-done.1, s32[1024]{0:T(1024)S(1)} %pad_clamp_fusion.1), kind=kCustom, calls=%fused_computation.1 | custom fusion | bytes 4718640 | tf_op jit(solution)/shard_map/gather | solution.py:70
  178.1 2.4 select_reduce_fusion
  180.5 0.2 fusion.14
  180.7 5.8 %collective-permute-start.14 = (f32[2,6,128]{2,1,0:T(8,128)S(1)}, f32[2,6,128]{2,1,0:T(8,128)S(1)}, u32[]{:S(2)}, u32[]{:S(2)}) collective-permute-start(f32[2,6,128]{2,1,0:T(8,128)S(1)} %pad_maximum_fusion.4), channel_id=1, source_target_pairs={{0,224},{32,0},{64,32},{96,64},{128,96},{160,128},{192,160},{224,1... | collective-permute-start | bytes 18440 | tf_op jit(solution)/shard_map/ppermute | solution.py:27
  186.6 0.2 bitcast_dynamic-update-slice_fusion.7
  186.8 2.7 collective-permute-start
  189.6 2.7 collective-permute-start.15
  192.2 5.4 %collective-permute-done.15 = f32[2,6,128]{2,1,0:T(8,128)S(1)} collective-permute-done((f32[2,6,128]{2,1,0:T(8,128)S(1)}, f32[2,6,128]{2,1,0:T(8,128)S(1)}, u32[]{:S(2)}, u32[]{:S(2)}) %collective-permute-start.15) | collective-permute-done | bytes 6176 | tf_op jit(solution)/shard_map/ppermute | solution.py:27
  197.6 3.4 %collective-permute-start.16 = (f32[2,6,128]{2,1,0:T(8,128)S(1)}, f32[2,6,128]{2,1,0:T(8,128)S(1)}, u32[]{:S(2)}, u32[]{:S(2)}) collective-permute-start(f32[2,6,128]{2,1,0:T(8,128)S(1)} %collective-permute-done.15), channel_id=1, source_target_pairs={{0,224},{32,0},{64,32},{96,64},{128,96},{160,128},{192,160},{224,1... | collective-permute-start | bytes 18440 | tf_op jit(solution)/shard_map/ppermute | solution.py:27
  201.1 3.7 %collective-permute-done.19 = f32[2,6,128]{2,1,0:T(8,128)S(1)} collective-permute-done((f32[2,6,128]{2,1,0:T(8,128)S(1)}, f32[2,6,128]{2,1,0:T(8,128)S(1)}, u32[]{:S(2)}, u32[]{:S(2)}) %collective-permute-start.19) | collective-permute-done | bytes 6176 | tf_op jit(solution)/shard_map/ppermute | solution.py:24
  204.8 3.7 %collective-permute-done.20 = f32[2,6,128]{2,1,0:T(8,128)S(1)} collective-permute-done((f32[2,6,128]{2,1,0:T(8,128)S(1)}, f32[2,6,128]{2,1,0:T(8,128)S(1)}, u32[]{:S(2)}, u32[]{:S(2)}) %collective-permute-start.20) | collective-permute-done | bytes 6176 | tf_op jit(solution)/shard_map/ppermute | solution.py:24
  208.5 0.1 collective-permute-start.4
  208.6 2.6 collective-permute-start.1
  211.3 5.1 %collective-permute-done.4 = bf16[6,128,256]{1,2,0:T(8,128)(2,1)S(1)} collective-permute-done((bf16[6,128,256]{1,2,0:T(8,128)(2,1)S(1)}, bf16[6,128,256]{1,2,0:T(8,128)(2,1)S(1)}, u32[]{:S(2)}, u32[]{:S(2)}) %collective-permute-start.4) | collective-permute-done | bytes 393248 | tf_op jit(solution)/shard_map/ppermute | solution.py:24
  216.4 2.7 collective-permute-start.2
  219.2 5.8 %collective-permute-done.5 = bf16[6,128,256]{1,2,0:T(8,128)(2,1)S(1)} collective-permute-done((bf16[6,128,256]{1,2,0:T(8,128)(2,1)S(1)}, bf16[6,128,256]{1,2,0:T(8,128)(2,1)S(1)}, u32[]{:S(2)}, u32[]{:S(2)}) %collective-permute-start.5) | collective-permute-done | bytes 393248 | tf_op jit(solution)/shard_map/ppermute | solution.py:24
  225.2 9.7 %collective-permute-done.6 = bf16[6,128,256]{1,2,0:T(8,128)(2,1)S(1)} collective-permute-done((bf16[6,128,256]{1,2,0:T(8,128)(2,1)S(1)}, bf16[6,128,256]{1,2,0:T(8,128)(2,1)S(1)}, u32[]{:S(2)}, u32[]{:S(2)}) %collective-permute-start.6) | collective-permute-done | bytes 393248 | tf_op jit(solution)/shard_map/ppermute | solution.py:24
  235.2 5.8 %convert_reduce_fusion.1 = f32[6,128,128]{2,1,0:T(8,128)S(1)} fusion(f32[8,6,128]{2,1,0:T(8,128)S(1)} %fusion.21, bf16[8,6,128,256]{2,3,1,0:T(8,128)(2,1)S(1)} %bitcast_dynamic-update-slice_fusion, bf16[6,8,256,128]{3,2,1,0:T(8,128)(2,1)S(1)} %bitcast.141, bf16[6,8,256,128]{3,2,1,0:T(8,128)(2,1)S(1)} %bitcast.142, pred[6,8,256]{2,1,0:T(8,128)(4,1)S(1)} %broadcast_in_dim.45), kind=kOutput, calls=%fused_computation.17 | convolution fusion | flops 407273472 | bytes 9867264 | tf_op jit(solution)/shard_map/gtmk,tgkc->gtmc/dot_general | solution.py:104
  241.1 0.3 collective-permute-start.22
  241.5 2.7 collective-permute-start.21
  244.1 3.1 collective-permute-done.22
  247.2 5.7 %collective-permute-done.23 = bf16[6,128,128]{2,1,0:T(8,128)(2,1)S(1)} collective-permute-done((bf16[6,128,128]{2,1,0:T(8,128)(2,1)S(1)}, bf16[6,128,128]{2,1,0:T(8,128)(2,1)S(1)}, u32[]{:S(2)}, u32[]{:S(2)}) %collective-permute-start.23) | collective-permute-done | bytes 196640 | tf_op jit(solution)/shard_map/ppermute | solution.py:24
  252.9 0.1 fusion.49
  253.0 0.1 collective-permute-start.25
  253.1 2.7 collective-permute-start.24
  255.8 9.4 %collective-permute-done.25 = bf16[4,6,128,128]{3,2,1,0:T(8,128)(2,1)S(1)} collective-permute-done((bf16[4,6,128,128]{3,2,1,0:T(8,128)(2,1)S(1)}, bf16[4,6,128,128]{3,2,1,0:T(8,128)(2,1)S(1)}, u32[]{:S(2)}, u32[]{:S(2)}) %collective-permute-start.25) | collective-permute-done | bytes 786464 | tf_op jit(solution)/shard_map/ppermute | solution.py:24
  265.2 18.6 %collective-permute-done.26 = bf16[4,6,128,128]{3,2,1,0:T(8,128)(2,1)S(1)} collective-permute-done((bf16[4,6,128,128]{3,2,1,0:T(8,128)(2,1)S(1)}, bf16[4,6,128,128]{3,2,1,0:T(8,128)(2,1)S(1)}, u32[]{:S(2)}, u32[]{:S(2)}) %collective-permute-start.26) | collective-permute-done | bytes 786464 | tf_op jit(solution)/shard_map/ppermute | solution.py:24
  283.8 1.8 pad_maximum_fusion.1
  285.7 12.0 %collective-permute-start.27 = (bf16[4,4,6,128,128]{4,3,2,1,0:T(8,128)(2,1)}, bf16[4,4,6,128,128]{4,3,2,1,0:T(8,128)(2,1)}, u32[]{:S(2)}, u32[]{:S(2)}) collective-permute-start(bf16[4,4,6,128,128]{4,3,2,1,0:T(8,128)(2,1)} %pad_maximum_fusion.1), channel_id=1, source_target_pairs={{0,1},{1,0},{2,3},{3,2},{4,5},{5,4},{6,7},{7,6},{8,9},{9,8},{10,11... | collective-permute-start | bytes 9437192 | tf_op jit(solution)/shard_map/ppermute | solution.py:36
  297.7 5.2 %gather_fusion.5 = bf16[96,128,128]{2,1,0:T(8,128)(2,1)} fusion(bf16[4,4,6,128,128]{4,3,2,1,0:T(8,128)(2,1)} %pad_maximum_fusion.1, s32[96]{0:T(128)S(1)} %reshape.436), kind=kCustom, calls=%fused_computation.5 | custom fusion | bytes 6292608 | tf_op jit(solution)/shard_map/gather | solution.py:102
  302.9 0.4 collective-permute-done.27
  303.3 5.2 %gather_fusion.6 = bf16[96,128,128]{2,1,0:T(8,128)(2,1)} fusion(bf16[4,4,6,128,128]{4,3,2,1,0:T(8,128)(2,1)} %collective-permute-done.27, s32[96]{0:T(128)S(1)} %reshape.436), kind=kCustom, calls=%fused_computation.6 | custom fusion | bytes 6292608 | tf_op jit(solution)/shard_map/gather | solution.py:102
  308.5 6.6 %convert_reduce_fusion = f32[6,128,128]{2,1,0:T(8,128)S(1)} fusion(f32[8,6,128]{2,1,0:T(8,128)S(1)} %fusion.21, bf16[8,6,128,256]{2,3,1,0:T(8,128)(2,1)} %copy-done.5, bf16[6,8,256,128]{3,2,1,0:T(8,128)(2,1)} %bitcast.143, bf16[6,8,256,128]{3,2,1,0:T(8,128)(2,1)} %bitcast.144, pred[6,8,256]{2,1,0:T(8,128)(4,1)S(1)} %broadcast_in_dim.45), kind=kOutput, calls=%fused_computation.15 | convolution fusion | flops 407273472 | bytes 9867264 | tf_op jit(solution)/shard_map/gtmk,tgkc->gtmc/dot_general | solution.py:104
  315.2 0.7 fusion.16
  (78 shorter events, 1.2 us)
Async XLA Ops:
  0.0 27.1 %copy-start = (bf16[768,1000]{0,1:T(8,128)(2,1)S(1)}, bf16[768,1000]{0,1:T(8,128)(2,1)}, u32[]{:S(2)}) copy-start(bf16[768,1000]{0,1:T(8,128)(2,1)} %param.6) | copy-start | bytes 4608004
  22.0 151.0 %all-to-all-start.1 = ((bf16[32,128,768]{2,1,0:T(8,128)(2,1)}), bf16[32,128,768]{2,1,0:T(8,128)(2,1)}, u32[]{:S(2)}, u32[]{:S(2)}) async-start(bf16[32,128,768]{2,1,0:T(8,128)(2,1)} %gather_fusion), calls=%async_computation.1 | async-start | bytes 12582912 | tf_op jit(solution)/shard_map/all_to_all | solution.py:69
  27.4 76.6 %collective-permute-start.8 = (bf16[6,128,128]{2,1,0:T(8,128)(2,1)S(1)}, bf16[6,128,128]{2,1,0:T(8,128)(2,1)S(1)}, u32[]{:S(2)}, u32[]{:S(2)}) collective-permute-start(bf16[6,128,128]{2,1,0:T(8,128)(2,1)S(1)} %bitcast.156), channel_id=1, source_target_pairs={{0,2},{2,4},{4,6},{6,0},{1,3},{3,5},{5,7},{7,1},{8,10},{10,12},{12... | collective-permute-start | bytes 589832 | tf_op jit(solution)/shard_map/ppermute | solution.py:24
  28.9 76.4 %collective-permute-start.7 = (bf16[6,128,128]{2,1,0:T(8,128)(2,1)S(1)}, bf16[6,128,128]{2,1,0:T(8,128)(2,1)S(1)}, u32[]{:S(2)}, u32[]{:S(2)}) collective-permute-start(bf16[6,128,128]{2,1,0:T(8,128)(2,1)S(1)} %bitcast.157), channel_id=1, source_target_pairs={{0,6},{2,0},{4,2},{6,4},{1,7},{3,1},{5,3},{7,5},{8,14},{10,8},{12,... | collective-permute-start | bytes 589832 | tf_op jit(solution)/shard_map/ppermute | solution.py:27
  104.0 7.6 %collective-permute-start.9 = (bf16[6,128,128]{2,1,0:T(8,128)(2,1)S(1)}, bf16[6,128,128]{2,1,0:T(8,128)(2,1)S(1)}, u32[]{:S(2)}, u32[]{:S(2)}) collective-permute-start(bf16[6,128,128]{2,1,0:T(8,128)(2,1)S(1)} %collective-permute-done.8), channel_id=1, source_target_pairs={{0,2},{2,4},{4,6},{6,0},{1,3},{3,5},{5,7},{7,1},{8,10},{10,12},{12... | collective-permute-start | bytes 589832 | tf_op jit(solution)/shard_map/ppermute | solution.py:24
  111.8 18.8 %collective-permute-start.11 = (bf16[4,6,128,128]{3,2,1,0:T(8,128)(2,1)S(1)}, bf16[4,6,128,128]{3,2,1,0:T(8,128)(2,1)S(1)}, u32[]{:S(2)}, u32[]{:S(2)}) collective-permute-start(bf16[4,6,128,128]{3,2,1,0:T(8,128)(2,1)S(1)} %get-tuple-element.12), channel_id=1, source_target_pairs={{0,8},{8,16},{16,24},{24,0},{1,9},{9,17},{17,25},{25,1},{2,10},{10... | collective-permute-start | bytes 2359304 | tf_op jit(solution)/shard_map/ppermute | solution.py:24
  113.0 17.6 %collective-permute-start.10 = (bf16[4,6,128,128]{3,2,1,0:T(8,128)(2,1)S(1)}, bf16[4,6,128,128]{3,2,1,0:T(8,128)(2,1)S(1)}, u32[]{:S(2)}, u32[]{:S(2)}) collective-permute-start(bf16[4,6,128,128]{3,2,1,0:T(8,128)(2,1)S(1)} %get-tuple-element.12), channel_id=1, source_target_pairs={{0,24},{8,0},{16,8},{24,16},{1,25},{9,1},{17,9},{25,17},{2,26},{10... | collective-permute-start | bytes 2359304 | tf_op jit(solution)/shard_map/ppermute | solution.py:27
  130.6 17.9 %collective-permute-start.12 = (bf16[4,6,128,128]{3,2,1,0:T(8,128)(2,1)S(1)}, bf16[4,6,128,128]{3,2,1,0:T(8,128)(2,1)S(1)}, u32[]{:S(2)}, u32[]{:S(2)}) collective-permute-start(bf16[4,6,128,128]{3,2,1,0:T(8,128)(2,1)S(1)} %collective-permute-done.11), channel_id=1, source_target_pairs={{0,8},{8,16},{16,24},{24,0},{1,9},{9,17},{17,25},{25,1},{2,10},{10... | collective-permute-start | bytes 2359304 | tf_op jit(solution)/shard_map/ppermute | solution.py:24
  148.5 5.1 %copy-start.6 = (s32[6,16]{1,0:T(8,128)S(1)}, s32[6,16]{1,0:T(8,128)}, u32[]{:S(2)}) copy-start(s32[6,16]{1,0:T(8,128)} %param.8) | copy-start | bytes 1156
  148.5 5.2 %copy-start.4 = (s32[768,50]{0,1:T(8,128)S(1)}, s32[768,50]{0,1:T(8,128)}, u32[]{:S(2)}) copy-start(s32[768,50]{0,1:T(8,128)} %param.9) | copy-start | bytes 460804
  148.5 14.0 %copy-start.7 = (f32[768]{0:T(1024)S(1)}, f32[768]{0:T(1024)}, u32[]{:S(2)}) copy-start(f32[768]{0:T(1024)} %param.7) | copy-start | bytes 9220
  150.4 17.3 %collective-permute-start.13 = (bf16[4,4,6,128,128]{4,3,2,1,0:T(8,128)(2,1)}, bf16[4,4,6,128,128]{4,3,2,1,0:T(8,128)(2,1)}, u32[]{:S(2)}, u32[]{:S(2)}) collective-permute-start(bf16[4,4,6,128,128]{4,3,2,1,0:T(8,128)(2,1)} %pad_maximum_fusion), channel_id=1, source_target_pairs={{0,1},{1,0},{2,3},{3,2},{4,5},{5,4},{6,7},{7,6},{8,9},{9,8},{10,11... | collective-permute-start | bytes 9437192 | tf_op jit(solution)/shard_map/ppermute | solution.py:36
  172.9 5.1 %copy-start.1 = (bf16[768,768]{1,0:T(8,128)(2,1)S(1)}, bf16[768,768]{1,0:T(8,128)(2,1)}, u32[]{:S(2)}) copy-start(bf16[768,768]{1,0:T(8,128)(2,1)} %param.5) | copy-start | bytes 3538948
  180.7 8.8 %collective-permute-start.14 = (f32[2,6,128]{2,1,0:T(8,128)S(1)}, f32[2,6,128]{2,1,0:T(8,128)S(1)}, u32[]{:S(2)}, u32[]{:S(2)}) collective-permute-start(f32[2,6,128]{2,1,0:T(8,128)S(1)} %pad_maximum_fusion.4), channel_id=1, source_target_pairs={{0,224},{32,0},{64,32},{96,64},{128,96},{160,128},{192,160},{224,1... | collective-permute-start | bytes 18440 | tf_op jit(solution)/shard_map/ppermute | solution.py:27
  186.6 5.7 %collective-permute-start.17 = (f32[2,6,128]{2,1,0:T(8,128)S(1)}, f32[2,6,128]{2,1,0:T(8,128)S(1)}, u32[]{:S(2)}, u32[]{:S(2)}) collective-permute-start(f32[2,6,128]{2,1,0:T(8,128)S(1)} %pad_maximum_fusion.4), channel_id=1, source_target_pairs={{0,32},{32,64},{64,96},{96,128},{128,160},{160,192},{192,224},{224... | collective-permute-start | bytes 18440 | tf_op jit(solution)/shard_map/ppermute | solution.py:24
  186.6 48.6 %copy-start.3 = (bf16[96,128,128]{2,1,0:T(8,128)(2,1)S(1)}, bf16[96,128,128]{2,1,0:T(8,128)(2,1)}, u32[]{:S(2)}) copy-start(bf16[96,128,128]{2,1,0:T(8,128)(2,1)} %gather_fusion.4) | copy-start | bytes 9437188
  186.8 48.4 %copy-start.2 = (bf16[96,128,128]{2,1,0:T(8,128)(2,1)S(1)}, bf16[96,128,128]{2,1,0:T(8,128)(2,1)}, u32[]{:S(2)}) copy-start(bf16[96,128,128]{2,1,0:T(8,128)(2,1)} %gather_fusion.3) | copy-start | bytes 9437188
  186.8 21.8 %collective-permute-start = (bf16[6,128,256]{1,2,0:T(8,128)(2,1)S(1)}, bf16[6,128,256]{1,2,0:T(8,128)(2,1)S(1)}, u32[]{:S(2)}, u32[]{:S(2)}) collective-permute-start(bf16[6,128,256]{1,2,0:T(8,128)(2,1)S(1)} %get-tuple-element.6), channel_id=1, source_target_pairs={{0,224},{32,0},{64,32},{96,64},{128,96},{160,128},{192,160},{224,1... | collective-permute-start | bytes 1179656 | tf_op jit(solution)/shard_map/ppermute | solution.py:27
  189.6 18.9 %collective-permute-start.3 = (bf16[6,128,256]{1,2,0:T(8,128)(2,1)S(1)}, bf16[6,128,256]{1,2,0:T(8,128)(2,1)S(1)}, u32[]{:S(2)}, u32[]{:S(2)}) collective-permute-start(bf16[6,128,256]{1,2,0:T(8,128)(2,1)S(1)} %get-tuple-element.6), channel_id=1, source_target_pairs={{0,32},{32,64},{64,96},{96,128},{128,160},{160,192},{192,224},{224... | collective-permute-start | bytes 1179656 | tf_op jit(solution)/shard_map/ppermute | solution.py:24
  189.6 8.1 %collective-permute-start.15 = (f32[2,6,128]{2,1,0:T(8,128)S(1)}, f32[2,6,128]{2,1,0:T(8,128)S(1)}, u32[]{:S(2)}, u32[]{:S(2)}) collective-permute-start(f32[2,6,128]{2,1,0:T(8,128)S(1)} %collective-permute-done.14), channel_id=1, source_target_pairs={{0,224},{32,0},{64,32},{96,64},{128,96},{160,128},{192,160},{224,1... | collective-permute-start | bytes 18440 | tf_op jit(solution)/shard_map/ppermute | solution.py:27
  192.2 8.8 %collective-permute-start.18 = (f32[2,6,128]{2,1,0:T(8,128)S(1)}, f32[2,6,128]{2,1,0:T(8,128)S(1)}, u32[]{:S(2)}, u32[]{:S(2)}) collective-permute-start(f32[2,6,128]{2,1,0:T(8,128)S(1)} %collective-permute-done.17), channel_id=1, source_target_pairs={{0,32},{32,64},{64,96},{96,128},{128,160},{160,192},{192,224},{224... | collective-permute-start | bytes 18440 | tf_op jit(solution)/shard_map/ppermute | solution.py:24
  197.6 7.1 %collective-permute-start.16 = (f32[2,6,128]{2,1,0:T(8,128)S(1)}, f32[2,6,128]{2,1,0:T(8,128)S(1)}, u32[]{:S(2)}, u32[]{:S(2)}) collective-permute-start(f32[2,6,128]{2,1,0:T(8,128)S(1)} %collective-permute-done.15), channel_id=1, source_target_pairs={{0,224},{32,0},{64,32},{96,64},{128,96},{160,128},{192,160},{224,1... | collective-permute-start | bytes 18440 | tf_op jit(solution)/shard_map/ppermute | solution.py:27
  201.1 3.7 %collective-permute-start.19 = (f32[2,6,128]{2,1,0:T(8,128)S(1)}, f32[2,6,128]{2,1,0:T(8,128)S(1)}, u32[]{:S(2)}, u32[]{:S(2)}) collective-permute-start(f32[2,6,128]{2,1,0:T(8,128)S(1)} %collective-permute-done.18), channel_id=1, source_target_pairs={{0,32},{32,64},{64,96},{96,128},{128,160},{160,192},{192,224},{224... | collective-permute-start | bytes 18440 | tf_op jit(solution)/shard_map/ppermute | solution.py:24
  204.8 3.7 %collective-permute-start.20 = (f32[2,6,128]{2,1,0:T(8,128)S(1)}, f32[2,6,128]{2,1,0:T(8,128)S(1)}, u32[]{:S(2)}, u32[]{:S(2)}) collective-permute-start(f32[2,6,128]{2,1,0:T(8,128)S(1)} %collective-permute-done.19), channel_id=1, source_target_pairs={{0,32},{32,64},{64,96},{96,128},{128,160},{160,192},{192,224},{224... | collective-permute-start | bytes 18440 | tf_op jit(solution)/shard_map/ppermute | solution.py:24
  208.5 7.9 %collective-permute-start.4 = (bf16[6,128,256]{1,2,0:T(8,128)(2,1)S(1)}, bf16[6,128,256]{1,2,0:T(8,128)(2,1)S(1)}, u32[]{:S(2)}, u32[]{:S(2)}) collective-permute-start(bf16[6,128,256]{1,2,0:T(8,128)(2,1)S(1)} %collective-permute-done.3), channel_id=1, source_target_pairs={{0,32},{32,64},{64,96},{96,128},{128,160},{160,192},{192,224},{224... | collective-permute-start | bytes 1179656 | tf_op jit(solution)/shard_map/ppermute | solution.py:24
  208.6 7.8 %collective-permute-start.1 = (bf16[6,128,256]{1,2,0:T(8,128)(2,1)S(1)}, bf16[6,128,256]{1,2,0:T(8,128)(2,1)S(1)}, u32[]{:S(2)}, u32[]{:S(2)}) collective-permute-start(bf16[6,128,256]{1,2,0:T(8,128)(2,1)S(1)} %collective-permute-done), channel_id=1, source_target_pairs={{0,224},{32,0},{64,32},{96,64},{128,96},{160,128},{192,160},{224,1... | collective-permute-start | bytes 1179656 | tf_op jit(solution)/shard_map/ppermute | solution.py:27
  216.4 8.7 %collective-permute-start.5 = (bf16[6,128,256]{1,2,0:T(8,128)(2,1)S(1)}, bf16[6,128,256]{1,2,0:T(8,128)(2,1)S(1)}, u32[]{:S(2)}, u32[]{:S(2)}) collective-permute-start(bf16[6,128,256]{1,2,0:T(8,128)(2,1)S(1)} %collective-permute-done.4), channel_id=1, source_target_pairs={{0,32},{32,64},{64,96},{96,128},{128,160},{160,192},{192,224},{224... | collective-permute-start | bytes 1179656 | tf_op jit(solution)/shard_map/ppermute | solution.py:24
  216.4 8.7 %collective-permute-start.2 = (bf16[6,128,256]{1,2,0:T(8,128)(2,1)S(1)}, bf16[6,128,256]{1,2,0:T(8,128)(2,1)S(1)}, u32[]{:S(2)}, u32[]{:S(2)}) collective-permute-start(bf16[6,128,256]{1,2,0:T(8,128)(2,1)S(1)} %collective-permute-done.1), channel_id=1, source_target_pairs={{0,224},{32,0},{64,32},{96,64},{128,96},{160,128},{192,160},{224,1... | collective-permute-start | bytes 1179656 | tf_op jit(solution)/shard_map/ppermute | solution.py:27
  225.1 9.8 %collective-permute-start.6 = (bf16[6,128,256]{1,2,0:T(8,128)(2,1)S(1)}, bf16[6,128,256]{1,2,0:T(8,128)(2,1)S(1)}, u32[]{:S(2)}, u32[]{:S(2)}) collective-permute-start(bf16[6,128,256]{1,2,0:T(8,128)(2,1)S(1)} %collective-permute-done.5), channel_id=1, source_target_pairs={{0,32},{32,64},{64,96},{96,128},{128,160},{160,192},{192,224},{224... | collective-permute-start | bytes 1179656 | tf_op jit(solution)/shard_map/ppermute | solution.py:24
  235.1 5.9 %copy-start.5 = (bf16[8,6,128,256]{2,3,1,0:T(8,128)(2,1)}, bf16[8,6,128,256]{2,3,1,0:T(8,128)(2,1)S(1)}, u32[]{:S(2)}) copy-start(bf16[8,6,128,256]{2,3,1,0:T(8,128)(2,1)S(1)} %bitcast_dynamic-update-slice_fusion) | copy-start | bytes 9437188
  241.1 6.0 %collective-permute-start.22 = (bf16[6,128,128]{2,1,0:T(8,128)(2,1)S(1)}, bf16[6,128,128]{2,1,0:T(8,128)(2,1)S(1)}, u32[]{:S(2)}, u32[]{:S(2)}) collective-permute-start(bf16[6,128,128]{2,1,0:T(8,128)(2,1)S(1)} %bitcast.153), channel_id=1, source_target_pairs={{0,2},{2,4},{4,6},{6,0},{1,3},{3,5},{5,7},{7,1},{8,10},{10,12},{12... | collective-permute-start | bytes 589832 | tf_op jit(solution)/shard_map/ppermute | solution.py:24
  241.5 5.7 %collective-permute-start.21 = (bf16[6,128,128]{2,1,0:T(8,128)(2,1)S(1)}, bf16[6,128,128]{2,1,0:T(8,128)(2,1)S(1)}, u32[]{:S(2)}, u32[]{:S(2)}) collective-permute-start(bf16[6,128,128]{2,1,0:T(8,128)(2,1)S(1)} %bitcast.154), channel_id=1, source_target_pairs={{0,6},{2,0},{4,2},{6,4},{1,7},{3,1},{5,3},{7,5},{8,14},{10,8},{12,... | collective-permute-start | bytes 589832 | tf_op jit(solution)/shard_map/ppermute | solution.py:27
  247.2 5.7 %collective-permute-start.23 = (bf16[6,128,128]{2,1,0:T(8,128)(2,1)S(1)}, bf16[6,128,128]{2,1,0:T(8,128)(2,1)S(1)}, u32[]{:S(2)}, u32[]{:S(2)}) collective-permute-start(bf16[6,128,128]{2,1,0:T(8,128)(2,1)S(1)} %collective-permute-done.22), channel_id=1, source_target_pairs={{0,2},{2,4},{4,6},{6,0},{1,3},{3,5},{5,7},{7,1},{8,10},{10,12},{12... | collective-permute-start | bytes 589832 | tf_op jit(solution)/shard_map/ppermute | solution.py:24
  253.0 12.1 %collective-permute-start.25 = (bf16[4,6,128,128]{3,2,1,0:T(8,128)(2,1)S(1)}, bf16[4,6,128,128]{3,2,1,0:T(8,128)(2,1)S(1)}, u32[]{:S(2)}, u32[]{:S(2)}) collective-permute-start(bf16[4,6,128,128]{3,2,1,0:T(8,128)(2,1)S(1)} %get-tuple-element.10), channel_id=1, source_target_pairs={{0,8},{8,16},{16,24},{24,0},{1,9},{9,17},{17,25},{25,1},{2,10},{10... | collective-permute-start | bytes 2359304 | tf_op jit(solution)/shard_map/ppermute | solution.py:24
  253.1 12.0 %collective-permute-start.24 = (bf16[4,6,128,128]{3,2,1,0:T(8,128)(2,1)S(1)}, bf16[4,6,128,128]{3,2,1,0:T(8,128)(2,1)S(1)}, u32[]{:S(2)}, u32[]{:S(2)}) collective-permute-start(bf16[4,6,128,128]{3,2,1,0:T(8,128)(2,1)S(1)} %get-tuple-element.10), channel_id=1, source_target_pairs={{0,24},{8,0},{16,8},{24,16},{1,25},{9,1},{17,9},{25,17},{2,26},{10... | collective-permute-start | bytes 2359304 | tf_op jit(solution)/shard_map/ppermute | solution.py:27
  265.2 18.6 %collective-permute-start.26 = (bf16[4,6,128,128]{3,2,1,0:T(8,128)(2,1)S(1)}, bf16[4,6,128,128]{3,2,1,0:T(8,128)(2,1)S(1)}, u32[]{:S(2)}, u32[]{:S(2)}) collective-permute-start(bf16[4,6,128,128]{3,2,1,0:T(8,128)(2,1)S(1)} %collective-permute-done.25), channel_id=1, source_target_pairs={{0,8},{8,16},{16,24},{24,0},{1,9},{9,17},{17,25},{25,1},{2,10},{10... | collective-permute-start | bytes 2359304 | tf_op jit(solution)/shard_map/ppermute | solution.py:24
  285.7 17.7 %collective-permute-start.27 = (bf16[4,4,6,128,128]{4,3,2,1,0:T(8,128)(2,1)}, bf16[4,4,6,128,128]{4,3,2,1,0:T(8,128)(2,1)}, u32[]{:S(2)}, u32[]{:S(2)}) collective-permute-start(bf16[4,4,6,128,128]{4,3,2,1,0:T(8,128)(2,1)} %pad_maximum_fusion.1), channel_id=1, source_target_pairs={{0,1},{1,0},{2,3},{3,2},{4,5},{5,4},{6,7},{7,6},{8,9},{9,8},{10,11... | collective-permute-start | bytes 9437192 | tf_op jit(solution)/shard_map/ppermute | solution.py:36

commit v9 on v7

--- a/solution.py
+++ b/solution.py
@@ -73,9 +73,12 @@
     on_this_core = (shard_of % 2 == lax.axis_index("core"))[..., None, None]
     pair_ids = (shard_of // 2) * blocks_here + pattern % blocks_here
 
-    def propagate_using(gathered, seed):
-        same_core, other_core = gathered
-        candidates = jnp.where(on_this_core, same_core[pair_ids], other_core[pair_ids])
+    def propagate_using(gathered, seed, whole=False):
+        if whole:
+            candidates = gathered[pattern]
+        else:
+            same_core, other_core = gathered
+            candidates = jnp.where(on_this_core, same_core[pair_ids], other_core[pair_ids])
         candidates = candidates.reshape(blocks_here, n_row, span, lanes)
         pieces = jnp.einsum(
             "gtmk,tgkc->gtmc", all_weights, candidates, preferred_element_type=jnp.float32
@@ -85,8 +88,8 @@
         return (mixing * summed + (1.0 - mixing) * seed.astype(jnp.float32)).astype(jnp.bfloat16)
 
     spread = propagate_using(all_labels, my_labels)
-    all_spread = gather_columns(spread)
-    return propagate_using(all_spread, my_labels)[:, :per_device]
+    whole_spread = lax.all_gather(spread, COL, tiled=True).reshape(-1, BLOCK, lanes)
+    return propagate_using(whole_spread, my_labels, whole=True)[:, :per_device]
 
 
 def solution(mesh):

time: 259 us -> 253 us (0.977)
  local copies, waits for them, and re-layouts: 31.1 us -> 27.4 us
    all_gather x0 -> x1, waiting for transfers between devices: none -> 53.4 us  [body(): lax.all_gather(spread, COL, tiled=True).reshape(-1, BLOCK, lanes)]
    all_gather x2 -> x1, waiting for transfers between devices: 59.8 us -> 8.61 us  [gather_columns(): same_core = lax.all_gather(x, 'chip', tiled=True).reshape(-1, BLOCK, width)]
    gather x0 -> x1, local copies, waits for them, and re-layouts: none -> 5.46 us  [propagate_using(): candidates = gathered[pattern]]
    gather x2 -> x1, local copies, waits for them, and re-layouts: 9.28 us -> 4.57 us  [propagate_using(): same_core[pair_ids]]
    gather x2 -> x1, local copies, waits for them, and re-layouts: 9.16 us -> 4.67 us  [propagate_using(): other_core[pair_ids]]
  transfers between devices with their start and end apart: 6 -> 5, of which waited for: 5 -> 4; matrix products, arithmetic and copies ran while one was open for 12% -> 11% of each run, Pallas kernels for 0% -> 0%
where the time goes in v9:
time: 253 us; the launch traced here: 252 us
  waiting for transfers between devices  143 us (57%)
  blocking collectives  37.7 us (15%)
  local copies, waits for them, and re-layouts  27.4 us (11%)
  between operations  13.3 us (5%)
  matrix products  12.2 us (5%)
  other arithmetic  11.5 us (5%)
  starting transfers between devices  6.68 us (3%)
    all_to_all x1, waiting for transfers between devices, body(): lax.all_to_all(send_emb, COL, split_axis=0, concat_axis=0, tiled=True)  68.2 us
    all_gather x1, waiting for transfers between devices, body(): lax.all_gather(spread, COL, tiled=True).reshape(-1, BLOCK, lanes)  53.4 us
    all_gather x1, blocking collectives, body(): stats = lax.all_gather(jnp.stack([local_max, local_sum]), 'row')  22.3 us
    all_to_all x1, blocking collectives, body(): lax.all_to_all(wanted, COL, split_axis=0, concat_axis=0, tiled=True)  15.3 us
    all_gather x1, waiting for transfers between devices, body(): all_weights = lax.all_gather(local_weights, 'row')  13.1 us
    dot_general x2, matrix products, propagate_using(): jnp.einsum('gtmk,tgkc->gtmc', all_weights, candidates, preferred_element_...  9.73 us
    all_gather x1, waiting for transfers between devices, gather_columns(): same_core = lax.all_gather(x, 'chip', tiled=True).reshape(-1, BLOCK, width)  8.61 us
    reduce_or x1, other arithmetic, body(): in_mask = jnp.any(shifted[:, :, None] == positions[None, None, :], axis=1)  7.22 us
  transfers between devices with their start and end apart: 5, of which 4 were waited for; matrix products, arithmetic and copies ran while one was open for 11% of the time, Pallas kernels for 0%

profile of v9, /device:TPU:1, one launch (start us, length us, event | category | flops | bytes accessed | tf_op | source)
XLA Modules:
  0.0 252.2 jit_solution(4640348290725915735)
XLA Ops:
  6.5 0.0 copy-start
  6.5 0.8 fusion.23
  7.4 0.7 compare_select_fusion.1
  8.1 0.1 compare_select_fusion.3
  8.1 0.1 fusion.22
  8.2 0.1 copy.42
  8.3 15.3 %all_to_all.17 = s32[32,1,1]{2,1,0:T(1,128)S(1)} all-to-all(s32[32,1,1]{2,1,0:T(1,128)S(1)} %copy.42), channel_id=1, replica_groups=mesh['row'=8,'chip'=16,'core'=2] {'chip','core'}, dimensions={0} | all-to-all | bytes 256 | tf_op jit(solution)/shard_map/all_to_all | solution.py:42
  23.7 0.7 reduce.1
  24.4 4.9 %gather_fusion = bf16[32,128,768]{2,1,0:T(8,128)(2,1)} fusion(bf16[6,128,768]{2,1,0:T(8,128)(2,1)} %bitcast.49, s32[1024]{0:T(1024)S(1)} %pad_clamp_fusion.3), kind=kCustom, calls=%fused_computation | custom fusion | bytes 12583040 | tf_op jit(solution)/shard_map/gather | solution.py:44
  29.2 0.0 copy-start.2
  29.2 0.0 copy-start.3
  29.2 5.3 %all-to-all-start.1 = ((bf16[32,128,768]{2,1,0:T(8,128)(2,1)}), bf16[32,128,768]{2,1,0:T(8,128)(2,1)}, u32[]{:S(2)}, u32[]{:S(2)}) async-start(bf16[32,128,768]{2,1,0:T(8,128)(2,1)} %gather_fusion), calls=%async_computation.1 | async-start | bytes 12582912 | tf_op jit(solution)/shard_map/all_to_all | solution.py:55
  34.5 0.0 all-gather.6.cloned.1.call-start
  34.6 0.0 copy-done
  34.6 0.1 constant_dynamic-slice_fusion
  34.6 0.2 copy.51
  34.8 0.0 copy-start.1
  34.8 0.7 pad.4
  35.5 0.0 all-gather.6.cloned.1.call-update
  35.6 0.0 all-gather.10.cloned.1.call-start
  35.6 0.0 copy-done.2
  35.7 7.2 %fusion = pred[768,256]{1,0:T(8,128)(4,1)S(1)} fusion(s32[768,50]{0,1:T(8,128)S(1)} %and_select_fusion), kind=kLoop, calls=%fused_computation.6 | loop fusion | flops 19464192 | bytes 350208 | tf_op jit(solution)/shard_map/reduce_or | solution.py:52
  42.9 0.3 copy.44
  43.2 0.1 reshape.92
  43.3 0.0 copy-done.3
  43.3 68.2 %all-to-all-done.1 = bf16[32,128,768]{2,1,0:T(8,128)(2,1)} async-done(((bf16[32,128,768]{2,1,0:T(8,128)(2,1)}), bf16[32,128,768]{2,1,0:T(8,128)(2,1)}, u32[]{:S(2)}, u32[]{:S(2)}) %all-to-all-start.1) | async-done | bytes 6291488 | tf_op jit(solution)/shard_map/all_to_all | solution.py:55
  111.5 5.2 %gather_fusion.1 = bf16[12,128,768]{2,1,0:T(8,128)(2,1)} fusion(bf16[32,128,768]{2,1,0:T(8,128)(2,1)} %all-to-all-done.1, s32[1024]{0:T(1024)S(1)} %pad_clamp_fusion.2), kind=kCustom, calls=%fused_computation.1 | custom fusion | bytes 4718640 | tf_op jit(solution)/shard_map/gather | solution.py:56
  116.8 0.0 copy-done.1
  116.8 2.5 select_reduce_fusion
  119.3 0.2 fusion.15
  119.5 1.0 copy.45
  120.4 0.0 all-gather.10.cloned.1.call-update
  120.5 0.0 all-gather.8.cloned.1.call-start
  120.5 8.6 %all-gather.6.cloned.1.call-done = bf16[12288,128]{1,0:T(8,128)(2,1)} async-done(((bf16[768,128]{1,0:T(8,128)(2,1)}), bf16[12288,128]{1,0:T(8,128)(2,1)}) %all-gather.6.cloned.1.call-update) | async-done | bytes 3145744 | tf_op jit(solution)/shard_map/all_gather | solution.py:21
  129.1 1.3 collective-permute-start
  130.4 0.1 reshape.100
  130.5 0.1 broadcast_in_dim.63
  130.6 4.6 %gather_fusion.2 = bf16[96,128,128]{2,1,0:T(8,128)(2,1)} fusion(bf16[96,128,128]{2,1,0:T(8,128)(2,1)} %bitcast.52, s32[1024]{0:T(1024)S(1)} %pad_clamp_fusion.1), kind=kCustom, calls=%fused_computation.2 | custom fusion | bytes 6291840 | tf_op jit(solution)/shard_map/gather | solution.py:81
  135.2 22.3 %all-gather.1 = f32[16,6,128]{2,1,0:T(8,128)S(1)} all-gather(f32[2,6,128]{2,1,0:T(8,128)S(1)} %pad_maximum_fusion), channel_id=3, replica_groups=mesh['row'=8,'chip'=16,'core'=2] {'row'}, dimensions={0}, use_global_device_ids=true | all-gather | bytes 55296 | tf_op jit(solution)/shard_map/all_gather | solution.py:66
  157.6 0.0 collective-permute-done
  157.6 4.7 %gather_fusion.3 = bf16[96,128,128]{2,1,0:T(8,128)(2,1)} fusion(bf16[96,128,128]{2,1,0:T(8,128)(2,1)} %collective-permute-done, s32[1024]{0:T(1024)S(1)} %pad_clamp_fusion.1), kind=kCustom, calls=%fused_computation.3 | custom fusion | bytes 6291840 | tf_op jit(solution)/shard_map/gather | solution.py:81
  162.3 13.1 %all-gather.10.cloned.1.call-done = bf16[48,128,256]{2,1,0:T(8,128)(2,1)} async-done(((bf16[6,128,256]{2,1,0:T(8,128)(2,1)}), bf16[48,128,256]{2,1,0:T(8,128)(2,1)}) %all-gather.10.cloned.1.call-update) | async-done | bytes 3145744 | tf_op jit(solution)/shard_map/all_gather | solution.py:67
  175.4 5.9 %convert_reduce_fusion.1 = f32[6,128,128]{2,1,0:T(8,128)S(1)} fusion(f32[8,6,128]{2,1,0:T(8,128)S(1)} %fusion.21, bf16[8,6,128,256]{3,2,1,0:T(8,128)(2,1)} %bitcast.66, bf16[6,8,256,128]{3,2,1,0:T(8,128)(2,1)} %bitcast.53, bf16[6,8,256,128]{3,2,1,0:T(8,128)(2,1)} %bitcast.54, pred[6,8,256]{2,1,0:T(8,128)(4,1)S(1)} %broadcast_in_dim.64), kind=kOutput, calls=%fused_computation.13 | convolution fusion | flops 407273472 | bytes 9867264 | tf_op jit(solution)/shard_map/gtmk,tgkc->gtmc/dot_general | solution.py:83
  181.3 0.8 fusion.17
  182.0 0.0 all-gather.8.cloned.1.call-update
  182.1 0.1 reshape.116
  182.2 53.4 %all-gather.8.cloned.1.call-done = bf16[24576,128]{1,0:T(8,128)(2,1)} async-done(((bf16[768,128]{1,0:T(8,128)(2,1)}), bf16[24576,128]{1,0:T(8,128)(2,1)}) %all-gather.8.cloned.1.call-update) | async-done | bytes 6291472 | tf_op jit(solution)/shard_map/all_gather | solution.py:91
  235.5 5.5 %gather_fusion.4 = bf16[96,128,128]{2,1,0:T(8,128)(2,1)} fusion(bf16[192,128,128]{2,1,0:T(8,128)(2,1)} %bitcast.58, s32[1024]{0:T(1024)S(1)} %pad_clamp_fusion), kind=kCustom, calls=%fused_computation.4 | custom fusion | bytes 6291840 | tf_op jit(solution)/shard_map/gather | solution.py:78
  241.0 3.9 %convert_reduce_fusion = f32[6,128,128]{2,1,0:T(8,128)S(1)} fusion(f32[8,6,128]{2,1,0:T(8,128)S(1)} %fusion.21, bf16[8,6,128,256]{3,2,1,0:T(8,128)(2,1)} %bitcast.67, bf16[6,8,256,128]{3,2,1,0:T(8,128)(2,1)} %bitcast.55), kind=kOutput, calls=%fused_computation.11 | convolution fusion | flops 405700608 | bytes 6709248 | tf_op jit(solution)/shard_map/gtmk,tgkc->gtmc/dot_general | solution.py:83
  244.9 0.7 fusion.16
  (14 shorter events, 0.2 us)
Async XLA Ops:
  6.5 28.0 %copy-start = (bf16[768,1000]{0,1:T(8,128)(2,1)S(1)}, bf16[768,1000]{0,1:T(8,128)(2,1)}, u32[]{:S(2)}) copy-start(bf16[768,1000]{0,1:T(8,128)(2,1)} %param.6) | copy-start | bytes 4608004
  29.2 6.4 %copy-start.2 = (s32[768,50]{0,1:T(8,128)S(1)}, s32[768,50]{0,1:T(8,128)}, u32[]{:S(2)}) copy-start(s32[768,50]{0,1:T(8,128)} %param.9) | copy-start | bytes 460804
  29.2 14.0 %copy-start.3 = (f32[768]{0:T(1024)S(1)}, f32[768]{0:T(1024)}, u32[]{:S(2)}) copy-start(f32[768]{0:T(1024)} %param.7) | copy-start | bytes 9220
  29.2 82.3 %all-to-all-start.1 = ((bf16[32,128,768]{2,1,0:T(8,128)(2,1)}), bf16[32,128,768]{2,1,0:T(8,128)(2,1)}, u32[]{:S(2)}, u32[]{:S(2)}) async-start(bf16[32,128,768]{2,1,0:T(8,128)(2,1)} %gather_fusion), calls=%async_computation.1 | async-start | bytes 12582912 | tf_op jit(solution)/shard_map/all_to_all | solution.py:55
  34.5 94.6 %all-gather.6.cloned.1.call-start = ((), (), s32[]{:S(2)}) async-start(), calls=%async_computation.2 | async-start | bytes 3342336 | tf_op jit(solution)/shard_map/all_gather | solution.py:21
  34.8 82.0 %copy-start.1 = (bf16[768,768]{1,0:T(8,128)(2,1)S(1)}, bf16[768,768]{1,0:T(8,128)(2,1)}, u32[]{:S(2)}) copy-start(bf16[768,768]{1,0:T(8,128)(2,1)} %param.5) | copy-start | bytes 3538948
  35.6 139.8 %all-gather.10.cloned.1.call-start = ((), (), s32[]{:S(2)}) async-start(), calls=%async_computation.4 | async-start | bytes 3538944 | tf_op jit(solution)/shard_map/all_gather | solution.py:67
  120.5 115.1 %all-gather.8.cloned.1.call-start = ((), (), s32[]{:S(2)}) async-start(), calls=%async_computation.3 | async-start | bytes 6488064 | tf_op jit(solution)/shard_map/all_gather | solution.py:91
  129.1 28.5 %collective-permute-start = (bf16[96,128,128]{2,1,0:T(8,128)(2,1)}, bf16[96,128,128]{2,1,0:T(8,128)(2,1)}, u32[]{:S(2)}, u32[]{:S(2)}) collective-permute-start(bf16[96,128,128]{2,1,0:T(8,128)(2,1)} %bitcast.51), channel_id=1, source_target_pairs={{0,1},{1,0},{2,3},{3,2},{4,5},{5,4},{6,7},{7,6},{8,9},{9,8},{10,11... | collective-permute-start | bytes 9437192 | tf_op jit(solution)/shard_map/ppermute | solution.py:22
Sparse Core Ops, SparseCore 0:
  37.7 91.3 all-gather.5
  130.9 44.4 all-gather.9
  182.2 53.3 all-gather.7

commit v10 on v7

--- a/solution.py
+++ b/solution.py
@@ -1,8 +1,11 @@
+import functools
 import math
 
 import jax
 import jax.numpy as jnp
 from jax import lax
+from jax.experimental import pallas as pl
+from jax.experimental.pallas import tpu as pltpu
 from jax.sharding import PartitionSpec as P
 
 BLOCK = 128
@@ -14,6 +17,52 @@
 
 
 COL = ("chip", "core")
+
+
+def round_kernel(pat_ref, w_ref, f_ref, seed_ref, table_hbm, out_ref, buf, sems, *, n_blocks, n_groups, per_group, mixing):
+    n_slots = n_groups * per_group
+    copies = []
+    for t in range(n_blocks):
+        for slot in range(n_slots):
+            idx = t * n_slots + slot
+            c = pltpu.make_async_copy(table_hbm.at[pat_ref[t, slot]], buf.at[idx], sems.at[idx])
+            c.start()
+            copies.append(c)
+    bl = buf.shape[1]
+    for t in range(n_blocks):
+        total = jnp.zeros(out_ref.shape[1:], jnp.float32)
+        for g in range(n_groups):
+            acc = jnp.zeros(out_ref.shape[1:], jnp.float32)
+            for s in range(per_group):
+                idx = t * n_slots + g * per_group + s
+                copies[idx].wait()
+                acc = acc + jnp.dot(w_ref[g, t, :, s * bl:(s + 1) * bl], buf[idx], preferred_element_type=jnp.float32)
+            total = total + (acc * f_ref[g, t]).astype(jnp.bfloat16).astype(jnp.float32)
+        out_ref[t] = (mixing * total + (1.0 - mixing) * seed_ref[t].astype(jnp.float32)).astype(out_ref.dtype)
+
+def fused_round(pattern, weights, factors, seed, table, mixing=0.75, interpret=False):
+    n_groups, n_blocks, bl, span = weights.shape
+    per_group = span // bl
+    lanes = table.shape[-1]
+    n_slots = n_groups * per_group
+    kern = functools.partial(round_kernel, n_blocks=n_blocks, n_groups=n_groups, per_group=per_group, mixing=mixing)
+    return pl.pallas_call(
+        kern,
+        out_shape=jax.ShapeDtypeStruct((n_blocks, bl, lanes), seed.dtype),
+        grid_spec=pltpu.PrefetchScalarGridSpec(
+            num_scalar_prefetch=1,
+            grid=(1,),
+            in_specs=[
+                pl.BlockSpec(weights.shape, lambda i, p: (0, 0, 0, 0)),
+                pl.BlockSpec(factors.shape, lambda i, p: (0, 0, 0, 0)),
+                pl.BlockSpec(seed.shape, lambda i, p: (0, 0, 0)),
+                pl.BlockSpec(memory_space=pl.ANY),
+            ],
+            out_specs=pl.BlockSpec((n_blocks, bl, lanes), lambda i, p: (0, 0, 0)),
+            scratch_shapes=[pltpu.VMEM((n_blocks * n_slots, bl, lanes), table.dtype), pltpu.SemaphoreType.DMA((n_blocks * n_slots,))],
+        ),
+        interpret=interpret,
+    )(pattern, weights, factors, seed, table)
 
 
 def gather_columns(x):
@@ -85,8 +134,12 @@
         return (mixing * summed + (1.0 - mixing) * seed.astype(jnp.float32)).astype(jnp.bfloat16)
 
     spread = propagate_using(all_labels, my_labels)
-    all_spread = gather_columns(spread)
-    return propagate_using(all_spread, my_labels)[:, :per_device]
+    whole_spread = lax.all_gather(spread, COL, tiled=True).reshape(-1, BLOCK, lanes)
+    blended = fused_round(
+        pattern, all_weights, factors[..., None], my_labels.reshape(blocks_here, BLOCK, lanes),
+        whole_spread, mixing=mixing,
+    )
+    return blended.reshape(rows_here, lanes)[:, :per_device]
 
 
 def solution(mesh):

time: 259 us -> 257 us (level)
  Pallas kernels: 0 us -> 14.3 us
  local copies, waits for them, and re-layouts: 31.1 us -> 24.2 us
  matrix products: 14.2 us -> 8.36 us
  waiting for transfers between devices: 142 us -> 137 us
  other arithmetic: 11.4 us -> 14.8 us
    all_gather x2 -> x1, waiting for transfers between devices: 59.8 us -> 8.61 us  [gather_columns(): same_core = lax.all_gather(x, 'chip', tiled=True).reshape(-1, BLOCK, width)]
    all_gather x0 -> x1, waiting for transfers between devices: none -> 47.2 us  [body(): lax.all_gather(spread, COL, tiled=True).reshape(-1, BLOCK, lanes)]
    pallas_call x0 -> x1, Pallas kernels: none -> 14.3 us  [fused_round(): pl.pallas_call(kern, out_shape=jax.ShapeDtypeStruct((n_blocks, bl, lanes)...]
    dot_general x2 -> x1, matrix products: 11.7 us -> 5.87 us  [propagate_using(): jnp.einsum('gtmk,tgkc->gtmc', all_weights, candidates, preferred_element_...]
    gather x2 -> x1, local copies, waits for them, and re-layouts: 9.28 us -> 4.57 us  [propagate_using(): same_core[pair_ids]]
    gather x2 -> x1, local copies, waits for them, and re-layouts: 9.16 us -> 4.67 us  [propagate_using(): other_core[pair_ids]]
    div x1 -> x2, other arithmetic: 0.02 us -> 4.09 us  [body(): factors = jnp.exp(stats[:, 0] - top) / totals]
  transfers between devices with their start and end apart: 6 -> 5, of which waited for: 5 -> 4; matrix products, arithmetic and copies ran while one was open for 12% -> 13% of each run, Pallas kernels for 0% -> 0%
where the time goes in v10:
time: 257 us; the launch traced here: 256 us
  waiting for transfers between devices  137 us (53%)
  blocking collectives  37.7 us (15%)
  local copies, waits for them, and re-layouts  24.2 us (9%)
  other arithmetic  14.8 us (6%)
  Pallas kernels  14.3 us (6%)
  between operations  13.3 us (5%)
  matrix products  8.36 us (3%)
  starting transfers between devices  6.68 us (3%)
    all_to_all x1, waiting for transfers between devices, body(): lax.all_to_all(send_emb, COL, split_axis=0, concat_axis=0, tiled=True)  68.2 us
    all_gather x1, waiting for transfers between devices, body(): lax.all_gather(spread, COL, tiled=True).reshape(-1, BLOCK, lanes)  47.2 us
    all_gather x1, blocking collectives, body(): stats = lax.all_gather(jnp.stack([local_max, local_sum]), 'row')  22.3 us
    all_to_all x1, blocking collectives, body(): lax.all_to_all(wanted, COL, split_axis=0, concat_axis=0, tiled=True)  15.3 us
    pallas_call x1, Pallas kernels, fused_round(): pl.pallas_call(kern, out_shape=jax.ShapeDtypeStruct((n_blocks, bl, lanes)...  14.3 us
    all_gather x1, waiting for transfers between devices, body(): all_weights = lax.all_gather(local_weights, 'row')  13 us
    all_gather x1, waiting for transfers between devices, gather_columns(): same_core = lax.all_gather(x, 'chip', tiled=True).reshape(-1, BLOCK, width)  8.61 us
    reduce_or x1, other arithmetic, body(): in_mask = jnp.any(shifted[:, :, None] == positions[None, None, :], axis=1)  7.22 us
  transfers between devices with their start and end apart: 5, of which 4 were waited for; matrix products, arithmetic and copies ran while one was open for 13% of the time, Pallas kernels for 0%

profile of v10, /device:TPU:1, one launch (start us, length us, event | category | flops | bytes accessed | tf_op | source)
XLA Modules:
  0.0 256.4 jit_solution(17318688961547112512)
XLA Ops:
  6.5 0.0 copy-start
  6.5 0.8 fusion.13
  7.4 0.7 compare_select_fusion.1
  8.1 0.1 compare_select_fusion.2
  8.1 0.1 fusion.12
  8.2 0.1 copy.51
  8.3 15.3 %all_to_all.17 = s32[32,1,1]{2,1,0:T(1,128)S(1)} all-to-all(s32[32,1,1]{2,1,0:T(1,128)S(1)} %copy.51), channel_id=1, replica_groups=mesh['row'=8,'chip'=16,'core'=2] {'chip','core'}, dimensions={0} | all-to-all | bytes 256 | tf_op jit(solution)/shard_map/all_to_all | solution.py:91
  23.7 0.7 reduce.1
  24.4 4.9 %gather_fusion = bf16[32,128,768]{2,1,0:T(8,128)(2,1)} fusion(bf16[6,128,768]{2,1,0:T(8,128)(2,1)} %bitcast.36, s32[1024]{0:T(1024)S(1)} %pad_clamp_fusion.2), kind=kCustom, calls=%fused_computation | custom fusion | bytes 12583040 | tf_op jit(solution)/shard_map/gather | solution.py:93
  29.2 0.0 copy-start.2
  29.2 0.0 copy-start.3
  29.2 5.3 %all-to-all-start.1 = ((bf16[32,128,768]{2,1,0:T(8,128)(2,1)}), bf16[32,128,768]{2,1,0:T(8,128)(2,1)}, u32[]{:S(2)}, u32[]{:S(2)}) async-start(bf16[32,128,768]{2,1,0:T(8,128)(2,1)} %gather_fusion), calls=%async_computation.1 | async-start | bytes 12582912 | tf_op jit(solution)/shard_map/all_to_all | solution.py:104
  34.5 0.0 all-gather.6.cloned.1.call-start
  34.6 0.0 copy-done
  34.6 0.1 constant_dynamic-slice_fusion
  34.6 0.2 copy.62
  34.8 0.0 copy-start.1
  34.8 0.7 pad.4
  35.5 0.0 all-gather.6.cloned.1.call-update
  35.6 0.0 all-gather.10.cloned.1.call-start
  35.6 0.1 reshape.103
  35.7 0.0 copy-done.2
  35.7 7.2 %fusion = pred[768,256]{1,0:T(8,128)(4,1)S(1)} fusion(s32[768,50]{0,1:T(8,128)S(1)} %and_select_fusion), kind=kLoop, calls=%fused_computation.5 | loop fusion | flops 19464192 | bytes 350208 | tf_op jit(solution)/shard_map/reduce_or | solution.py:101
  42.9 0.3 copy.53
  43.2 0.0 copy-done.3
  43.3 68.2 %all-to-all-done.1 = bf16[32,128,768]{2,1,0:T(8,128)(2,1)} async-done(((bf16[32,128,768]{2,1,0:T(8,128)(2,1)}), bf16[32,128,768]{2,1,0:T(8,128)(2,1)}, u32[]{:S(2)}, u32[]{:S(2)}) %all-to-all-start.1) | async-done | bytes 6291488 | tf_op jit(solution)/shard_map/all_to_all | solution.py:104
  111.5 5.2 %gather_fusion.1 = bf16[12,128,768]{2,1,0:T(8,128)(2,1)} fusion(bf16[32,128,768]{2,1,0:T(8,128)(2,1)} %all-to-all-done.1, s32[1024]{0:T(1024)S(1)} %pad_clamp_fusion.1), kind=kCustom, calls=%fused_computation.1 | custom fusion | bytes 4718640 | tf_op jit(solution)/shard_map/gather | solution.py:105
  116.8 0.0 copy-done.1
  116.8 2.5 select_reduce_fusion
  119.3 0.2 fusion.8
  119.5 1.0 copy.54
  120.4 0.0 all-gather.10.cloned.1.call-update
  120.5 0.0 all-gather.8.cloned.1.call-start
  120.5 8.6 %all-gather.6.cloned.1.call-done = bf16[12288,128]{1,0:T(8,128)(2,1)} async-done(((bf16[768,128]{1,0:T(8,128)(2,1)}), bf16[12288,128]{1,0:T(8,128)(2,1)}) %all-gather.6.cloned.1.call-update) | async-done | bytes 3145744 | tf_op jit(solution)/shard_map/all_gather | solution.py:70
  129.1 1.3 collective-permute-start
  130.4 0.1 reshape.111
  130.5 0.1 broadcast_in_dim.60
  130.6 4.6 %gather_fusion.2 = bf16[96,128,128]{2,1,0:T(8,128)(2,1)} fusion(bf16[96,128,128]{2,1,0:T(8,128)(2,1)} %bitcast.40, s32[1024]{0:T(1024)S(1)} %pad_clamp_fusion), kind=kCustom, calls=%fused_computation.2 | custom fusion | bytes 6291840 | tf_op jit(solution)/shard_map/gather | solution.py:127
  135.2 22.3 %all-gather.1 = f32[16,6,128]{2,1,0:T(8,128)S(1)} all-gather(f32[2,6,128]{2,1,0:T(8,128)S(1)} %pad_maximum_fusion), channel_id=3, replica_groups=mesh['row'=8,'chip'=16,'core'=2] {'row'}, dimensions={0}, use_global_device_ids=true | all-gather | bytes 55296 | tf_op jit(solution)/shard_map/all_gather | solution.py:115
  157.7 0.0 collective-permute-done
  157.7 4.7 %gather_fusion.3 = bf16[96,128,128]{2,1,0:T(8,128)(2,1)} fusion(bf16[96,128,128]{2,1,0:T(8,128)(2,1)} %collective-permute-done, s32[1024]{0:T(1024)S(1)} %pad_clamp_fusion), kind=kCustom, calls=%fused_computation.3 | custom fusion | bytes 6291840 | tf_op jit(solution)/shard_map/gather | solution.py:127
  162.3 13.0 %all-gather.10.cloned.1.call-done = bf16[48,128,256]{2,1,0:T(8,128)(2,1)} async-done(((bf16[6,128,256]{2,1,0:T(8,128)(2,1)}), bf16[48,128,256]{2,1,0:T(8,128)(2,1)}) %all-gather.10.cloned.1.call-update) | async-done | bytes 3145744 | tf_op jit(solution)/shard_map/all_gather | solution.py:116
  175.4 5.9 %convert_reduce_fusion = f32[6,128,128]{2,1,0:T(8,128)S(1)} fusion(f32[8,6,128]{2,1,0:T(8,128)S(1)} %copy.60, bf16[8,6,128,256]{3,2,1,0:T(8,128)(2,1)} %bitcast.41, bf16[6,8,256,128]{3,2,1,0:T(8,128)(2,1)} %bitcast.43, bf16[6,8,256,128]{3,2,1,0:T(8,128)(2,1)} %bitcast.44, pred[6,8,256]{2,1,0:T(8,128)(4,1)S(1)} %broadcast_in_dim.61), kind=kOutput, calls=%fused_computation.8 | convolution fusion | flops 407273472 | bytes 9867264 | tf_op jit(solution)/shard_map/gtmk,tgkc->gtmc/dot_general | solution.py:129
  181.3 0.7 fusion.10
  182.0 0.0 all-gather.8.cloned.1.call-update
  182.1 2.2 copy.57
  184.3 4.1 %broadcast_divide_fusion.f_ref = f32[8,6,128,1]{3,2,1,0:T(8,128)} fusion(f32[8,6,128,1]{3,2,1,0:T(8,128)} %copy.57, f32[6,128]{1,0:T(8,128)S(1)} %multiply_reduce_fusion), kind=kLoop, calls=%fused_computation.11 | loop fusion | flops 6144 | bytes 52224 | tf_op jit(solution)/shard_map/div | solution.py:119
  188.4 47.2 %all-gather.8.cloned.1.call-done = bf16[24576,128]{1,0:T(8,128)(2,1)} async-done(((bf16[768,128]{1,0:T(8,128)(2,1)}), bf16[24576,128]{1,0:T(8,128)(2,1)}) %all-gather.8.cloned.1.call-update) | async-done | bytes 6291472 | tf_op jit(solution)/shard_map/all_gather | solution.py:137
  235.5 14.3 %shard_map.55 = bf16[6,128,128]{2,1,0:T(8,128)(2,1)} custom-call(s32[6,16]{1,0:T(8,128)} %pat_ref.1, bf16[8,6,128,256]{3,2,1,0:T(8,128)(2,1)} %bitcast.42, f32[8,6,128,1]{3,2,1,0:T(8,128)} %broadcast_divide_fusion.f_ref, bf16[6,128,128]{2,1,0:T(8,128)(2,1)} %bitcast.46, bf16[192,128,128]{2,1,0:T(8,128)(2,1)} %bitcast.38), custom_call_target="tpu_custom_call" | custom-call | tf_op jit(solution)/shard_map/pallas_call | solution.py:49
  (16 shorter events, 0.2 us)
Async XLA Ops:
  6.5 28.0 %copy-start = (bf16[768,1000]{0,1:T(8,128)(2,1)S(1)}, bf16[768,1000]{0,1:T(8,128)(2,1)}, u32[]{:S(2)}) copy-start(bf16[768,1000]{0,1:T(8,128)(2,1)} %param.6) | copy-start | bytes 4608004
  29.2 6.5 %copy-start.2 = (s32[768,50]{0,1:T(8,128)S(1)}, s32[768,50]{0,1:T(8,128)}, u32[]{:S(2)}) copy-start(s32[768,50]{0,1:T(8,128)} %param.9) | copy-start | bytes 460804
  29.2 14.0 %copy-start.3 = (f32[768]{0:T(1024)S(1)}, f32[768]{0:T(1024)}, u32[]{:S(2)}) copy-start(f32[768]{0:T(1024)} %param.7) | copy-start | bytes 9220
  29.2 82.3 %all-to-all-start.1 = ((bf16[32,128,768]{2,1,0:T(8,128)(2,1)}), bf16[32,128,768]{2,1,0:T(8,128)(2,1)}, u32[]{:S(2)}, u32[]{:S(2)}) async-start(bf16[32,128,768]{2,1,0:T(8,128)(2,1)} %gather_fusion), calls=%async_computation.1 | async-start | bytes 12582912 | tf_op jit(solution)/shard_map/all_to_all | solution.py:104
  34.5 94.6 %all-gather.6.cloned.1.call-start = ((), (), s32[]{:S(2)}) async-start(), calls=%async_computation.2 | async-start | bytes 3342336 | tf_op jit(solution)/shard_map/all_gather | solution.py:70
  34.8 82.0 %copy-start.1 = (bf16[768,768]{1,0:T(8,128)(2,1)S(1)}, bf16[768,768]{1,0:T(8,128)(2,1)}, u32[]{:S(2)}) copy-start(bf16[768,768]{1,0:T(8,128)(2,1)} %param.5) | copy-start | bytes 3538948
  35.6 139.8 %all-gather.10.cloned.1.call-start = ((), (), s32[]{:S(2)}) async-start(), calls=%async_computation.4 | async-start | bytes 3538944 | tf_op jit(solution)/shard_map/all_gather | solution.py:116
  120.5 115.1 %all-gather.8.cloned.1.call-start = ((), (), s32[]{:S(2)}) async-start(), calls=%async_computation.3 | async-start | bytes 6488064 | tf_op jit(solution)/shard_map/all_gather | solution.py:137
  129.1 28.5 %collective-permute-start = (bf16[96,128,128]{2,1,0:T(8,128)(2,1)}, bf16[96,128,128]{2,1,0:T(8,128)(2,1)}, u32[]{:S(2)}, u32[]{:S(2)}) collective-permute-start(bf16[96,128,128]{2,1,0:T(8,128)(2,1)} %bitcast.39), channel_id=1, source_target_pairs={{0,1},{1,0},{2,3},{3,2},{4,5},{5,4},{6,7},{7,6},{8,9},{9,8},{10,11... | collective-permute-start | bytes 9437192 | tf_op jit(solution)/shard_map/ppermute | solution.py:71
Sparse Core Ops, SparseCore 0:
  37.7 91.3 all-gather.5
  130.9 44.4 all-gather.9
  182.2 53.3 all-gather.7

commit v11 on v10

--- a/solution.py
+++ b/solution.py
@@ -32,11 +32,11 @@
     for t in range(n_blocks):
         total = jnp.zeros(out_ref.shape[1:], jnp.float32)
         for g in range(n_groups):
-            acc = jnp.zeros(out_ref.shape[1:], jnp.float32)
+            first = t * n_slots + g * per_group
             for s in range(per_group):
-                idx = t * n_slots + g * per_group + s
-                copies[idx].wait()
-                acc = acc + jnp.dot(w_ref[g, t, :, s * bl:(s + 1) * bl], buf[idx], preferred_element_type=jnp.float32)
+                copies[first + s].wait()
+            candidates = buf[first:first + per_group].reshape(per_group * bl, buf.shape[2])
+            acc = jnp.dot(w_ref[g, t], candidates, preferred_element_type=jnp.float32)
             total = total + (acc * f_ref[g, t]).astype(jnp.bfloat16).astype(jnp.float32)
         out_ref[t] = (mixing * total + (1.0 - mixing) * seed_ref[t].astype(jnp.float32)).astype(out_ref.dtype)
 

time: 257 us -> 257 us (level)
  no operation moved by 1% of the time
where the time goes in v11:
time: 257 us; the launch traced here: 256 us
  waiting for transfers between devices  137 us (53%)
  blocking collectives  37.7 us (15%)
  local copies, waits for them, and re-layouts  24.2 us (9%)
  other arithmetic  14.8 us (6%)
  Pallas kernels  14.1 us (5%)
  between operations  13.3 us (5%)
  matrix products  8.36 us (3%)
  starting transfers between devices  6.68 us (3%)
    all_to_all x1, waiting for transfers between devices, body(): lax.all_to_all(send_emb, COL, split_axis=0, concat_axis=0, tiled=True)  68.2 us
    all_gather x1, waiting for transfers between devices, body(): lax.all_gather(spread, COL, tiled=True).reshape(-1, BLOCK, lanes)  47.2 us
    all_gather x1, blocking collectives, body(): stats = lax.all_gather(jnp.stack([local_max, local_sum]), 'row')  22.3 us
    all_to_all x1, blocking collectives, body(): lax.all_to_all(wanted, COL, split_axis=0, concat_axis=0, tiled=True)  15.3 us
    pallas_call x1, Pallas kernels, fused_round(): pl.pallas_call(kern, out_shape=jax.ShapeDtypeStruct((n_blocks, bl, lanes)...  14.1 us
    all_gather x1, waiting for transfers between devices, body(): all_weights = lax.all_gather(local_weights, 'row')  13 us
    all_gather x1, waiting for transfers between devices, gather_columns(): same_core = lax.all_gather(x, 'chip', tiled=True).reshape(-1, BLOCK, width)  8.61 us
    reduce_or x1, other arithmetic, body(): in_mask = jnp.any(shifted[:, :, None] == positions[None, None, :], axis=1)  7.22 us
  transfers between devices with their start and end apart: 5, of which 4 were waited for; matrix products, arithmetic and copies ran while one was open for 13% of the time, Pallas kernels for 0%

profile of v11, /device:TPU:1, one launch (start us, length us, event | category | flops | bytes accessed | tf_op | source)
XLA Modules:
  0.0 256.2 jit_solution(1856771002640761475)
XLA Ops:
  6.5 0.0 copy-start
  6.5 0.8 fusion.13
  7.4 0.7 compare_select_fusion.1
  8.1 0.1 compare_select_fusion.2
  8.1 0.1 fusion.12
  8.2 0.1 copy.51
  8.3 15.3 %all_to_all.17 = s32[32,1,1]{2,1,0:T(1,128)S(1)} all-to-all(s32[32,1,1]{2,1,0:T(1,128)S(1)} %copy.51), channel_id=1, replica_groups=mesh['row'=8,'chip'=16,'core'=2] {'chip','core'}, dimensions={0} | all-to-all | bytes 256 | tf_op jit(solution)/shard_map/all_to_all | solution.py:91
  23.7 0.7 reduce.1
  24.4 4.9 %gather_fusion = bf16[32,128,768]{2,1,0:T(8,128)(2,1)} fusion(bf16[6,128,768]{2,1,0:T(8,128)(2,1)} %bitcast.36, s32[1024]{0:T(1024)S(1)} %pad_clamp_fusion.2), kind=kCustom, calls=%fused_computation | custom fusion | bytes 12583040 | tf_op jit(solution)/shard_map/gather | solution.py:93
  29.2 0.0 copy-start.2
  29.2 0.0 copy-start.3
  29.2 5.3 %all-to-all-start.1 = ((bf16[32,128,768]{2,1,0:T(8,128)(2,1)}), bf16[32,128,768]{2,1,0:T(8,128)(2,1)}, u32[]{:S(2)}, u32[]{:S(2)}) async-start(bf16[32,128,768]{2,1,0:T(8,128)(2,1)} %gather_fusion), calls=%async_computation.1 | async-start | bytes 12582912 | tf_op jit(solution)/shard_map/all_to_all | solution.py:104
  34.5 0.0 all-gather.6.cloned.1.call-start
  34.6 0.0 copy-done
  34.6 0.1 constant_dynamic-slice_fusion
  34.6 0.2 copy.62
  34.8 0.0 copy-start.1
  34.8 0.7 pad.4
  35.5 0.0 all-gather.6.cloned.1.call-update
  35.6 0.0 all-gather.10.cloned.1.call-start
  35.6 0.1 reshape.103
  35.7 0.0 copy-done.2
  35.7 7.2 %fusion = pred[768,256]{1,0:T(8,128)(4,1)S(1)} fusion(s32[768,50]{0,1:T(8,128)S(1)} %and_select_fusion), kind=kLoop, calls=%fused_computation.5 | loop fusion | flops 19464192 | bytes 350208 | tf_op jit(solution)/shard_map/reduce_or | solution.py:101
  42.9 0.3 copy.53
  43.2 0.0 copy-done.3
  43.3 68.2 %all-to-all-done.1 = bf16[32,128,768]{2,1,0:T(8,128)(2,1)} async-done(((bf16[32,128,768]{2,1,0:T(8,128)(2,1)}), bf16[32,128,768]{2,1,0:T(8,128)(2,1)}, u32[]{:S(2)}, u32[]{:S(2)}) %all-to-all-start.1) | async-done | bytes 6291488 | tf_op jit(solution)/shard_map/all_to_all | solution.py:104
  111.5 5.2 %gather_fusion.1 = bf16[12,128,768]{2,1,0:T(8,128)(2,1)} fusion(bf16[32,128,768]{2,1,0:T(8,128)(2,1)} %all-to-all-done.1, s32[1024]{0:T(1024)S(1)} %pad_clamp_fusion.1), kind=kCustom, calls=%fused_computation.1 | custom fusion | bytes 4718640 | tf_op jit(solution)/shard_map/gather | solution.py:105
  116.8 0.0 copy-done.1
  116.8 2.5 select_reduce_fusion
  119.3 0.2 fusion.8
  119.5 1.0 copy.54
  120.4 0.0 all-gather.10.cloned.1.call-update
  120.5 0.0 all-gather.8.cloned.1.call-start
  120.5 8.6 %all-gather.6.cloned.1.call-done = bf16[12288,128]{1,0:T(8,128)(2,1)} async-done(((bf16[768,128]{1,0:T(8,128)(2,1)}), bf16[12288,128]{1,0:T(8,128)(2,1)}) %all-gather.6.cloned.1.call-update) | async-done | bytes 3145744 | tf_op jit(solution)/shard_map/all_gather | solution.py:70
  129.1 1.3 collective-permute-start
  130.4 0.1 reshape.111
  130.5 0.1 broadcast_in_dim.60
  130.6 4.6 %gather_fusion.2 = bf16[96,128,128]{2,1,0:T(8,128)(2,1)} fusion(bf16[96,128,128]{2,1,0:T(8,128)(2,1)} %bitcast.40, s32[1024]{0:T(1024)S(1)} %pad_clamp_fusion), kind=kCustom, calls=%fused_computation.2 | custom fusion | bytes 6291840 | tf_op jit(solution)/shard_map/gather | solution.py:127
  135.2 22.3 %all-gather.1 = f32[16,6,128]{2,1,0:T(8,128)S(1)} all-gather(f32[2,6,128]{2,1,0:T(8,128)S(1)} %pad_maximum_fusion), channel_id=3, replica_groups=mesh['row'=8,'chip'=16,'core'=2] {'row'}, dimensions={0}, use_global_device_ids=true | all-gather | bytes 55296 | tf_op jit(solution)/shard_map/all_gather | solution.py:115
  157.7 0.0 collective-permute-done
  157.7 4.7 %gather_fusion.3 = bf16[96,128,128]{2,1,0:T(8,128)(2,1)} fusion(bf16[96,128,128]{2,1,0:T(8,128)(2,1)} %collective-permute-done, s32[1024]{0:T(1024)S(1)} %pad_clamp_fusion), kind=kCustom, calls=%fused_computation.3 | custom fusion | bytes 6291840 | tf_op jit(solution)/shard_map/gather | solution.py:127
  162.3 13.0 %all-gather.10.cloned.1.call-done = bf16[48,128,256]{2,1,0:T(8,128)(2,1)} async-done(((bf16[6,128,256]{2,1,0:T(8,128)(2,1)}), bf16[48,128,256]{2,1,0:T(8,128)(2,1)}) %all-gather.10.cloned.1.call-update) | async-done | bytes 3145744 | tf_op jit(solution)/shard_map/all_gather | solution.py:116
  175.4 5.9 %convert_reduce_fusion = f32[6,128,128]{2,1,0:T(8,128)S(1)} fusion(f32[8,6,128]{2,1,0:T(8,128)S(1)} %copy.60, bf16[8,6,128,256]{3,2,1,0:T(8,128)(2,1)} %bitcast.41, bf16[6,8,256,128]{3,2,1,0:T(8,128)(2,1)} %bitcast.43, bf16[6,8,256,128]{3,2,1,0:T(8,128)(2,1)} %bitcast.44, pred[6,8,256]{2,1,0:T(8,128)(4,1)S(1)} %broadcast_in_dim.61), kind=kOutput, calls=%fused_computation.8 | convolution fusion | flops 407273472 | bytes 9867264 | tf_op jit(solution)/shard_map/gtmk,tgkc->gtmc/dot_general | solution.py:129
  181.3 0.7 fusion.10
  182.0 0.0 all-gather.8.cloned.1.call-update
  182.1 2.2 copy.57
  184.3 4.1 %broadcast_divide_fusion.f_ref = f32[8,6,128,1]{3,2,1,0:T(8,128)} fusion(f32[8,6,128,1]{3,2,1,0:T(8,128)} %copy.57, f32[6,128]{1,0:T(8,128)S(1)} %multiply_reduce_fusion), kind=kLoop, calls=%fused_computation.11 | loop fusion | flops 6144 | bytes 52224 | tf_op jit(solution)/shard_map/div | solution.py:119
  188.4 47.2 %all-gather.8.cloned.1.call-done = bf16[24576,128]{1,0:T(8,128)(2,1)} async-done(((bf16[768,128]{1,0:T(8,128)(2,1)}), bf16[24576,128]{1,0:T(8,128)(2,1)}) %all-gather.8.cloned.1.call-update) | async-done | bytes 6291472 | tf_op jit(solution)/shard_map/all_gather | solution.py:137
  235.5 14.1 %shard_map.55 = bf16[6,128,128]{2,1,0:T(8,128)(2,1)} custom-call(s32[6,16]{1,0:T(8,128)} %pat_ref.1, bf16[8,6,128,256]{3,2,1,0:T(8,128)(2,1)} %bitcast.42, f32[8,6,128,1]{3,2,1,0:T(8,128)} %broadcast_divide_fusion.f_ref, bf16[6,128,128]{2,1,0:T(8,128)(2,1)} %bitcast.46, bf16[192,128,128]{2,1,0:T(8,128)(2,1)} %bitcast.38), custom_call_target="tpu_custom_call" | custom-call | tf_op jit(solution)/shard_map/pallas_call | solution.py:49
  (16 shorter events, 0.2 us)
Async XLA Ops:
  6.5 28.0 %copy-start = (bf16[768,1000]{0,1:T(8,128)(2,1)S(1)}, bf16[768,1000]{0,1:T(8,128)(2,1)}, u32[]{:S(2)}) copy-start(bf16[768,1000]{0,1:T(8,128)(2,1)} %param.6) | copy-start | bytes 4608004
  29.2 6.5 %copy-start.2 = (s32[768,50]{0,1:T(8,128)S(1)}, s32[768,50]{0,1:T(8,128)}, u32[]{:S(2)}) copy-start(s32[768,50]{0,1:T(8,128)} %param.9) | copy-start | bytes 460804
  29.2 14.0 %copy-start.3 = (f32[768]{0:T(1024)S(1)}, f32[768]{0:T(1024)}, u32[]{:S(2)}) copy-start(f32[768]{0:T(1024)} %param.7) | copy-start | bytes 9220
  29.2 82.3 %all-to-all-start.1 = ((bf16[32,128,768]{2,1,0:T(8,128)(2,1)}), bf16[32,128,768]{2,1,0:T(8,128)(2,1)}, u32[]{:S(2)}, u32[]{:S(2)}) async-start(bf16[32,128,768]{2,1,0:T(8,128)(2,1)} %gather_fusion), calls=%async_computation.1 | async-start | bytes 12582912 | tf_op jit(solution)/shard_map/all_to_all | solution.py:104
  34.5 94.6 %all-gather.6.cloned.1.call-start = ((), (), s32[]{:S(2)}) async-start(), calls=%async_computation.2 | async-start | bytes 3342336 | tf_op jit(solution)/shard_map/all_gather | solution.py:70
  34.8 82.0 %copy-start.1 = (bf16[768,768]{1,0:T(8,128)(2,1)S(1)}, bf16[768,768]{1,0:T(8,128)(2,1)}, u32[]{:S(2)}) copy-start(bf16[768,768]{1,0:T(8,128)(2,1)} %param.5) | copy-start | bytes 3538948
  35.6 139.8 %all-gather.10.cloned.1.call-start = ((), (), s32[]{:S(2)}) async-start(), calls=%async_computation.4 | async-start | bytes 3538944 | tf_op jit(solution)/shard_map/all_gather | solution.py:116
  120.5 115.1 %all-gather.8.cloned.1.call-start = ((), (), s32[]{:S(2)}) async-start(), calls=%async_computation.3 | async-start | bytes 6488064 | tf_op jit(solution)/shard_map/all_gather | solution.py:137
  129.1 28.5 %collective-permute-start = (bf16[96,128,128]{2,1,0:T(8,128)(2,1)}, bf16[96,128,128]{2,1,0:T(8,128)(2,1)}, u32[]{:S(2)}, u32[]{:S(2)}) collective-permute-start(bf16[96,128,128]{2,1,0:T(8,128)(2,1)} %bitcast.39), channel_id=1, source_target_pairs={{0,1},{1,0},{2,3},{3,2},{4,5},{5,4},{6,7},{7,6},{8,9},{9,8},{10,11... | collective-permute-start | bytes 9437192 | tf_op jit(solution)/shard_map/ppermute | solution.py:71
Sparse Core Ops, SparseCore 0:
  37.7 91.3 all-gather.5
  130.9 44.4 all-gather.9
  182.2 53.3 all-gather.7
